TPU v7x, 1024 devices: a whole 8x8x8 slice. The times are simulated.
1024 devices in a mesh: dp: 64 (over y, z), sub: 16 (over x, core).
Axes of the slice: x: 8, y: 8, z: 8, core: 2. Of those that a mesh axis runs over, the one named last changes fastest.
Arguments:
- activations: bfloat16 [196608, 5632], P(('dp', 'sub')), may hold values from -6 to 6
- grad_out: bfloat16 [196608, 1408], P(('dp', 'sub'))
- q_prev: bfloat16 [1408, 32], replicated, may hold values from -0.15625 to 0.15625
Outputs:
- grad_approx: float32 [5632, 1408], P('sub')
- q_new: float32 [1408, 32], replicated
All inputs are finite; a program needn't handle non-finite values.
Results may differ from a plain program's by a relative error of at most 0.0036.
Values may be sent and summed in bfloat16 or wider, within the bound.
No kernel may reach another device: no remote copies, remote signals or barrier semaphores. Data moves between devices by JAX's collectives and lax.ppermute only.
A program may use at most 32 MiB of HBM per device.

v0:
```python
import jax
import jax.numpy as jnp
from jax import lax
from jax.sharding import PartitionSpec as P


def orthonormal(rows_part, gram):
    lower = lax.linalg.cholesky(gram)
    return lax.linalg.triangular_solve(
        lower, rows_part, left_side=False, lower=True, transpose_a=True
    )


def per_device(activations, grad_out, q_prev):
    u_low = jnp.dot(grad_out, q_prev, preferred_element_type=jnp.float32).astype(jnp.bfloat16)
    p_local = jnp.einsum("tf,tr->fr", activations, u_low, preferred_element_type=jnp.float32)
    hidden = activations.shape[1]
    block_rows = hidden // lax.axis_size("sub")
    p_sum = lax.psum(p_local, ("dp", "sub"))
    gram = jnp.dot(p_sum.T, p_sum, precision=lax.Precision.HIGHEST)
    p_hat = orthonormal(p_sum, gram)
    p_low = p_hat.astype(jnp.bfloat16)
    my_hat = lax.dynamic_slice_in_dim(p_hat, lax.axis_index("sub") * block_rows, block_rows, 0)
    v_low = jnp.dot(activations, p_low, preferred_element_type=jnp.float32).astype(jnp.bfloat16)
    q_local = jnp.einsum("tc,tr->cr", grad_out, v_low, preferred_element_type=jnp.float32)
    q_sum = lax.psum(q_local, ("dp", "sub"))
    q_new = q_sum / (lax.axis_size("dp") * lax.axis_size("sub"))
    grad_approx = jnp.dot(my_hat, q_new.T, precision=lax.Precision.HIGHEST)
    return (grad_approx, q_new)


def solution(mesh):
    in_specs = (P(("dp", "sub"), None), P(("dp", "sub"), None), P())
    out_specs = (P("sub", None), P())
    return jax.shard_map(
        per_device, mesh=mesh, in_specs=in_specs, out_specs=out_specs, check_vma=False
    )
```

profile of v0, /device:TPU:1, one launch (start us, length us, event | category | flops | bytes accessed | tf_op | source)
XLA Modules:
  0.0 618.5 jit_solution(17296722265113637711)
XLA Ops:
  7.2 0.0 copy-start
  7.2 0.0 all-reduce.3.cloned.1.call-start
  7.2 1.6 copy-done
  8.8 2.9 convolution_bitcast_fusion
  11.7 0.0 copy-start.1
  11.7 0.0 all-reduce.3.cloned.1.call-update
  11.7 0.0 all-reduce.5.cloned.1.call-start
  11.7 304.7 %all-reduce.3.cloned.1.call-done = f32[5632,32]{0,1:T(8,128)} async-done(((f32[5632,32]{0,1:T(8,128)}), f32[5632,32]{0,1:T(8,128)}) %all-reduce.3.cloned.1.call-update) | async-done | bytes 720912 | tf_op jit(solution)/shard_map/psum | solution.py:19
  316.5 2.0 fusion.9
  318.5 0.1 copy.5
  318.6 2.9 cholesky.16
  321.5 0.6 compare_reduce_fusion
  322.2 0.7 fusion.4
  322.8 2.4 custom-call.5
  325.3 1.9 fusion.5
  327.2 0.0 copy-done.1
  327.2 1.8 convolution_bitcast_fusion.1
  329.0 0.0 all-reduce.5.cloned.1.call-update
  329.0 278.6 %all-reduce.5.cloned.1.call-done = f32[1408,32]{0,1:T(8,128)} async-done(((f32[1408,32]{0,1:T(8,128)}), f32[1408,32]{0,1:T(8,128)}) %all-reduce.5.cloned.1.call-update) | async-done | bytes 180240 | tf_op jit(solution)/shard_map/psum | solution.py:26
  607.6 0.9 broadcast_multiply_fusion
  608.5 0.0 copy-start.2
  608.5 3.1 fusion.2
  611.6 0.0 copy-done.2
  (2 shorter events, 0.0 us)
Async XLA Ops:
  7.2 1.6 copy-start
  7.2 309.3 %all-reduce.3.cloned.1.call-start = ((), (), s32[]{:S(2)}) async-start(), calls=%async_computation | async-start | bytes 1441792 | tf_op jit(solution)/shard_map/psum | solution.py:19
  11.7 315.5 %copy-start.1 = (bf16[192,1408]{1,0:T(8,128)(2,1)S(1)}, bf16[192,1408]{1,0:T(8,128)(2,1)}, u32[]{:S(2)}) copy-start(bf16[192,1408]{1,0:T(8,128)(2,1)} %param.4) | copy-start | bytes 1622020
  11.7 595.9 %all-reduce.5.cloned.1.call-start = ((), (), s32[]{:S(2)}) async-start(), calls=%async_computation.1 | async-start | bytes 360448 | tf_op jit(solution)/shard_map/psum | solution.py:26
  608.5 3.1 copy-start.2
Sparse Core Ops, SparseCore 0:
  13.3 303.0 all-reduce.2
  329.1 278.4 all-reduce.4
where the time goes:
time: 619 us; the launch traced here: 618 us
  waiting for transfers between devices  583 us (94%)
  between operations  14.1 us (2%)
  matrix products  11.7 us (2%)
  other arithmetic  7.62 us (1%)
    psum x1, waiting for transfers between devices, per_device(): p_sum = lax.psum(p_local, ('dp', 'sub'))  305 us
    psum x1, waiting for transfers between devices, per_device(): q_sum = lax.psum(q_local, ('dp', 'sub'))  279 us
  transfers between devices with their start and end apart: 2, of which 2 were waited for; matrix products, arithmetic and copies ran while one was open for 0% of the time, Pallas kernels for 0%

commit v1 on v0

v1 whole, which is shorter than its diff:
```python
import jax
import jax.numpy as jnp
from jax import lax
from jax.sharding import PartitionSpec as P

AXES = ("dp", "sub")


def exchange_order(n_dp, n_sub):
    core_bits = [0]
    sub_bits = list(range(1, (n_sub // 2).bit_length()))
    dp_len = n_dp.bit_length() - 1
    z_bits = [n_sub.bit_length() - 1 + k for k in range(dp_len // 2)]
    y_bits = [z_bits[-1] + 1 + k for k in range(dp_len - len(z_bits))]
    order = list(core_bits)
    for level in range(max(len(sub_bits), len(z_bits), len(y_bits))):
        for bits in (sub_bits, z_bits, y_bits):
            if level < len(bits):
                order.append(bits[level])
    return order


def xor_pairs(n, bit):
    return [(i, i ^ (1 << bit)) for i in range(n)]


def butterfly_sum(x, order, n, max_halvings):
    idx = lax.axis_index(AXES)
    halved = []
    for bit in order:
        rows = x.shape[0]
        if len(halved) < max_halvings and rows % 16 == 0:
            half = rows // 2
            mine = (idx >> bit) & 1
            lo, hi = x[:half], x[half:]
            send = jnp.where(mine == 1, lo, hi)
            keep = jnp.where(mine == 1, hi, lo)
            x = keep + lax.ppermute(send, AXES, xor_pairs(n, bit))
            halved.append(bit)
        else:
            x = x + lax.ppermute(x, AXES, xor_pairs(n, bit))
    for bit in reversed(halved):
        mine = (idx >> bit) & 1
        other = lax.ppermute(x, AXES, xor_pairs(n, bit))
        x = jnp.where(mine == 1, jnp.concatenate([other, x]), jnp.concatenate([x, other]))
    return x


def orthonormal(rows_part, gram):
    lower = lax.linalg.cholesky(gram)
    return lax.linalg.triangular_solve(
        lower, rows_part, left_side=False, lower=True, transpose_a=True
    )


def make_per_device(n_dp, n_sub):
    n = n_dp * n_sub
    order = exchange_order(n_dp, n_sub)

    def per_device(activations, grad_out, q_prev):
        u_low = jnp.dot(grad_out, q_prev, preferred_element_type=jnp.float32).astype(jnp.bfloat16)
        p_local = jnp.einsum("tf,tr->fr", activations, u_low, preferred_element_type=jnp.float32)
        hidden = activations.shape[1]
        block_rows = hidden // n_sub
        p_sum = butterfly_sum(p_local, order, n, 5)
        gram = jnp.dot(p_sum.T, p_sum, precision=lax.Precision.HIGHEST)
        p_hat = orthonormal(p_sum, gram)
        p_low = p_hat.astype(jnp.bfloat16)
        my_hat = lax.dynamic_slice_in_dim(p_hat, lax.axis_index("sub") * block_rows, block_rows, 0)
        v_low = jnp.dot(activations, p_low, preferred_element_type=jnp.float32).astype(jnp.bfloat16)
        q_local = jnp.einsum("tc,tr->cr", grad_out, v_low, preferred_element_type=jnp.float32)
        q_sum = butterfly_sum(q_local, order, n, 3)
        q_new = q_sum / n
        grad_approx = jnp.dot(my_hat, q_new.T, precision=lax.Precision.HIGHEST)
        return (grad_approx, q_new)

    return per_device


def solution(mesh):
    in_specs = (P(AXES, None), P(AXES, None), P())
    out_specs = (P("sub", None), P())
    per_device = make_per_device(mesh.shape["dp"], mesh.shape["sub"])
    return jax.shard_map(
        per_device, mesh=mesh, in_specs=in_specs, out_specs=out_specs, check_vma=False
    )
```

time: 619 us -> 229 us (0.37)
  waiting for transfers between devices: 583 us -> 95.5 us
  starting transfers between devices: 0.08 us -> 108 us
  between operations: 14.1 us -> 1.09 us
    psum x2 -> x0, waiting for transfers between devices: 583 us -> none  [the longest x1 305 us: per_device(): p_sum = lax.psum(p_local, ('dp', 'sub'))]
    ppermute x0 -> x28, starting transfers between devices: none -> 108 us  [the longest x8 42.3 us: butterfly_sum(): other = lax.ppermute(x, AXES, xor_pairs(n, bit))]
    ppermute x0 -> x28, waiting for transfers between devices: none -> 95.5 us  [the longest x12 48.9 us: butterfly_sum(): x = x + lax.ppermute(x, AXES, xor_pairs(n, bit))]
  transfers between devices with their start and end apart: 2 -> 28, of which waited for: 2 -> 28; matrix products, arithmetic and copies ran while one was open for 0% -> 0% of each run, Pallas kernels for 0% -> 0%
where the time goes in v1:
time: 229 us; the launch traced here: 228 us
  starting transfers between devices  108 us (47%)
  waiting for transfers between devices  95.5 us (42%)
  other arithmetic  11.4 us (5%)
  matrix products  9.79 us (4%)
  local copies, waits for them, and re-layouts  2.42 us (1%)
    ppermute x12, waiting for transfers between devices, butterfly_sum(): x = x + lax.ppermute(x, AXES, xor_pairs(n, bit))  48.9 us
    ppermute x8, starting transfers between devices, butterfly_sum(): other = lax.ppermute(x, AXES, xor_pairs(n, bit))  42.3 us
    ppermute x12, starting transfers between devices, butterfly_sum(): x = x + lax.ppermute(x, AXES, xor_pairs(n, bit))  35.5 us
    ppermute x8, starting transfers between devices, butterfly_sum(): x = keep + lax.ppermute(send, AXES, xor_pairs(n, bit))  29.8 us
    ppermute x8, waiting for transfers between devices, butterfly_sum(): x = keep + lax.ppermute(send, AXES, xor_pairs(n, bit))  24 us
    ppermute x8, waiting for transfers between devices, butterfly_sum(): other = lax.ppermute(x, AXES, xor_pairs(n, bit))  22.6 us
  transfers between devices with their start and end apart: 28, of which 28 were waited for; matrix products, arithmetic and copies ran while one was open for 0% of the time, Pallas kernels for 0%

profile of v1, /device:TPU:1, one launch (start us, length us, event | category | flops | bytes accessed | tf_op | source)
XLA Modules:
  0.0 227.8 jit_solution(15040149536109184140)
XLA Ops:
  2.2 2.0 convolution_bitcast_fusion
  4.3 16.0 %collective-permute-start = (f32[2816,32]{0,1:T(8,128)S(1)}, f32[2816,32]{0,1:T(8,128)}, u32[]{:S(2)}, u32[]{:S(2)}) collective-permute-start(f32[2816,32]{0,1:T(8,128)S(1)} %slice_select_fusion), channel_id=1, source_target_pairs={{0,1},{1,0},{2,3},{3,2},{4,5},{5,4},{6,7},{7,6},{8,9},{9,8},{10,11... | collective-permute-start | bytes 1081352 | tf_op jit(solution)/shard_map/ppermute | solution.py:38
  22.8 1.9 collective-permute-start.1
  24.8 5.7 %collective-permute-done.1 = f32[1408,32]{0,1:T(8,128)S(1)} collective-permute-done((f32[1408,32]{0,1:T(8,128)S(1)}, f32[1408,32]{0,1:T(8,128)S(1)}, u32[]{:S(2)}, u32[]{:S(2)}) %collective-permute-start.1) | collective-permute-done | bytes 180256 | tf_op jit(solution)/shard_map/ppermute | solution.py:38
  30.6 1.9 collective-permute-start.2
  32.5 3.4 %collective-permute-done.2 = f32[704,32]{0,1:T(8,128)S(1)} collective-permute-done((f32[704,32]{0,1:T(8,128)S(1)}, f32[704,32]{0,1:T(8,128)S(1)}, u32[]{:S(2)}, u32[]{:S(2)}) %collective-permute-start.2) | collective-permute-done | bytes 90144 | tf_op jit(solution)/shard_map/ppermute | solution.py:38
  36.1 1.9 collective-permute-start.3
  38.1 2.9 %collective-permute-done.3 = f32[352,32]{0,1:T(8,128)S(1)} collective-permute-done((f32[352,32]{0,1:T(8,128)S(1)}, f32[352,32]{0,1:T(8,128)S(1)}, u32[]{:S(2)}, u32[]{:S(2)}) %collective-permute-start.3) | collective-permute-done | bytes 45088 | tf_op jit(solution)/shard_map/ppermute | solution.py:38
  41.1 1.9 collective-permute-start.4
  43.0 4.0 %collective-permute-done.4 = f32[176,32]{0,1:T(8,128)S(1)} collective-permute-done((f32[176,32]{0,1:T(8,128)S(1)}, f32[176,32]{0,1:T(8,128)S(1)}, u32[]{:S(2)}, u32[]{:S(2)}) %collective-permute-start.4) | collective-permute-done | bytes 22560 | tf_op jit(solution)/shard_map/ppermute | solution.py:38
  49.0 3.7 %collective-permute-done.5 = f32[176,32]{0,1:T(8,128)S(1)} collective-permute-done((f32[176,32]{0,1:T(8,128)S(1)}, f32[176,32]{0,1:T(8,128)S(1)}, u32[]{:S(2)}, u32[]{:S(2)}) %collective-permute-start.5) | collective-permute-done | bytes 22560 | tf_op jit(solution)/shard_map/ppermute | solution.py:41
  54.6 3.7 %collective-permute-done.6 = f32[176,32]{0,1:T(8,128)S(1)} collective-permute-done((f32[176,32]{0,1:T(8,128)S(1)}, f32[176,32]{0,1:T(8,128)S(1)}, u32[]{:S(2)}, u32[]{:S(2)}) %collective-permute-start.6) | collective-permute-done | bytes 22560 | tf_op jit(solution)/shard_map/ppermute | solution.py:41
  60.3 6.6 %collective-permute-done.7 = f32[176,32]{0,1:T(8,128)S(1)} collective-permute-done((f32[176,32]{0,1:T(8,128)S(1)}, f32[176,32]{0,1:T(8,128)S(1)}, u32[]{:S(2)}, u32[]{:S(2)}) %collective-permute-start.7) | collective-permute-done | bytes 22560 | tf_op jit(solution)/shard_map/ppermute | solution.py:41
  66.9 3.8 %collective-permute-start.8 = (f32[176,32]{0,1:T(8,128)S(1)}, f32[176,32]{0,1:T(8,128)S(1)}, u32[]{:S(2)}, u32[]{:S(2)}) collective-permute-start(f32[176,32]{0,1:T(8,128)S(1)} %add.84), channel_id=1, source_target_pairs={{0,64},{1,65},{2,66},{3,67},{4,68},{5,69},{6,70},{7,71},{8,72},{9,... | collective-permute-start | bytes 67592 | tf_op jit(solution)/shard_map/ppermute | solution.py:41
  70.8 4.7 %collective-permute-done.8 = f32[176,32]{0,1:T(8,128)S(1)} collective-permute-done((f32[176,32]{0,1:T(8,128)S(1)}, f32[176,32]{0,1:T(8,128)S(1)}, u32[]{:S(2)}, u32[]{:S(2)}) %collective-permute-start.8) | collective-permute-done | bytes 22560 | tf_op jit(solution)/shard_map/ppermute | solution.py:41
  75.5 4.6 %collective-permute-start.9 = (f32[176,32]{0,1:T(8,128)S(1)}, f32[176,32]{0,1:T(8,128)S(1)}, u32[]{:S(2)}, u32[]{:S(2)}) collective-permute-start(f32[176,32]{0,1:T(8,128)S(1)} %add.85), channel_id=1, source_target_pairs={{0,512},{1,513},{2,514},{3,515},{4,516},{5,517},{6,518},{7,519},{8... | collective-permute-start | bytes 67592 | tf_op jit(solution)/shard_map/ppermute | solution.py:41
  80.1 3.9 %collective-permute-done.9 = f32[176,32]{0,1:T(8,128)S(1)} collective-permute-done((f32[176,32]{0,1:T(8,128)S(1)}, f32[176,32]{0,1:T(8,128)S(1)}, u32[]{:S(2)}, u32[]{:S(2)}) %collective-permute-start.9) | collective-permute-done | bytes 22560 | tf_op jit(solution)/shard_map/ppermute | solution.py:41
  86.0 3.9 %collective-permute-done.10 = f32[176,32]{0,1:T(8,128)S(1)} collective-permute-done((f32[176,32]{0,1:T(8,128)S(1)}, f32[176,32]{0,1:T(8,128)S(1)}, u32[]{:S(2)}, u32[]{:S(2)}) %collective-permute-start.10) | collective-permute-done | bytes 22560 | tf_op jit(solution)/shard_map/ppermute | solution.py:44
  89.9 1.9 collective-permute-start.11
  91.9 2.9 %collective-permute-done.11 = f32[352,32]{0,1:T(8,128)S(1)} collective-permute-done((f32[352,32]{0,1:T(8,128)S(1)}, f32[352,32]{0,1:T(8,128)S(1)}, u32[]{:S(2)}, u32[]{:S(2)}) %collective-permute-start.11) | collective-permute-done | bytes 45088 | tf_op jit(solution)/shard_map/ppermute | solution.py:44
  94.9 2.1 collective-permute-start.12
  97.0 3.7 %collective-permute-done.12 = f32[704,32]{0,1:T(8,128)S(1)} collective-permute-done((f32[704,32]{0,1:T(8,128)S(1)}, f32[704,32]{0,1:T(8,128)S(1)}, u32[]{:S(2)}, u32[]{:S(2)}) %collective-permute-start.12) | collective-permute-done | bytes 90144 | tf_op jit(solution)/shard_map/ppermute | solution.py:44
  100.8 1.9 collective-permute-start.13
  102.7 4.3 %collective-permute-done.13 = f32[1408,32]{0,1:T(8,128)S(1)} collective-permute-done((f32[1408,32]{0,1:T(8,128)S(1)}, f32[1408,32]{0,1:T(8,128)S(1)}, u32[]{:S(2)}, u32[]{:S(2)}) %collective-permute-start.13) | collective-permute-done | bytes 180256 | tf_op jit(solution)/shard_map/ppermute | solution.py:44
  107.1 16.3 %collective-permute-start.14 = (f32[2816,32]{0,1:T(8,128)S(1)}, f32[2816,32]{0,1:T(8,128)S(1)}, u32[]{:S(2)}, u32[]{:S(2)}) collective-permute-start(f32[2816,32]{0,1:T(8,128)S(1)} %maximum_select_fusion.3), channel_id=1, source_target_pairs={{0,1},{1,0},{2,3},{3,2},{4,5},{5,4},{6,7},{7,6},{8,9},{9,8},{10,11... | collective-permute-start | bytes 1081352 | tf_op jit(solution)/shard_map/ppermute | solution.py:44
  126.2 2.9 %cholesky.16 = f32[32,32]{1,0:T(8,128)S(1)} custom-call(f32[32,32]{1,0:T(8,128)S(1)} %fusion.11), custom_call_target="Cholesky" | custom-call | tf_op jit(solution)/shard_map/cholesky | solution.py:50
  130.4 2.4 %custom-call.5 = f32[1,32,32]{1,2,0:T(8,128)S(1)} custom-call(f32[1,32,32]{2,1,0:T(8,128)S(1)} %fusion.9), custom_call_target="InvertDiagBlocksLowerTriangular" | custom-call | tf_op jit(solution)/shard_map/triangular_solve | solution.py:51
  132.9 2.2 fusion
  137.9 2.3 %collective-permute-start.15 = (f32[704,32]{0,1:T(8,128)S(1)}, f32[704,32]{0,1:T(8,128)S(1)}, u32[]{:S(2)}, u32[]{:S(2)}) collective-permute-start(f32[704,32]{0,1:T(8,128)S(1)} %slice_select_fusion.2), channel_id=1, source_target_pairs={{0,1},{1,0},{2,3},{3,2},{4,5},{5,4},{6,7},{7,6},{8,9},{9,8},{10,11... | collective-permute-start | bytes 270344 | tf_op jit(solution)/shard_map/ppermute | solution.py:38
  142.3 1.9 collective-permute-start.16
  144.2 2.9 %collective-permute-done.16 = f32[352,32]{0,1:T(8,128)S(1)} collective-permute-done((f32[352,32]{0,1:T(8,128)S(1)}, f32[352,32]{0,1:T(8,128)S(1)}, u32[]{:S(2)}, u32[]{:S(2)}) %collective-permute-start.16) | collective-permute-done | bytes 45088 | tf_op jit(solution)/shard_map/ppermute | solution.py:38
  147.3 1.9 collective-permute-start.17
  149.2 2.7 %collective-permute-done.17 = f32[176,32]{0,1:T(8,128)S(1)} collective-permute-done((f32[176,32]{0,1:T(8,128)S(1)}, f32[176,32]{0,1:T(8,128)S(1)}, u32[]{:S(2)}, u32[]{:S(2)}) %collective-permute-start.17) | collective-permute-done | bytes 22560 | tf_op jit(solution)/shard_map/ppermute | solution.py:38
  153.9 2.7 %collective-permute-done.18 = f32[176,32]{0,1:T(8,128)S(1)} collective-permute-done((f32[176,32]{0,1:T(8,128)S(1)}, f32[176,32]{0,1:T(8,128)S(1)}, u32[]{:S(2)}, u32[]{:S(2)}) %collective-permute-start.18) | collective-permute-done | bytes 22560 | tf_op jit(solution)/shard_map/ppermute | solution.py:41
  158.6 3.7 %collective-permute-done.19 = f32[176,32]{0,1:T(8,128)S(1)} collective-permute-done((f32[176,32]{0,1:T(8,128)S(1)}, f32[176,32]{0,1:T(8,128)S(1)}, u32[]{:S(2)}, u32[]{:S(2)}) %collective-permute-start.19) | collective-permute-done | bytes 22560 | tf_op jit(solution)/shard_map/ppermute | solution.py:41
  164.2 3.7 %collective-permute-done.20 = f32[176,32]{0,1:T(8,128)S(1)} collective-permute-done((f32[176,32]{0,1:T(8,128)S(1)}, f32[176,32]{0,1:T(8,128)S(1)}, u32[]{:S(2)}, u32[]{:S(2)}) %collective-permute-start.20) | collective-permute-done | bytes 22560 | tf_op jit(solution)/shard_map/ppermute | solution.py:41
  169.8 3.8 %collective-permute-done.21 = f32[176,32]{0,1:T(8,128)S(1)} collective-permute-done((f32[176,32]{0,1:T(8,128)S(1)}, f32[176,32]{0,1:T(8,128)S(1)}, u32[]{:S(2)}, u32[]{:S(2)}) %collective-permute-start.21) | collective-permute-done | bytes 22560 | tf_op jit(solution)/shard_map/ppermute | solution.py:41
  173.6 4.4 %collective-permute-start.22 = (f32[176,32]{0,1:T(8,128)S(1)}, f32[176,32]{0,1:T(8,128)S(1)}, u32[]{:S(2)}, u32[]{:S(2)}) collective-permute-start(f32[176,32]{0,1:T(8,128)S(1)} %add.95), channel_id=1, source_target_pairs={{0,8},{1,9},{2,10},{3,11},{4,12},{5,13},{6,14},{7,15},{8,0},{9,1},... | collective-permute-start | bytes 67592 | tf_op jit(solution)/shard_map/ppermute | solution.py:41
  178.0 4.5 %collective-permute-done.22 = f32[176,32]{0,1:T(8,128)S(1)} collective-permute-done((f32[176,32]{0,1:T(8,128)S(1)}, f32[176,32]{0,1:T(8,128)S(1)}, u32[]{:S(2)}, u32[]{:S(2)}) %collective-permute-start.22) | collective-permute-done | bytes 22560 | tf_op jit(solution)/shard_map/ppermute | solution.py:41
  182.5 4.4 %collective-permute-start.23 = (f32[176,32]{0,1:T(8,128)S(1)}, f32[176,32]{0,1:T(8,128)S(1)}, u32[]{:S(2)}, u32[]{:S(2)}) collective-permute-start(f32[176,32]{0,1:T(8,128)S(1)} %add.96), channel_id=1, source_target_pairs={{0,64},{1,65},{2,66},{3,67},{4,68},{5,69},{6,70},{7,71},{8,72},{9,... | collective-permute-start | bytes 67592 | tf_op jit(solution)/shard_map/ppermute | solution.py:41
  186.9 4.2 %collective-permute-done.23 = f32[176,32]{0,1:T(8,128)S(1)} collective-permute-done((f32[176,32]{0,1:T(8,128)S(1)}, f32[176,32]{0,1:T(8,128)S(1)}, u32[]{:S(2)}, u32[]{:S(2)}) %collective-permute-start.23) | collective-permute-done | bytes 22560 | tf_op jit(solution)/shard_map/ppermute | solution.py:41
  191.1 5.0 %collective-permute-start.24 = (f32[176,32]{0,1:T(8,128)S(1)}, f32[176,32]{0,1:T(8,128)S(1)}, u32[]{:S(2)}, u32[]{:S(2)}) collective-permute-start(f32[176,32]{0,1:T(8,128)S(1)} %add.97), channel_id=1, source_target_pairs={{0,512},{1,513},{2,514},{3,515},{4,516},{5,517},{6,518},{7,519},{8... | collective-permute-start | bytes 67592 | tf_op jit(solution)/shard_map/ppermute | solution.py:41
  196.1 3.6 %collective-permute-done.24 = f32[176,32]{0,1:T(8,128)S(1)} collective-permute-done((f32[176,32]{0,1:T(8,128)S(1)}, f32[176,32]{0,1:T(8,128)S(1)}, u32[]{:S(2)}, u32[]{:S(2)}) %collective-permute-start.24) | collective-permute-done | bytes 22560 | tf_op jit(solution)/shard_map/ppermute | solution.py:41
  201.6 2.7 %collective-permute-done.25 = f32[176,32]{0,1:T(8,128)S(1)} collective-permute-done((f32[176,32]{0,1:T(8,128)S(1)}, f32[176,32]{0,1:T(8,128)S(1)}, u32[]{:S(2)}, u32[]{:S(2)}) %collective-permute-start.25) | collective-permute-done | bytes 22560 | tf_op jit(solution)/shard_map/ppermute | solution.py:44
  204.4 2.1 collective-permute-start.26
  206.5 2.9 %collective-permute-done.26 = f32[352,32]{0,1:T(8,128)S(1)} collective-permute-done((f32[352,32]{0,1:T(8,128)S(1)}, f32[352,32]{0,1:T(8,128)S(1)}, u32[]{:S(2)}, u32[]{:S(2)}) %collective-permute-start.26) | collective-permute-done | bytes 45088 | tf_op jit(solution)/shard_map/ppermute | solution.py:44
  209.4 14.2 %collective-permute-start.27 = (f32[704,32]{0,1:T(8,128)S(1)}, f32[704,32]{0,1:T(8,128)S(1)}, u32[]{:S(2)}, u32[]{:S(2)}) collective-permute-start(f32[704,32]{0,1:T(8,128)S(1)} %maximum_select_fusion.7), channel_id=1, source_target_pairs={{0,1},{1,0},{2,3},{3,2},{4,5},{5,4},{6,7},{7,6},{8,9},{9,8},{10,11... | collective-permute-start | bytes 270344 | tf_op jit(solution)/shard_map/ppermute | solution.py:44
  224.7 3.1 %fusion.7 = f32[352,1408]{1,0:T(8,128)} fusion(f32[1408,32]{0,1:T(8,128)S(1)} %fusion.6, f32[5632,32]{0,1:T(8,128)S(1)} %fusion, s32[]{:T(128)S(6)} %select_n.172), kind=kOutput, calls=%fused_computation.27 | convolution fusion | flops 190316544 | bytes 2211844 | tf_op jit(solution)/shard_map/dot_general | solution.py:74
  (65 shorter events, 32.6 us)
Async XLA Ops:
  0.6 1.6 copy-start
  4.3 17.4 %collective-permute-start = (f32[2816,32]{0,1:T(8,128)S(1)}, f32[2816,32]{0,1:T(8,128)}, u32[]{:S(2)}, u32[]{:S(2)}) collective-permute-start(f32[2816,32]{0,1:T(8,128)S(1)} %slice_select_fusion), channel_id=1, source_target_pairs={{0,1},{1,0},{2,3},{3,2},{4,5},{5,4},{6,7},{7,6},{8,9},{9,8},{10,11... | collective-permute-start | bytes 1081352 | tf_op jit(solution)/shard_map/ppermute | solution.py:38
  22.8 7.6 %collective-permute-start.1 = (f32[1408,32]{0,1:T(8,128)S(1)}, f32[1408,32]{0,1:T(8,128)S(1)}, u32[]{:S(2)}, u32[]{:S(2)}) collective-permute-start(f32[1408,32]{0,1:T(8,128)S(1)} %slice_select_fusion.1), channel_id=1, source_target_pairs={{0,2},{1,3},{2,0},{3,1},{4,6},{5,7},{6,4},{7,5},{8,10},{9,11},{10,... | collective-permute-start | bytes 540680 | tf_op jit(solution)/shard_map/ppermute | solution.py:38
  30.6 5.4 %collective-permute-start.2 = (f32[704,32]{0,1:T(8,128)S(1)}, f32[704,32]{0,1:T(8,128)S(1)}, u32[]{:S(2)}, u32[]{:S(2)}) collective-permute-start(f32[704,32]{0,1:T(8,128)S(1)} %slice_select_fusion.3), channel_id=1, source_target_pairs={{0,16},{1,17},{2,18},{3,19},{4,20},{5,21},{6,22},{7,23},{8,24},{9,... | collective-permute-start | bytes 270344 | tf_op jit(solution)/shard_map/ppermute | solution.py:38
  36.1 4.8 %collective-permute-start.3 = (f32[352,32]{0,1:T(8,128)S(1)}, f32[352,32]{0,1:T(8,128)S(1)}, u32[]{:S(2)}, u32[]{:S(2)}) collective-permute-start(f32[352,32]{0,1:T(8,128)S(1)} %slice_select_fusion.5), channel_id=1, source_target_pairs={{0,128},{1,129},{2,130},{3,131},{4,132},{5,133},{6,134},{7,135},{8... | collective-permute-start | bytes 135176 | tf_op jit(solution)/shard_map/ppermute | solution.py:38
  41.1 5.9 %collective-permute-start.4 = (f32[176,32]{0,1:T(8,128)S(1)}, f32[176,32]{0,1:T(8,128)S(1)}, u32[]{:S(2)}, u32[]{:S(2)}) collective-permute-start(f32[176,32]{0,1:T(8,128)S(1)} %slice_select_fusion.7), channel_id=1, source_target_pairs={{0,4},{1,5},{2,6},{3,7},{4,0},{5,1},{6,2},{7,3},{8,12},{9,13},{10,... | collective-permute-start | bytes 67592 | tf_op jit(solution)/shard_map/ppermute | solution.py:38
  47.1 5.6 %collective-permute-start.5 = (f32[176,32]{0,1:T(8,128)S(1)}, f32[176,32]{0,1:T(8,128)S(1)}, u32[]{:S(2)}, u32[]{:S(2)}) collective-permute-start(f32[176,32]{0,1:T(8,128)S(1)} %select_add_fusion.7), channel_id=1, source_target_pairs={{0,32},{1,33},{2,34},{3,35},{4,36},{5,37},{6,38},{7,39},{8,40},{9,... | collective-permute-start | bytes 67592 | tf_op jit(solution)/shard_map/ppermute | solution.py:41
  52.7 5.6 %collective-permute-start.6 = (f32[176,32]{0,1:T(8,128)S(1)}, f32[176,32]{0,1:T(8,128)S(1)}, u32[]{:S(2)}, u32[]{:S(2)}) collective-permute-start(f32[176,32]{0,1:T(8,128)S(1)} %add.82), channel_id=1, source_target_pairs={{0,256},{1,257},{2,258},{3,259},{4,260},{5,261},{6,262},{7,263},{8... | collective-permute-start | bytes 67592 | tf_op jit(solution)/shard_map/ppermute | solution.py:41
  58.4 8.6 %collective-permute-start.7 = (f32[176,32]{0,1:T(8,128)S(1)}, f32[176,32]{0,1:T(8,128)S(1)}, u32[]{:S(2)}, u32[]{:S(2)}) collective-permute-start(f32[176,32]{0,1:T(8,128)S(1)} %add.83), channel_id=1, source_target_pairs={{0,8},{1,9},{2,10},{3,11},{4,12},{5,13},{6,14},{7,15},{8,0},{9,1},... | collective-permute-start | bytes 67592 | tf_op jit(solution)/shard_map/ppermute | solution.py:41
  66.9 8.6 %collective-permute-start.8 = (f32[176,32]{0,1:T(8,128)S(1)}, f32[176,32]{0,1:T(8,128)S(1)}, u32[]{:S(2)}, u32[]{:S(2)}) collective-permute-start(f32[176,32]{0,1:T(8,128)S(1)} %add.84), channel_id=1, source_target_pairs={{0,64},{1,65},{2,66},{3,67},{4,68},{5,69},{6,70},{7,71},{8,72},{9,... | collective-permute-start | bytes 67592 | tf_op jit(solution)/shard_map/ppermute | solution.py:41
  75.5 8.6 %collective-permute-start.9 = (f32[176,32]{0,1:T(8,128)S(1)}, f32[176,32]{0,1:T(8,128)S(1)}, u32[]{:S(2)}, u32[]{:S(2)}) collective-permute-start(f32[176,32]{0,1:T(8,128)S(1)} %add.85), channel_id=1, source_target_pairs={{0,512},{1,513},{2,514},{3,515},{4,516},{5,517},{6,518},{7,519},{8... | collective-permute-start | bytes 67592 | tf_op jit(solution)/shard_map/ppermute | solution.py:41
  84.0 5.8 %collective-permute-start.10 = (f32[176,32]{0,1:T(8,128)S(1)}, f32[176,32]{0,1:T(8,128)S(1)}, u32[]{:S(2)}, u32[]{:S(2)}) collective-permute-start(f32[176,32]{0,1:T(8,128)S(1)} %add.86), channel_id=1, source_target_pairs={{0,4},{1,5},{2,6},{3,7},{4,0},{5,1},{6,2},{7,3},{8,12},{9,13},{10,... | collective-permute-start | bytes 67592 | tf_op jit(solution)/shard_map/ppermute | solution.py:44
  89.9 4.8 %collective-permute-start.11 = (f32[352,32]{0,1:T(8,128)S(1)}, f32[352,32]{0,1:T(8,128)S(1)}, u32[]{:S(2)}, u32[]{:S(2)}) collective-permute-start(f32[352,32]{0,1:T(8,128)S(1)} %maximum_select_fusion.8), channel_id=1, source_target_pairs={{0,128},{1,129},{2,130},{3,131},{4,132},{5,133},{6,134},{7,135},{8... | collective-permute-start | bytes 135176 | tf_op jit(solution)/shard_map/ppermute | solution.py:44
  94.9 40.2 %copy-start.1 = (bf16[192,1408]{1,0:T(8,128)(2,1)S(1)}, bf16[192,1408]{1,0:T(8,128)(2,1)}, u32[]{:S(2)}) copy-start(bf16[192,1408]{1,0:T(8,128)(2,1)} %param.4) | copy-start | bytes 1622020
  94.9 5.8 %collective-permute-start.12 = (f32[704,32]{0,1:T(8,128)S(1)}, f32[704,32]{0,1:T(8,128)S(1)}, u32[]{:S(2)}, u32[]{:S(2)}) collective-permute-start(f32[704,32]{0,1:T(8,128)S(1)} %maximum_select_fusion.6), channel_id=1, source_target_pairs={{0,16},{1,17},{2,18},{3,19},{4,20},{5,21},{6,22},{7,23},{8,24},{9,... | collective-permute-start | bytes 270344 | tf_op jit(solution)/shard_map/ppermute | solution.py:44
  100.8 6.2 %collective-permute-start.13 = (f32[1408,32]{0,1:T(8,128)S(1)}, f32[1408,32]{0,1:T(8,128)S(1)}, u32[]{:S(2)}, u32[]{:S(2)}) collective-permute-start(f32[1408,32]{0,1:T(8,128)S(1)} %maximum_select_fusion.4), channel_id=1, source_target_pairs={{0,2},{1,3},{2,0},{3,1},{4,6},{5,7},{6,4},{7,5},{8,10},{9,11},{10,... | collective-permute-start | bytes 540680 | tf_op jit(solution)/shard_map/ppermute | solution.py:44
  107.1 17.6 %copy-start.2 = (f32[2816,32]{0,1:T(8,128)}, f32[2816,32]{0,1:T(8,128)S(1)}, u32[]{:S(2)}) copy-start(f32[2816,32]{0,1:T(8,128)S(1)} %maximum_select_fusion.3) | copy-start | bytes 1081348
  107.1 17.6 %collective-permute-start.14 = (f32[2816,32]{0,1:T(8,128)S(1)}, f32[2816,32]{0,1:T(8,128)S(1)}, u32[]{:S(2)}, u32[]{:S(2)}) collective-permute-start(f32[2816,32]{0,1:T(8,128)S(1)} %maximum_select_fusion.3), channel_id=1, source_target_pairs={{0,1},{1,0},{2,3},{3,2},{4,5},{5,4},{6,7},{7,6},{8,9},{9,8},{10,11... | collective-permute-start | bytes 1081352 | tf_op jit(solution)/shard_map/ppermute | solution.py:44
  124.7 0.7 copy-start.4
  137.9 3.2 %collective-permute-start.15 = (f32[704,32]{0,1:T(8,128)S(1)}, f32[704,32]{0,1:T(8,128)S(1)}, u32[]{:S(2)}, u32[]{:S(2)}) collective-permute-start(f32[704,32]{0,1:T(8,128)S(1)} %slice_select_fusion.2), channel_id=1, source_target_pairs={{0,1},{1,0},{2,3},{3,2},{4,5},{5,4},{6,7},{7,6},{8,9},{9,8},{10,11... | collective-permute-start | bytes 270344 | tf_op jit(solution)/shard_map/ppermute | solution.py:38
  142.3 4.8 %collective-permute-start.16 = (f32[352,32]{0,1:T(8,128)S(1)}, f32[352,32]{0,1:T(8,128)S(1)}, u32[]{:S(2)}, u32[]{:S(2)}) collective-permute-start(f32[352,32]{0,1:T(8,128)S(1)} %slice_select_fusion.4), channel_id=1, source_target_pairs={{0,2},{1,3},{2,0},{3,1},{4,6},{5,7},{6,4},{7,5},{8,10},{9,11},{10,... | collective-permute-start | bytes 135176 | tf_op jit(solution)/shard_map/ppermute | solution.py:38
  147.3 4.7 %collective-permute-start.17 = (f32[176,32]{0,1:T(8,128)S(1)}, f32[176,32]{0,1:T(8,128)S(1)}, u32[]{:S(2)}, u32[]{:S(2)}) collective-permute-start(f32[176,32]{0,1:T(8,128)S(1)} %slice_select_fusion.6), channel_id=1, source_target_pairs={{0,16},{1,17},{2,18},{3,19},{4,20},{5,21},{6,22},{7,23},{8,24},{9,... | collective-permute-start | bytes 67592 | tf_op jit(solution)/shard_map/ppermute | solution.py:38
  152.0 4.7 %collective-permute-start.18 = (f32[176,32]{0,1:T(8,128)S(1)}, f32[176,32]{0,1:T(8,128)S(1)}, u32[]{:S(2)}, u32[]{:S(2)}) collective-permute-start(f32[176,32]{0,1:T(8,128)S(1)} %select_add_fusion.6), channel_id=1, source_target_pairs={{0,128},{1,129},{2,130},{3,131},{4,132},{5,133},{6,134},{7,135},{8... | collective-permute-start | bytes 67592 | tf_op jit(solution)/shard_map/ppermute | solution.py:41
  156.7 5.6 %collective-permute-start.19 = (f32[176,32]{0,1:T(8,128)S(1)}, f32[176,32]{0,1:T(8,128)S(1)}, u32[]{:S(2)}, u32[]{:S(2)}) collective-permute-start(f32[176,32]{0,1:T(8,128)S(1)} %add.92), channel_id=1, source_target_pairs={{0,4},{1,5},{2,6},{3,7},{4,0},{5,1},{6,2},{7,3},{8,12},{9,13},{10,... | collective-permute-start | bytes 67592 | tf_op jit(solution)/shard_map/ppermute | solution.py:41
  162.3 5.6 %collective-permute-start.20 = (f32[176,32]{0,1:T(8,128)S(1)}, f32[176,32]{0,1:T(8,128)S(1)}, u32[]{:S(2)}, u32[]{:S(2)}) collective-permute-start(f32[176,32]{0,1:T(8,128)S(1)} %add.93), channel_id=1, source_target_pairs={{0,32},{1,33},{2,34},{3,35},{4,36},{5,37},{6,38},{7,39},{8,40},{9,... | collective-permute-start | bytes 67592 | tf_op jit(solution)/shard_map/ppermute | solution.py:41
  167.9 5.7 %collective-permute-start.21 = (f32[176,32]{0,1:T(8,128)S(1)}, f32[176,32]{0,1:T(8,128)S(1)}, u32[]{:S(2)}, u32[]{:S(2)}) collective-permute-start(f32[176,32]{0,1:T(8,128)S(1)} %add.94), channel_id=1, source_target_pairs={{0,256},{1,257},{2,258},{3,259},{4,260},{5,261},{6,262},{7,263},{8... | collective-permute-start | bytes 67592 | tf_op jit(solution)/shard_map/ppermute | solution.py:41
  173.6 8.9 %collective-permute-start.22 = (f32[176,32]{0,1:T(8,128)S(1)}, f32[176,32]{0,1:T(8,128)S(1)}, u32[]{:S(2)}, u32[]{:S(2)}) collective-permute-start(f32[176,32]{0,1:T(8,128)S(1)} %add.95), channel_id=1, source_target_pairs={{0,8},{1,9},{2,10},{3,11},{4,12},{5,13},{6,14},{7,15},{8,0},{9,1},... | collective-permute-start | bytes 67592 | tf_op jit(solution)/shard_map/ppermute | solution.py:41
  182.5 8.6 %collective-permute-start.23 = (f32[176,32]{0,1:T(8,128)S(1)}, f32[176,32]{0,1:T(8,128)S(1)}, u32[]{:S(2)}, u32[]{:S(2)}) collective-permute-start(f32[176,32]{0,1:T(8,128)S(1)} %add.96), channel_id=1, source_target_pairs={{0,64},{1,65},{2,66},{3,67},{4,68},{5,69},{6,70},{7,71},{8,72},{9,... | collective-permute-start | bytes 67592 | tf_op jit(solution)/shard_map/ppermute | solution.py:41
  191.1 8.6 %collective-permute-start.24 = (f32[176,32]{0,1:T(8,128)S(1)}, f32[176,32]{0,1:T(8,128)S(1)}, u32[]{:S(2)}, u32[]{:S(2)}) collective-permute-start(f32[176,32]{0,1:T(8,128)S(1)} %add.97), channel_id=1, source_target_pairs={{0,512},{1,513},{2,514},{3,515},{4,516},{5,517},{6,518},{7,519},{8... | collective-permute-start | bytes 67592 | tf_op jit(solution)/shard_map/ppermute | solution.py:41
  199.7 4.6 %collective-permute-start.25 = (f32[176,32]{0,1:T(8,128)S(1)}, f32[176,32]{0,1:T(8,128)S(1)}, u32[]{:S(2)}, u32[]{:S(2)}) collective-permute-start(f32[176,32]{0,1:T(8,128)S(1)} %add.98), channel_id=1, source_target_pairs={{0,16},{1,17},{2,18},{3,19},{4,20},{5,21},{6,22},{7,23},{8,24},{9,... | collective-permute-start | bytes 67592 | tf_op jit(solution)/shard_map/ppermute | solution.py:44
  204.4 4.9 %collective-permute-start.26 = (f32[352,32]{0,1:T(8,128)S(1)}, f32[352,32]{0,1:T(8,128)S(1)}, u32[]{:S(2)}, u32[]{:S(2)}) collective-permute-start(f32[352,32]{0,1:T(8,128)S(1)} %maximum_select_fusion.9), channel_id=1, source_target_pairs={{0,2},{1,3},{2,0},{3,1},{4,6},{5,7},{6,4},{7,5},{8,10},{9,11},{10,... | collective-permute-start | bytes 135176 | tf_op jit(solution)/shard_map/ppermute | solution.py:44
  209.4 15.1 %collective-permute-start.27 = (f32[704,32]{0,1:T(8,128)S(1)}, f32[704,32]{0,1:T(8,128)S(1)}, u32[]{:S(2)}, u32[]{:S(2)}) collective-permute-start(f32[704,32]{0,1:T(8,128)S(1)} %maximum_select_fusion.7), channel_id=1, source_target_pairs={{0,1},{1,0},{2,3},{3,2},{4,5},{5,4},{6,7},{7,6},{8,9},{9,8},{10,11... | collective-permute-start | bytes 270344 | tf_op jit(solution)/shard_map/ppermute | solution.py:44
  224.7 3.1 %copy-start.3 = (f32[1408,32]{0,1:T(8,128)}, f32[1408,32]{0,1:T(8,128)S(1)}, u32[]{:S(2)}) copy-start(f32[1408,32]{0,1:T(8,128)S(1)} %fusion.6) | copy-start | bytes 540676

commit v2 on v1

--- a/solution.py
+++ b/solution.py
@@ -63,7 +63,7 @@
         hidden = activations.shape[1]
         block_rows = hidden // n_sub
         p_sum = butterfly_sum(p_local, order, n, 5)
-        gram = jnp.dot(p_sum.T, p_sum, precision=lax.Precision.HIGHEST)
+        gram = jnp.dot(p_sum.T, p_sum, precision=lax.Precision.HIGH)
         p_hat = orthonormal(p_sum, gram)
         p_low = p_hat.astype(jnp.bfloat16)
         my_hat = lax.dynamic_slice_in_dim(p_hat, lax.axis_index("sub") * block_rows, block_rows, 0)
@@ -71,7 +71,7 @@
         q_local = jnp.einsum("tc,tr->cr", grad_out, v_low, preferred_element_type=jnp.float32)
         q_sum = butterfly_sum(q_local, order, n, 3)
         q_new = q_sum / n
-        grad_approx = jnp.dot(my_hat, q_new.T, precision=lax.Precision.HIGHEST)
+        grad_approx = jnp.dot(my_hat, q_new.T, precision=lax.Precision.HIGH)
         return (grad_approx, q_new)
 
     return per_device

time: 229 us -> 228 us (level)
  no operation moved by 1% of the time
where the time goes in v2:
time: 228 us; the launch traced here: 227 us
  starting transfers between devices  108 us (47%)
  waiting for transfers between devices  95.4 us (42%)
  other arithmetic  11.4 us (5%)
  matrix products  8.74 us (4%)
  local copies, waits for them, and re-layouts  2.42 us (1%)
    ppermute x12, waiting for transfers between devices, butterfly_sum(): x = x + lax.ppermute(x, AXES, xor_pairs(n, bit))  48.9 us
    ppermute x8, starting transfers between devices, butterfly_sum(): other = lax.ppermute(x, AXES, xor_pairs(n, bit))  42.3 us
    ppermute x12, starting transfers between devices, butterfly_sum(): x = x + lax.ppermute(x, AXES, xor_pairs(n, bit))  35.5 us
    ppermute x8, starting transfers between devices, butterfly_sum(): x = keep + lax.ppermute(send, AXES, xor_pairs(n, bit))  29.8 us
    ppermute x8, waiting for transfers between devices, butterfly_sum(): x = keep + lax.ppermute(send, AXES, xor_pairs(n, bit))  24 us
    ppermute x8, waiting for transfers between devices, butterfly_sum(): other = lax.ppermute(x, AXES, xor_pairs(n, bit))  22.6 us
  transfers between devices with their start and end apart: 28, of which 28 were waited for; matrix products, arithmetic and copies ran while one was open for 0% of the time, Pallas kernels for 0%

profile of v2, /device:TPU:1, one launch (start us, length us, event | category | flops | bytes accessed | tf_op | source)
XLA Modules:
  0.0 226.8 jit_solution(2321495482956975543)
XLA Ops:
  2.2 2.0 convolution_bitcast_fusion
  4.3 16.0 %collective-permute-start = (f32[2816,32]{0,1:T(8,128)S(1)}, f32[2816,32]{0,1:T(8,128)}, u32[]{:S(2)}, u32[]{:S(2)}) collective-permute-start(f32[2816,32]{0,1:T(8,128)S(1)} %slice_select_fusion), channel_id=1, source_target_pairs={{0,1},{1,0},{2,3},{3,2},{4,5},{5,4},{6,7},{7,6},{8,9},{9,8},{10,11... | collective-permute-start | bytes 1081352 | tf_op jit(solution)/shard_map/ppermute | solution.py:38
  22.8 1.9 collective-permute-start.1
  24.8 5.7 %collective-permute-done.1 = f32[1408,32]{0,1:T(8,128)S(1)} collective-permute-done((f32[1408,32]{0,1:T(8,128)S(1)}, f32[1408,32]{0,1:T(8,128)S(1)}, u32[]{:S(2)}, u32[]{:S(2)}) %collective-permute-start.1) | collective-permute-done | bytes 180256 | tf_op jit(solution)/shard_map/ppermute | solution.py:38
  30.6 1.9 collective-permute-start.2
  32.5 3.4 %collective-permute-done.2 = f32[704,32]{0,1:T(8,128)S(1)} collective-permute-done((f32[704,32]{0,1:T(8,128)S(1)}, f32[704,32]{0,1:T(8,128)S(1)}, u32[]{:S(2)}, u32[]{:S(2)}) %collective-permute-start.2) | collective-permute-done | bytes 90144 | tf_op jit(solution)/shard_map/ppermute | solution.py:38
  36.1 1.9 collective-permute-start.3
  38.1 2.9 %collective-permute-done.3 = f32[352,32]{0,1:T(8,128)S(1)} collective-permute-done((f32[352,32]{0,1:T(8,128)S(1)}, f32[352,32]{0,1:T(8,128)S(1)}, u32[]{:S(2)}, u32[]{:S(2)}) %collective-permute-start.3) | collective-permute-done | bytes 45088 | tf_op jit(solution)/shard_map/ppermute | solution.py:38
  41.1 1.9 collective-permute-start.4
  43.0 4.0 %collective-permute-done.4 = f32[176,32]{0,1:T(8,128)S(1)} collective-permute-done((f32[176,32]{0,1:T(8,128)S(1)}, f32[176,32]{0,1:T(8,128)S(1)}, u32[]{:S(2)}, u32[]{:S(2)}) %collective-permute-start.4) | collective-permute-done | bytes 22560 | tf_op jit(solution)/shard_map/ppermute | solution.py:38
  49.0 3.7 %collective-permute-done.5 = f32[176,32]{0,1:T(8,128)S(1)} collective-permute-done((f32[176,32]{0,1:T(8,128)S(1)}, f32[176,32]{0,1:T(8,128)S(1)}, u32[]{:S(2)}, u32[]{:S(2)}) %collective-permute-start.5) | collective-permute-done | bytes 22560 | tf_op jit(solution)/shard_map/ppermute | solution.py:41
  54.6 3.7 %collective-permute-done.6 = f32[176,32]{0,1:T(8,128)S(1)} collective-permute-done((f32[176,32]{0,1:T(8,128)S(1)}, f32[176,32]{0,1:T(8,128)S(1)}, u32[]{:S(2)}, u32[]{:S(2)}) %collective-permute-start.6) | collective-permute-done | bytes 22560 | tf_op jit(solution)/shard_map/ppermute | solution.py:41
  60.3 6.6 %collective-permute-done.7 = f32[176,32]{0,1:T(8,128)S(1)} collective-permute-done((f32[176,32]{0,1:T(8,128)S(1)}, f32[176,32]{0,1:T(8,128)S(1)}, u32[]{:S(2)}, u32[]{:S(2)}) %collective-permute-start.7) | collective-permute-done | bytes 22560 | tf_op jit(solution)/shard_map/ppermute | solution.py:41
  66.9 3.8 %collective-permute-start.8 = (f32[176,32]{0,1:T(8,128)S(1)}, f32[176,32]{0,1:T(8,128)S(1)}, u32[]{:S(2)}, u32[]{:S(2)}) collective-permute-start(f32[176,32]{0,1:T(8,128)S(1)} %add.84), channel_id=1, source_target_pairs={{0,64},{1,65},{2,66},{3,67},{4,68},{5,69},{6,70},{7,71},{8,72},{9,... | collective-permute-start | bytes 67592 | tf_op jit(solution)/shard_map/ppermute | solution.py:41
  70.8 4.7 %collective-permute-done.8 = f32[176,32]{0,1:T(8,128)S(1)} collective-permute-done((f32[176,32]{0,1:T(8,128)S(1)}, f32[176,32]{0,1:T(8,128)S(1)}, u32[]{:S(2)}, u32[]{:S(2)}) %collective-permute-start.8) | collective-permute-done | bytes 22560 | tf_op jit(solution)/shard_map/ppermute | solution.py:41
  75.5 4.6 %collective-permute-start.9 = (f32[176,32]{0,1:T(8,128)S(1)}, f32[176,32]{0,1:T(8,128)S(1)}, u32[]{:S(2)}, u32[]{:S(2)}) collective-permute-start(f32[176,32]{0,1:T(8,128)S(1)} %add.85), channel_id=1, source_target_pairs={{0,512},{1,513},{2,514},{3,515},{4,516},{5,517},{6,518},{7,519},{8... | collective-permute-start | bytes 67592 | tf_op jit(solution)/shard_map/ppermute | solution.py:41
  80.1 3.9 %collective-permute-done.9 = f32[176,32]{0,1:T(8,128)S(1)} collective-permute-done((f32[176,32]{0,1:T(8,128)S(1)}, f32[176,32]{0,1:T(8,128)S(1)}, u32[]{:S(2)}, u32[]{:S(2)}) %collective-permute-start.9) | collective-permute-done | bytes 22560 | tf_op jit(solution)/shard_map/ppermute | solution.py:41
  86.0 3.9 %collective-permute-done.10 = f32[176,32]{0,1:T(8,128)S(1)} collective-permute-done((f32[176,32]{0,1:T(8,128)S(1)}, f32[176,32]{0,1:T(8,128)S(1)}, u32[]{:S(2)}, u32[]{:S(2)}) %collective-permute-start.10) | collective-permute-done | bytes 22560 | tf_op jit(solution)/shard_map/ppermute | solution.py:44
  89.9 1.9 collective-permute-start.11
  91.9 2.9 %collective-permute-done.11 = f32[352,32]{0,1:T(8,128)S(1)} collective-permute-done((f32[352,32]{0,1:T(8,128)S(1)}, f32[352,32]{0,1:T(8,128)S(1)}, u32[]{:S(2)}, u32[]{:S(2)}) %collective-permute-start.11) | collective-permute-done | bytes 45088 | tf_op jit(solution)/shard_map/ppermute | solution.py:44
  94.9 2.1 collective-permute-start.12
  97.0 3.7 %collective-permute-done.12 = f32[704,32]{0,1:T(8,128)S(1)} collective-permute-done((f32[704,32]{0,1:T(8,128)S(1)}, f32[704,32]{0,1:T(8,128)S(1)}, u32[]{:S(2)}, u32[]{:S(2)}) %collective-permute-start.12) | collective-permute-done | bytes 90144 | tf_op jit(solution)/shard_map/ppermute | solution.py:44
  100.8 1.9 collective-permute-start.13
  102.7 4.3 %collective-permute-done.13 = f32[1408,32]{0,1:T(8,128)S(1)} collective-permute-done((f32[1408,32]{0,1:T(8,128)S(1)}, f32[1408,32]{0,1:T(8,128)S(1)}, u32[]{:S(2)}, u32[]{:S(2)}) %collective-permute-start.13) | collective-permute-done | bytes 180256 | tf_op jit(solution)/shard_map/ppermute | solution.py:44
  107.1 16.3 %collective-permute-start.14 = (f32[2816,32]{0,1:T(8,128)S(1)}, f32[2816,32]{0,1:T(8,128)S(1)}, u32[]{:S(2)}, u32[]{:S(2)}) collective-permute-start(f32[2816,32]{0,1:T(8,128)S(1)} %maximum_select_fusion.3), channel_id=1, source_target_pairs={{0,1},{1,0},{2,3},{3,2},{4,5},{5,4},{6,7},{7,6},{8,9},{9,8},{10,11... | collective-permute-start | bytes 1081352 | tf_op jit(solution)/shard_map/ppermute | solution.py:44
  125.9 2.9 %cholesky.16 = f32[32,32]{1,0:T(8,128)S(1)} custom-call(f32[32,32]{1,0:T(8,128)S(1)} %fusion.11), custom_call_target="Cholesky" | custom-call | tf_op jit(solution)/shard_map/cholesky | solution.py:50
  130.2 2.4 %custom-call.5 = f32[1,32,32]{1,2,0:T(8,128)S(1)} custom-call(f32[1,32,32]{2,1,0:T(8,128)S(1)} %fusion.9), custom_call_target="InvertDiagBlocksLowerTriangular" | custom-call | tf_op jit(solution)/shard_map/triangular_solve | solution.py:51
  132.6 2.2 fusion
  137.7 2.3 %collective-permute-start.15 = (f32[704,32]{0,1:T(8,128)S(1)}, f32[704,32]{0,1:T(8,128)S(1)}, u32[]{:S(2)}, u32[]{:S(2)}) collective-permute-start(f32[704,32]{0,1:T(8,128)S(1)} %slice_select_fusion.2), channel_id=1, source_target_pairs={{0,1},{1,0},{2,3},{3,2},{4,5},{5,4},{6,7},{7,6},{8,9},{9,8},{10,11... | collective-permute-start | bytes 270344 | tf_op jit(solution)/shard_map/ppermute | solution.py:38
  142.0 1.9 collective-permute-start.16
  143.9 2.9 %collective-permute-done.16 = f32[352,32]{0,1:T(8,128)S(1)} collective-permute-done((f32[352,32]{0,1:T(8,128)S(1)}, f32[352,32]{0,1:T(8,128)S(1)}, u32[]{:S(2)}, u32[]{:S(2)}) %collective-permute-start.16) | collective-permute-done | bytes 45088 | tf_op jit(solution)/shard_map/ppermute | solution.py:38
  147.0 1.9 collective-permute-start.17
  148.9 2.7 %collective-permute-done.17 = f32[176,32]{0,1:T(8,128)S(1)} collective-permute-done((f32[176,32]{0,1:T(8,128)S(1)}, f32[176,32]{0,1:T(8,128)S(1)}, u32[]{:S(2)}, u32[]{:S(2)}) %collective-permute-start.17) | collective-permute-done | bytes 22560 | tf_op jit(solution)/shard_map/ppermute | solution.py:38
  153.7 2.7 %collective-permute-done.18 = f32[176,32]{0,1:T(8,128)S(1)} collective-permute-done((f32[176,32]{0,1:T(8,128)S(1)}, f32[176,32]{0,1:T(8,128)S(1)}, u32[]{:S(2)}, u32[]{:S(2)}) %collective-permute-start.18) | collective-permute-done | bytes 22560 | tf_op jit(solution)/shard_map/ppermute | solution.py:41
  158.3 3.7 %collective-permute-done.19 = f32[176,32]{0,1:T(8,128)S(1)} collective-permute-done((f32[176,32]{0,1:T(8,128)S(1)}, f32[176,32]{0,1:T(8,128)S(1)}, u32[]{:S(2)}, u32[]{:S(2)}) %collective-permute-start.19) | collective-permute-done | bytes 22560 | tf_op jit(solution)/shard_map/ppermute | solution.py:41
  163.9 3.7 %collective-permute-done.20 = f32[176,32]{0,1:T(8,128)S(1)} collective-permute-done((f32[176,32]{0,1:T(8,128)S(1)}, f32[176,32]{0,1:T(8,128)S(1)}, u32[]{:S(2)}, u32[]{:S(2)}) %collective-permute-start.20) | collective-permute-done | bytes 22560 | tf_op jit(solution)/shard_map/ppermute | solution.py:41
  169.6 3.8 %collective-permute-done.21 = f32[176,32]{0,1:T(8,128)S(1)} collective-permute-done((f32[176,32]{0,1:T(8,128)S(1)}, f32[176,32]{0,1:T(8,128)S(1)}, u32[]{:S(2)}, u32[]{:S(2)}) %collective-permute-start.21) | collective-permute-done | bytes 22560 | tf_op jit(solution)/shard_map/ppermute | solution.py:41
  173.4 4.4 %collective-permute-start.22 = (f32[176,32]{0,1:T(8,128)S(1)}, f32[176,32]{0,1:T(8,128)S(1)}, u32[]{:S(2)}, u32[]{:S(2)}) collective-permute-start(f32[176,32]{0,1:T(8,128)S(1)} %add.95), channel_id=1, source_target_pairs={{0,8},{1,9},{2,10},{3,11},{4,12},{5,13},{6,14},{7,15},{8,0},{9,1},... | collective-permute-start | bytes 67592 | tf_op jit(solution)/shard_map/ppermute | solution.py:41
  177.7 4.5 %collective-permute-done.22 = f32[176,32]{0,1:T(8,128)S(1)} collective-permute-done((f32[176,32]{0,1:T(8,128)S(1)}, f32[176,32]{0,1:T(8,128)S(1)}, u32[]{:S(2)}, u32[]{:S(2)}) %collective-permute-start.22) | collective-permute-done | bytes 22560 | tf_op jit(solution)/shard_map/ppermute | solution.py:41
  182.3 4.4 %collective-permute-start.23 = (f32[176,32]{0,1:T(8,128)S(1)}, f32[176,32]{0,1:T(8,128)S(1)}, u32[]{:S(2)}, u32[]{:S(2)}) collective-permute-start(f32[176,32]{0,1:T(8,128)S(1)} %add.96), channel_id=1, source_target_pairs={{0,64},{1,65},{2,66},{3,67},{4,68},{5,69},{6,70},{7,71},{8,72},{9,... | collective-permute-start | bytes 67592 | tf_op jit(solution)/shard_map/ppermute | solution.py:41
  186.7 4.2 %collective-permute-done.23 = f32[176,32]{0,1:T(8,128)S(1)} collective-permute-done((f32[176,32]{0,1:T(8,128)S(1)}, f32[176,32]{0,1:T(8,128)S(1)}, u32[]{:S(2)}, u32[]{:S(2)}) %collective-permute-start.23) | collective-permute-done | bytes 22560 | tf_op jit(solution)/shard_map/ppermute | solution.py:41
  190.8 5.0 %collective-permute-start.24 = (f32[176,32]{0,1:T(8,128)S(1)}, f32[176,32]{0,1:T(8,128)S(1)}, u32[]{:S(2)}, u32[]{:S(2)}) collective-permute-start(f32[176,32]{0,1:T(8,128)S(1)} %add.97), channel_id=1, source_target_pairs={{0,512},{1,513},{2,514},{3,515},{4,516},{5,517},{6,518},{7,519},{8... | collective-permute-start | bytes 67592 | tf_op jit(solution)/shard_map/ppermute | solution.py:41
  195.8 3.6 %collective-permute-done.24 = f32[176,32]{0,1:T(8,128)S(1)} collective-permute-done((f32[176,32]{0,1:T(8,128)S(1)}, f32[176,32]{0,1:T(8,128)S(1)}, u32[]{:S(2)}, u32[]{:S(2)}) %collective-permute-start.24) | collective-permute-done | bytes 22560 | tf_op jit(solution)/shard_map/ppermute | solution.py:41
  201.3 2.7 %collective-permute-done.25 = f32[176,32]{0,1:T(8,128)S(1)} collective-permute-done((f32[176,32]{0,1:T(8,128)S(1)}, f32[176,32]{0,1:T(8,128)S(1)}, u32[]{:S(2)}, u32[]{:S(2)}) %collective-permute-start.25) | collective-permute-done | bytes 22560 | tf_op jit(solution)/shard_map/ppermute | solution.py:44
  204.1 2.1 collective-permute-start.26
  206.2 2.8 %collective-permute-done.26 = f32[352,32]{0,1:T(8,128)S(1)} collective-permute-done((f32[352,32]{0,1:T(8,128)S(1)}, f32[352,32]{0,1:T(8,128)S(1)}, u32[]{:S(2)}, u32[]{:S(2)}) %collective-permute-start.26) | collective-permute-done | bytes 45088 | tf_op jit(solution)/shard_map/ppermute | solution.py:44
  209.2 14.2 %collective-permute-start.27 = (f32[704,32]{0,1:T(8,128)S(1)}, f32[704,32]{0,1:T(8,128)S(1)}, u32[]{:S(2)}, u32[]{:S(2)}) collective-permute-start(f32[704,32]{0,1:T(8,128)S(1)} %maximum_select_fusion.7), channel_id=1, source_target_pairs={{0,1},{1,0},{2,3},{3,2},{4,5},{5,4},{6,7},{7,6},{8,9},{9,8},{10,11... | collective-permute-start | bytes 270344 | tf_op jit(solution)/shard_map/ppermute | solution.py:44
  224.4 2.3 %fusion.7 = f32[352,1408]{1,0:T(8,128)} fusion(f32[1408,32]{0,1:T(8,128)S(1)} %fusion.6, f32[5632,32]{0,1:T(8,128)S(1)} %fusion, s32[]{:T(128)S(6)} %select_n.172), kind=kOutput, calls=%fused_computation.27 | convolution fusion | flops 95158272 | bytes 2211844 | tf_op jit(solution)/shard_map/dot_general | solution.py:74
  (65 shorter events, 32.4 us)
Async XLA Ops:
  0.6 1.6 copy-start
  4.3 17.4 %collective-permute-start = (f32[2816,32]{0,1:T(8,128)S(1)}, f32[2816,32]{0,1:T(8,128)}, u32[]{:S(2)}, u32[]{:S(2)}) collective-permute-start(f32[2816,32]{0,1:T(8,128)S(1)} %slice_select_fusion), channel_id=1, source_target_pairs={{0,1},{1,0},{2,3},{3,2},{4,5},{5,4},{6,7},{7,6},{8,9},{9,8},{10,11... | collective-permute-start | bytes 1081352 | tf_op jit(solution)/shard_map/ppermute | solution.py:38
  22.8 7.6 %collective-permute-start.1 = (f32[1408,32]{0,1:T(8,128)S(1)}, f32[1408,32]{0,1:T(8,128)S(1)}, u32[]{:S(2)}, u32[]{:S(2)}) collective-permute-start(f32[1408,32]{0,1:T(8,128)S(1)} %slice_select_fusion.1), channel_id=1, source_target_pairs={{0,2},{1,3},{2,0},{3,1},{4,6},{5,7},{6,4},{7,5},{8,10},{9,11},{10,... | collective-permute-start | bytes 540680 | tf_op jit(solution)/shard_map/ppermute | solution.py:38
  30.6 5.4 %collective-permute-start.2 = (f32[704,32]{0,1:T(8,128)S(1)}, f32[704,32]{0,1:T(8,128)S(1)}, u32[]{:S(2)}, u32[]{:S(2)}) collective-permute-start(f32[704,32]{0,1:T(8,128)S(1)} %slice_select_fusion.3), channel_id=1, source_target_pairs={{0,16},{1,17},{2,18},{3,19},{4,20},{5,21},{6,22},{7,23},{8,24},{9,... | collective-permute-start | bytes 270344 | tf_op jit(solution)/shard_map/ppermute | solution.py:38
  36.1 4.8 %collective-permute-start.3 = (f32[352,32]{0,1:T(8,128)S(1)}, f32[352,32]{0,1:T(8,128)S(1)}, u32[]{:S(2)}, u32[]{:S(2)}) collective-permute-start(f32[352,32]{0,1:T(8,128)S(1)} %slice_select_fusion.5), channel_id=1, source_target_pairs={{0,128},{1,129},{2,130},{3,131},{4,132},{5,133},{6,134},{7,135},{8... | collective-permute-start | bytes 135176 | tf_op jit(solution)/shard_map/ppermute | solution.py:38
  41.1 5.9 %collective-permute-start.4 = (f32[176,32]{0,1:T(8,128)S(1)}, f32[176,32]{0,1:T(8,128)S(1)}, u32[]{:S(2)}, u32[]{:S(2)}) collective-permute-start(f32[176,32]{0,1:T(8,128)S(1)} %slice_select_fusion.7), channel_id=1, source_target_pairs={{0,4},{1,5},{2,6},{3,7},{4,0},{5,1},{6,2},{7,3},{8,12},{9,13},{10,... | collective-permute-start | bytes 67592 | tf_op jit(solution)/shard_map/ppermute | solution.py:38
  47.1 5.6 %collective-permute-start.5 = (f32[176,32]{0,1:T(8,128)S(1)}, f32[176,32]{0,1:T(8,128)S(1)}, u32[]{:S(2)}, u32[]{:S(2)}) collective-permute-start(f32[176,32]{0,1:T(8,128)S(1)} %select_add_fusion.7), channel_id=1, source_target_pairs={{0,32},{1,33},{2,34},{3,35},{4,36},{5,37},{6,38},{7,39},{8,40},{9,... | collective-permute-start | bytes 67592 | tf_op jit(solution)/shard_map/ppermute | solution.py:41
  52.7 5.6 %collective-permute-start.6 = (f32[176,32]{0,1:T(8,128)S(1)}, f32[176,32]{0,1:T(8,128)S(1)}, u32[]{:S(2)}, u32[]{:S(2)}) collective-permute-start(f32[176,32]{0,1:T(8,128)S(1)} %add.82), channel_id=1, source_target_pairs={{0,256},{1,257},{2,258},{3,259},{4,260},{5,261},{6,262},{7,263},{8... | collective-permute-start | bytes 67592 | tf_op jit(solution)/shard_map/ppermute | solution.py:41
  58.4 8.6 %collective-permute-start.7 = (f32[176,32]{0,1:T(8,128)S(1)}, f32[176,32]{0,1:T(8,128)S(1)}, u32[]{:S(2)}, u32[]{:S(2)}) collective-permute-start(f32[176,32]{0,1:T(8,128)S(1)} %add.83), channel_id=1, source_target_pairs={{0,8},{1,9},{2,10},{3,11},{4,12},{5,13},{6,14},{7,15},{8,0},{9,1},... | collective-permute-start | bytes 67592 | tf_op jit(solution)/shard_map/ppermute | solution.py:41
  66.9 8.6 %collective-permute-start.8 = (f32[176,32]{0,1:T(8,128)S(1)}, f32[176,32]{0,1:T(8,128)S(1)}, u32[]{:S(2)}, u32[]{:S(2)}) collective-permute-start(f32[176,32]{0,1:T(8,128)S(1)} %add.84), channel_id=1, source_target_pairs={{0,64},{1,65},{2,66},{3,67},{4,68},{5,69},{6,70},{7,71},{8,72},{9,... | collective-permute-start | bytes 67592 | tf_op jit(solution)/shard_map/ppermute | solution.py:41
  75.5 8.6 %collective-permute-start.9 = (f32[176,32]{0,1:T(8,128)S(1)}, f32[176,32]{0,1:T(8,128)S(1)}, u32[]{:S(2)}, u32[]{:S(2)}) collective-permute-start(f32[176,32]{0,1:T(8,128)S(1)} %add.85), channel_id=1, source_target_pairs={{0,512},{1,513},{2,514},{3,515},{4,516},{5,517},{6,518},{7,519},{8... | collective-permute-start | bytes 67592 | tf_op jit(solution)/shard_map/ppermute | solution.py:41
  84.0 5.8 %collective-permute-start.10 = (f32[176,32]{0,1:T(8,128)S(1)}, f32[176,32]{0,1:T(8,128)S(1)}, u32[]{:S(2)}, u32[]{:S(2)}) collective-permute-start(f32[176,32]{0,1:T(8,128)S(1)} %add.86), channel_id=1, source_target_pairs={{0,4},{1,5},{2,6},{3,7},{4,0},{5,1},{6,2},{7,3},{8,12},{9,13},{10,... | collective-permute-start | bytes 67592 | tf_op jit(solution)/shard_map/ppermute | solution.py:44
  89.9 4.8 %collective-permute-start.11 = (f32[352,32]{0,1:T(8,128)S(1)}, f32[352,32]{0,1:T(8,128)S(1)}, u32[]{:S(2)}, u32[]{:S(2)}) collective-permute-start(f32[352,32]{0,1:T(8,128)S(1)} %maximum_select_fusion.8), channel_id=1, source_target_pairs={{0,128},{1,129},{2,130},{3,131},{4,132},{5,133},{6,134},{7,135},{8... | collective-permute-start | bytes 135176 | tf_op jit(solution)/shard_map/ppermute | solution.py:44
  94.9 39.9 %copy-start.1 = (bf16[192,1408]{1,0:T(8,128)(2,1)S(1)}, bf16[192,1408]{1,0:T(8,128)(2,1)}, u32[]{:S(2)}) copy-start(bf16[192,1408]{1,0:T(8,128)(2,1)} %param.4) | copy-start | bytes 1622020
  94.9 5.8 %collective-permute-start.12 = (f32[704,32]{0,1:T(8,128)S(1)}, f32[704,32]{0,1:T(8,128)S(1)}, u32[]{:S(2)}, u32[]{:S(2)}) collective-permute-start(f32[704,32]{0,1:T(8,128)S(1)} %maximum_select_fusion.6), channel_id=1, source_target_pairs={{0,16},{1,17},{2,18},{3,19},{4,20},{5,21},{6,22},{7,23},{8,24},{9,... | collective-permute-start | bytes 270344 | tf_op jit(solution)/shard_map/ppermute | solution.py:44
  100.8 6.2 %collective-permute-start.13 = (f32[1408,32]{0,1:T(8,128)S(1)}, f32[1408,32]{0,1:T(8,128)S(1)}, u32[]{:S(2)}, u32[]{:S(2)}) collective-permute-start(f32[1408,32]{0,1:T(8,128)S(1)} %maximum_select_fusion.4), channel_id=1, source_target_pairs={{0,2},{1,3},{2,0},{3,1},{4,6},{5,7},{6,4},{7,5},{8,10},{9,11},{10,... | collective-permute-start | bytes 540680 | tf_op jit(solution)/shard_map/ppermute | solution.py:44
  107.1 17.6 %copy-start.2 = (f32[2816,32]{0,1:T(8,128)}, f32[2816,32]{0,1:T(8,128)S(1)}, u32[]{:S(2)}) copy-start(f32[2816,32]{0,1:T(8,128)S(1)} %maximum_select_fusion.3) | copy-start | bytes 1081348
  107.1 17.6 %collective-permute-start.14 = (f32[2816,32]{0,1:T(8,128)S(1)}, f32[2816,32]{0,1:T(8,128)S(1)}, u32[]{:S(2)}, u32[]{:S(2)}) collective-permute-start(f32[2816,32]{0,1:T(8,128)S(1)} %maximum_select_fusion.3), channel_id=1, source_target_pairs={{0,1},{1,0},{2,3},{3,2},{4,5},{5,4},{6,7},{7,6},{8,9},{9,8},{10,11... | collective-permute-start | bytes 1081352 | tf_op jit(solution)/shard_map/ppermute | solution.py:44
  124.7 0.7 copy-start.4
  137.7 3.2 %collective-permute-start.15 = (f32[704,32]{0,1:T(8,128)S(1)}, f32[704,32]{0,1:T(8,128)S(1)}, u32[]{:S(2)}, u32[]{:S(2)}) collective-permute-start(f32[704,32]{0,1:T(8,128)S(1)} %slice_select_fusion.2), channel_id=1, source_target_pairs={{0,1},{1,0},{2,3},{3,2},{4,5},{5,4},{6,7},{7,6},{8,9},{9,8},{10,11... | collective-permute-start | bytes 270344 | tf_op jit(solution)/shard_map/ppermute | solution.py:38
  142.0 4.8 %collective-permute-start.16 = (f32[352,32]{0,1:T(8,128)S(1)}, f32[352,32]{0,1:T(8,128)S(1)}, u32[]{:S(2)}, u32[]{:S(2)}) collective-permute-start(f32[352,32]{0,1:T(8,128)S(1)} %slice_select_fusion.4), channel_id=1, source_target_pairs={{0,2},{1,3},{2,0},{3,1},{4,6},{5,7},{6,4},{7,5},{8,10},{9,11},{10,... | collective-permute-start | bytes 135176 | tf_op jit(solution)/shard_map/ppermute | solution.py:38
  147.0 4.7 %collective-permute-start.17 = (f32[176,32]{0,1:T(8,128)S(1)}, f32[176,32]{0,1:T(8,128)S(1)}, u32[]{:S(2)}, u32[]{:S(2)}) collective-permute-start(f32[176,32]{0,1:T(8,128)S(1)} %slice_select_fusion.6), channel_id=1, source_target_pairs={{0,16},{1,17},{2,18},{3,19},{4,20},{5,21},{6,22},{7,23},{8,24},{9,... | collective-permute-start | bytes 67592 | tf_op jit(solution)/shard_map/ppermute | solution.py:38
  151.7 4.7 %collective-permute-start.18 = (f32[176,32]{0,1:T(8,128)S(1)}, f32[176,32]{0,1:T(8,128)S(1)}, u32[]{:S(2)}, u32[]{:S(2)}) collective-permute-start(f32[176,32]{0,1:T(8,128)S(1)} %select_add_fusion.6), channel_id=1, source_target_pairs={{0,128},{1,129},{2,130},{3,131},{4,132},{5,133},{6,134},{7,135},{8... | collective-permute-start | bytes 67592 | tf_op jit(solution)/shard_map/ppermute | solution.py:41
  156.4 5.6 %collective-permute-start.19 = (f32[176,32]{0,1:T(8,128)S(1)}, f32[176,32]{0,1:T(8,128)S(1)}, u32[]{:S(2)}, u32[]{:S(2)}) collective-permute-start(f32[176,32]{0,1:T(8,128)S(1)} %add.92), channel_id=1, source_target_pairs={{0,4},{1,5},{2,6},{3,7},{4,0},{5,1},{6,2},{7,3},{8,12},{9,13},{10,... | collective-permute-start | bytes 67592 | tf_op jit(solution)/shard_map/ppermute | solution.py:41
  162.0 5.6 %collective-permute-start.20 = (f32[176,32]{0,1:T(8,128)S(1)}, f32[176,32]{0,1:T(8,128)S(1)}, u32[]{:S(2)}, u32[]{:S(2)}) collective-permute-start(f32[176,32]{0,1:T(8,128)S(1)} %add.93), channel_id=1, source_target_pairs={{0,32},{1,33},{2,34},{3,35},{4,36},{5,37},{6,38},{7,39},{8,40},{9,... | collective-permute-start | bytes 67592 | tf_op jit(solution)/shard_map/ppermute | solution.py:41
  167.7 5.7 %collective-permute-start.21 = (f32[176,32]{0,1:T(8,128)S(1)}, f32[176,32]{0,1:T(8,128)S(1)}, u32[]{:S(2)}, u32[]{:S(2)}) collective-permute-start(f32[176,32]{0,1:T(8,128)S(1)} %add.94), channel_id=1, source_target_pairs={{0,256},{1,257},{2,258},{3,259},{4,260},{5,261},{6,262},{7,263},{8... | collective-permute-start | bytes 67592 | tf_op jit(solution)/shard_map/ppermute | solution.py:41
  173.4 8.9 %collective-permute-start.22 = (f32[176,32]{0,1:T(8,128)S(1)}, f32[176,32]{0,1:T(8,128)S(1)}, u32[]{:S(2)}, u32[]{:S(2)}) collective-permute-start(f32[176,32]{0,1:T(8,128)S(1)} %add.95), channel_id=1, source_target_pairs={{0,8},{1,9},{2,10},{3,11},{4,12},{5,13},{6,14},{7,15},{8,0},{9,1},... | collective-permute-start | bytes 67592 | tf_op jit(solution)/shard_map/ppermute | solution.py:41
  182.3 8.6 %collective-permute-start.23 = (f32[176,32]{0,1:T(8,128)S(1)}, f32[176,32]{0,1:T(8,128)S(1)}, u32[]{:S(2)}, u32[]{:S(2)}) collective-permute-start(f32[176,32]{0,1:T(8,128)S(1)} %add.96), channel_id=1, source_target_pairs={{0,64},{1,65},{2,66},{3,67},{4,68},{5,69},{6,70},{7,71},{8,72},{9,... | collective-permute-start | bytes 67592 | tf_op jit(solution)/shard_map/ppermute | solution.py:41
  190.8 8.6 %collective-permute-start.24 = (f32[176,32]{0,1:T(8,128)S(1)}, f32[176,32]{0,1:T(8,128)S(1)}, u32[]{:S(2)}, u32[]{:S(2)}) collective-permute-start(f32[176,32]{0,1:T(8,128)S(1)} %add.97), channel_id=1, source_target_pairs={{0,512},{1,513},{2,514},{3,515},{4,516},{5,517},{6,518},{7,519},{8... | collective-permute-start | bytes 67592 | tf_op jit(solution)/shard_map/ppermute | solution.py:41
  199.4 4.6 %collective-permute-start.25 = (f32[176,32]{0,1:T(8,128)S(1)}, f32[176,32]{0,1:T(8,128)S(1)}, u32[]{:S(2)}, u32[]{:S(2)}) collective-permute-start(f32[176,32]{0,1:T(8,128)S(1)} %add.98), channel_id=1, source_target_pairs={{0,16},{1,17},{2,18},{3,19},{4,20},{5,21},{6,22},{7,23},{8,24},{9,... | collective-permute-start | bytes 67592 | tf_op jit(solution)/shard_map/ppermute | solution.py:44
  204.1 4.9 %collective-permute-start.26 = (f32[352,32]{0,1:T(8,128)S(1)}, f32[352,32]{0,1:T(8,128)S(1)}, u32[]{:S(2)}, u32[]{:S(2)}) collective-permute-start(f32[352,32]{0,1:T(8,128)S(1)} %maximum_select_fusion.9), channel_id=1, source_target_pairs={{0,2},{1,3},{2,0},{3,1},{4,6},{5,7},{6,4},{7,5},{8,10},{9,11},{10,... | collective-permute-start | bytes 135176 | tf_op jit(solution)/shard_map/ppermute | solution.py:44
  209.2 15.1 %collective-permute-start.27 = (f32[704,32]{0,1:T(8,128)S(1)}, f32[704,32]{0,1:T(8,128)S(1)}, u32[]{:S(2)}, u32[]{:S(2)}) collective-permute-start(f32[704,32]{0,1:T(8,128)S(1)} %maximum_select_fusion.7), channel_id=1, source_target_pairs={{0,1},{1,0},{2,3},{3,2},{4,5},{5,4},{6,7},{7,6},{8,9},{9,8},{10,11... | collective-permute-start | bytes 270344 | tf_op jit(solution)/shard_map/ppermute | solution.py:44
  224.4 2.4 %copy-start.3 = (f32[1408,32]{0,1:T(8,128)}, f32[1408,32]{0,1:T(8,128)S(1)}, u32[]{:S(2)}) copy-start(f32[1408,32]{0,1:T(8,128)S(1)} %fusion.6) | copy-start | bytes 540676

commit v3 on v2

--- a/solution.py
+++ b/solution.py
@@ -24,12 +24,26 @@
     return [(i, i ^ (1 << bit)) for i in range(n)]
 
 
-def butterfly_sum(x, order, n, max_halvings):
+def group_pairs(n, bits, t):
+    mask = sum(1 << b for k, b in enumerate(bits) if (t >> k) & 1)
+    return [(i, i ^ mask) for i in range(n)]
+
+
+def butterfly_sum(x, order, n, max_halvings, first_group=2):
     idx = lax.axis_index(AXES)
+    group, rest = order[:first_group], order[first_group:]
+    parts = 1 << len(group)
+    c = sum(((idx >> b) & 1) << k for k, b in enumerate(group))
+    piece = x.shape[0] // parts
+    acc = lax.dynamic_slice_in_dim(x, c * piece, piece, 0)
+    for t in range(1, parts):
+        send = lax.dynamic_slice_in_dim(x, (c ^ t) * piece, piece, 0)
+        acc = acc + lax.ppermute(send, AXES, group_pairs(n, group, t))
+    x = acc
     halved = []
-    for bit in order:
+    for bit in rest:
         rows = x.shape[0]
-        if len(halved) < max_halvings and rows % 16 == 0:
+        if len(halved) + len(group) < max_halvings and rows % 16 == 0:
             half = rows // 2
             mine = (idx >> bit) & 1
             lo, hi = x[:half], x[half:]
@@ -43,7 +57,12 @@
         mine = (idx >> bit) & 1
         other = lax.ppermute(x, AXES, xor_pairs(n, bit))
         x = jnp.where(mine == 1, jnp.concatenate([other, x]), jnp.concatenate([x, other]))
-    return x
+    out = jnp.zeros((parts * x.shape[0],) + x.shape[1:], x.dtype)
+    out = lax.dynamic_update_slice_in_dim(out, x, c * x.shape[0], 0)
+    for t in range(1, parts):
+        got = lax.ppermute(x, AXES, group_pairs(n, group, t))
+        out = lax.dynamic_update_slice_in_dim(out, got, (c ^ t) * x.shape[0], 0)
+    return out
 
 
 def orthonormal(rows_part, gram):

time: 228 us -> 237 us (1.039)
  starting transfers between devices: 108 us -> 122 us
  waiting for transfers between devices: 95.4 us -> 87.5 us
  local copies, waits for them, and re-layouts: 2.42 us -> 5.36 us
    ppermute x0 -> x12, starting transfers between devices: none -> 68.7 us  [the longest x6 39.9 us: butterfly_sum(): got = lax.ppermute(x, AXES, group_pairs(n, group, t))]
    ppermute x8 -> x4, starting transfers between devices: 42.3 us -> 7.66 us  [butterfly_sum(): other = lax.ppermute(x, AXES, xor_pairs(n, bit))]
    ppermute x8 -> x4, starting transfers between devices: 29.8 us -> 7.67 us  [butterfly_sum(): x = keep + lax.ppermute(send, AXES, xor_pairs(n, bit))]
    ppermute x0 -> x12, waiting for transfers between devices: none -> 15.5 us  [the longest x6 7.96 us: butterfly_sum(): acc = acc + lax.ppermute(send, AXES, group_pairs(n, group, t))]
    ppermute x8 -> x4, waiting for transfers between devices: 24 us -> 13 us  [butterfly_sum(): x = keep + lax.ppermute(send, AXES, xor_pairs(n, bit))]
    ppermute x8 -> x4, waiting for transfers between devices: 22.6 us -> 13 us  [butterfly_sum(): other = lax.ppermute(x, AXES, xor_pairs(n, bit))]
    dynamic_update_slice x0 -> x7, local copies, waits for them, and re-layouts: none -> 3.47 us  [the longest x6 2.74 us: butterfly_sum(): out = lax.dynamic_update_slice_in_dim(out, got, (c ^ t) * x.shape[0], 0)]
    ppermute x12, waiting for transfers between devices: 48.9 us -> 46 us  [butterfly_sum(): x = x + lax.ppermute(x, AXES, xor_pairs(n, bit))]
  transfers between devices with their start and end apart: 28 -> 32, of which waited for: 28 -> 27; matrix products, arithmetic and copies ran while one was open for 0% -> 1% of each run, Pallas kernels for 0% -> 0%
where the time goes in v3:
time: 237 us; the launch traced here: 236 us
  starting transfers between devices  122 us (51%)
  waiting for transfers between devices  87.5 us (37%)
  other arithmetic  9.69 us (4%)
  matrix products  9.54 us (4%)
  local copies, waits for them, and re-layouts  5.36 us (2%)
    ppermute x12, waiting for transfers between devices, butterfly_sum(): x = x + lax.ppermute(x, AXES, xor_pairs(n, bit))  46 us
    ppermute x6, starting transfers between devices, butterfly_sum(): got = lax.ppermute(x, AXES, group_pairs(n, group, t))  39.9 us
    ppermute x12, starting transfers between devices, butterfly_sum(): x = x + lax.ppermute(x, AXES, xor_pairs(n, bit))  38.4 us
    ppermute x6, starting transfers between devices, butterfly_sum(): acc = acc + lax.ppermute(send, AXES, group_pairs(n, group, t))  28.8 us
    ppermute x4, waiting for transfers between devices, butterfly_sum(): x = keep + lax.ppermute(send, AXES, xor_pairs(n, bit))  13 us
    ppermute x4, waiting for transfers between devices, butterfly_sum(): other = lax.ppermute(x, AXES, xor_pairs(n, bit))  13 us
    ppermute x6, waiting for transfers between devices, butterfly_sum(): acc = acc + lax.ppermute(send, AXES, group_pairs(n, group, t))  7.96 us
    ppermute x4, starting transfers between devices, butterfly_sum(): x = keep + lax.ppermute(send, AXES, xor_pairs(n, bit))  7.67 us
  transfers between devices with their start and end apart: 32, of which 27 were waited for; matrix products, arithmetic and copies ran while one was open for 1% of the time, Pallas kernels for 0%

profile of v3, /device:TPU:1, one launch (start us, length us, event | category | flops | bytes accessed | tf_op | source)
XLA Modules:
  0.0 235.6 jit_solution(607274819547315396)
XLA Ops:
  2.2 2.0 fusion
  4.3 16.0 %collective-permute-start = (f32[1408,32]{0,1:T(8,128)S(1)}, f32[1408,32]{0,1:T(8,128)}, u32[]{:S(2)}, u32[]{:S(2)}) collective-permute-start(f32[1408,32]{0,1:T(8,128)S(1)} %get-tuple-element.4), channel_id=1, source_target_pairs={{0,1},{1,0},{2,3},{3,2},{4,5},{5,4},{6,7},{7,6},{8,9},{9,8},{10,11... | collective-permute-start | bytes 540680 | tf_op jit(solution)/shard_map/ppermute | solution.py:41
  20.4 1.9 collective-permute-start.2
  22.3 3.3 %collective-permute-start.1 = (f32[1408,32]{0,1:T(8,128)S(1)}, f32[1408,32]{0,1:T(8,128)}, u32[]{:S(2)}, u32[]{:S(2)}) collective-permute-start(f32[1408,32]{0,1:T(8,128)S(1)} %get-tuple-element.6), channel_id=1, source_target_pairs={{0,2},{1,3},{2,0},{3,1},{4,6},{5,7},{6,4},{7,5},{8,10},{9,11},{10,... | collective-permute-start | bytes 540680 | tf_op jit(solution)/shard_map/ppermute | solution.py:41
  25.6 3.6 %collective-permute-done.2 = f32[1408,32]{0,1:T(8,128)} collective-permute-done((f32[1408,32]{0,1:T(8,128)S(1)}, f32[1408,32]{0,1:T(8,128)}, u32[]{:S(2)}, u32[]{:S(2)}) %collective-permute-start.2) | collective-permute-done | bytes 180256 | tf_op jit(solution)/shard_map/ppermute | solution.py:41
  29.2 2.8 %collective-permute-done.1 = f32[1408,32]{0,1:T(8,128)} collective-permute-done((f32[1408,32]{0,1:T(8,128)S(1)}, f32[1408,32]{0,1:T(8,128)}, u32[]{:S(2)}, u32[]{:S(2)}) %collective-permute-start.1) | collective-permute-done | bytes 180256 | tf_op jit(solution)/shard_map/ppermute | solution.py:41
  33.2 1.9 collective-permute-start.3
  35.2 3.4 %collective-permute-done.3 = f32[704,32]{0,1:T(8,128)S(1)} collective-permute-done((f32[704,32]{0,1:T(8,128)S(1)}, f32[704,32]{0,1:T(8,128)S(1)}, u32[]{:S(2)}, u32[]{:S(2)}) %collective-permute-start.3) | collective-permute-done | bytes 90144 | tf_op jit(solution)/shard_map/ppermute | solution.py:52
  40.7 2.9 %collective-permute-done.4 = f32[352,32]{0,1:T(8,128)S(1)} collective-permute-done((f32[352,32]{0,1:T(8,128)S(1)}, f32[352,32]{0,1:T(8,128)S(1)}, u32[]{:S(2)}, u32[]{:S(2)}) %collective-permute-start.4) | collective-permute-done | bytes 45088 | tf_op jit(solution)/shard_map/ppermute | solution.py:52
  45.7 4.0 %collective-permute-done.5 = f32[176,32]{0,1:T(8,128)S(1)} collective-permute-done((f32[176,32]{0,1:T(8,128)S(1)}, f32[176,32]{0,1:T(8,128)S(1)}, u32[]{:S(2)}, u32[]{:S(2)}) %collective-permute-start.5) | collective-permute-done | bytes 22560 | tf_op jit(solution)/shard_map/ppermute | solution.py:52
  51.7 3.6 %collective-permute-done.6 = f32[176,32]{0,1:T(8,128)S(1)} collective-permute-done((f32[176,32]{0,1:T(8,128)S(1)}, f32[176,32]{0,1:T(8,128)S(1)}, u32[]{:S(2)}, u32[]{:S(2)}) %collective-permute-start.6) | collective-permute-done | bytes 22560 | tf_op jit(solution)/shard_map/ppermute | solution.py:55
  57.2 3.7 %collective-permute-done.7 = f32[176,32]{0,1:T(8,128)S(1)} collective-permute-done((f32[176,32]{0,1:T(8,128)S(1)}, f32[176,32]{0,1:T(8,128)S(1)}, u32[]{:S(2)}, u32[]{:S(2)}) %collective-permute-start.7) | collective-permute-done | bytes 22560 | tf_op jit(solution)/shard_map/ppermute | solution.py:55
  62.9 6.6 %collective-permute-done.8 = f32[176,32]{0,1:T(8,128)S(1)} collective-permute-done((f32[176,32]{0,1:T(8,128)S(1)}, f32[176,32]{0,1:T(8,128)S(1)}, u32[]{:S(2)}, u32[]{:S(2)}) %collective-permute-start.8) | collective-permute-done | bytes 22560 | tf_op jit(solution)/shard_map/ppermute | solution.py:55
  69.5 3.9 %collective-permute-start.9 = (f32[176,32]{0,1:T(8,128)S(1)}, f32[176,32]{0,1:T(8,128)S(1)}, u32[]{:S(2)}, u32[]{:S(2)}) collective-permute-start(f32[176,32]{0,1:T(8,128)S(1)} %add.132), channel_id=1, source_target_pairs={{0,64},{1,65},{2,66},{3,67},{4,68},{5,69},{6,70},{7,71},{8,72},{9,... | collective-permute-start | bytes 67592 | tf_op jit(solution)/shard_map/ppermute | solution.py:55
  73.4 4.6 %collective-permute-done.9 = f32[176,32]{0,1:T(8,128)S(1)} collective-permute-done((f32[176,32]{0,1:T(8,128)S(1)}, f32[176,32]{0,1:T(8,128)S(1)}, u32[]{:S(2)}, u32[]{:S(2)}) %collective-permute-start.9) | collective-permute-done | bytes 22560 | tf_op jit(solution)/shard_map/ppermute | solution.py:55
  78.1 4.7 %collective-permute-start.10 = (f32[176,32]{0,1:T(8,128)S(1)}, f32[176,32]{0,1:T(8,128)S(1)}, u32[]{:S(2)}, u32[]{:S(2)}) collective-permute-start(f32[176,32]{0,1:T(8,128)S(1)} %add.133), channel_id=1, source_target_pairs={{0,512},{1,513},{2,514},{3,515},{4,516},{5,517},{6,518},{7,519},{8... | collective-permute-start | bytes 67592 | tf_op jit(solution)/shard_map/ppermute | solution.py:55
  82.8 3.8 %collective-permute-done.10 = f32[176,32]{0,1:T(8,128)S(1)} collective-permute-done((f32[176,32]{0,1:T(8,128)S(1)}, f32[176,32]{0,1:T(8,128)S(1)}, u32[]{:S(2)}, u32[]{:S(2)}) %collective-permute-start.10) | collective-permute-done | bytes 22560 | tf_op jit(solution)/shard_map/ppermute | solution.py:55
  88.5 3.6 %collective-permute-done.11 = f32[176,32]{0,1:T(8,128)S(1)} collective-permute-done((f32[176,32]{0,1:T(8,128)S(1)}, f32[176,32]{0,1:T(8,128)S(1)}, u32[]{:S(2)}, u32[]{:S(2)}) %collective-permute-start.11) | collective-permute-done | bytes 22560 | tf_op jit(solution)/shard_map/ppermute | solution.py:58
  92.3 1.9 collective-permute-start.12
  94.2 2.9 %collective-permute-done.12 = f32[352,32]{0,1:T(8,128)S(1)} collective-permute-done((f32[352,32]{0,1:T(8,128)S(1)}, f32[352,32]{0,1:T(8,128)S(1)}, u32[]{:S(2)}, u32[]{:S(2)}) %collective-permute-start.12) | collective-permute-done | bytes 45088 | tf_op jit(solution)/shard_map/ppermute | solution.py:58
  99.1 3.7 %collective-permute-done.13 = f32[704,32]{0,1:T(8,128)S(1)} collective-permute-done((f32[704,32]{0,1:T(8,128)S(1)}, f32[704,32]{0,1:T(8,128)S(1)}, u32[]{:S(2)}, u32[]{:S(2)}) %collective-permute-start.13) | collective-permute-done | bytes 90144 | tf_op jit(solution)/shard_map/ppermute | solution.py:58
  103.7 15.5 %collective-permute-start.14 = (f32[1408,32]{0,1:T(8,128)}, f32[1408,32]{0,1:T(8,128)}, u32[]{:S(2)}, u32[]{:S(2)}) collective-permute-start(f32[1408,32]{0,1:T(8,128)} %get-tuple-element.3), channel_id=1, source_target_pairs={{0,1},{1,0},{2,3},{3,2},{4,5},{5,4},{6,7},{7,6},{8,9},{9,8},{10,11... | collective-permute-start | bytes 540680 | tf_op jit(solution)/shard_map/ppermute | solution.py:63
  121.2 3.5 %collective-permute-start.16 = (f32[1408,32]{0,1:T(8,128)}, f32[1408,32]{0,1:T(8,128)S(1)}, u32[]{:S(2)}, u32[]{:S(2)}) collective-permute-start(f32[1408,32]{0,1:T(8,128)} %get-tuple-element.3), channel_id=1, source_target_pairs={{0,3},{1,2},{2,1},{3,0},{4,7},{5,6},{6,5},{7,4},{8,11},{9,10},{10,... | collective-permute-start | bytes 540680 | tf_op jit(solution)/shard_map/ppermute | solution.py:63
  127.5 4.0 %collective-permute-done.16 = f32[1408,32]{0,1:T(8,128)S(1)} collective-permute-done((f32[1408,32]{0,1:T(8,128)}, f32[1408,32]{0,1:T(8,128)S(1)}, u32[]{:S(2)}, u32[]{:S(2)}) %collective-permute-start.16) | collective-permute-done | bytes 180256 | tf_op jit(solution)/shard_map/ppermute | solution.py:63
  132.0 2.9 %cholesky.16 = f32[32,32]{1,0:T(8,128)S(1)} custom-call(f32[32,32]{1,0:T(8,128)S(1)} %fusion.13), custom_call_target="Cholesky" | custom-call | tf_op jit(solution)/shard_map/cholesky | solution.py:69
  136.3 2.4 %custom-call.5 = f32[1,32,32]{1,2,0:T(8,128)S(1)} custom-call(f32[1,32,32]{2,1,0:T(8,128)S(1)} %fusion.10), custom_call_target="InvertDiagBlocksLowerTriangular" | custom-call | tf_op jit(solution)/shard_map/triangular_solve | solution.py:70
  140.4 2.2 fusion.1
  142.7 2.1 collective-permute-start.17
  144.8 2.2 collective-permute-start.19
  147.0 3.3 %collective-permute-start.18 = (f32[352,32]{0,1:T(8,128)S(1)}, f32[352,32]{0,1:T(8,128)S(1)}, u32[]{:S(2)}, u32[]{:S(2)}) collective-permute-start(f32[352,32]{0,1:T(8,128)S(1)} %get-tuple-element.9), channel_id=1, source_target_pairs={{0,2},{1,3},{2,0},{3,1},{4,6},{5,7},{6,4},{7,5},{8,10},{9,11},{10,... | collective-permute-start | bytes 135176 | tf_op jit(solution)/shard_map/ppermute | solution.py:41
  154.0 2.7 %collective-permute-done.20 = f32[176,32]{0,1:T(8,128)S(1)} collective-permute-done((f32[176,32]{0,1:T(8,128)S(1)}, f32[176,32]{0,1:T(8,128)S(1)}, u32[]{:S(2)}, u32[]{:S(2)}) %collective-permute-start.20) | collective-permute-done | bytes 22560 | tf_op jit(solution)/shard_map/ppermute | solution.py:52
  158.7 2.7 %collective-permute-done.21 = f32[176,32]{0,1:T(8,128)S(1)} collective-permute-done((f32[176,32]{0,1:T(8,128)S(1)}, f32[176,32]{0,1:T(8,128)S(1)}, u32[]{:S(2)}, u32[]{:S(2)}) %collective-permute-start.21) | collective-permute-done | bytes 22560 | tf_op jit(solution)/shard_map/ppermute | solution.py:55
  161.4 2.1 collective-permute-start.22
  163.6 3.4 %collective-permute-done.22 = f32[176,32]{0,1:T(8,128)S(1)} collective-permute-done((f32[176,32]{0,1:T(8,128)S(1)}, f32[176,32]{0,1:T(8,128)S(1)}, u32[]{:S(2)}, u32[]{:S(2)}) %collective-permute-start.22) | collective-permute-done | bytes 22560 | tf_op jit(solution)/shard_map/ppermute | solution.py:55
  167.0 2.8 %collective-permute-start.23 = (f32[176,32]{0,1:T(8,128)S(1)}, f32[176,32]{0,1:T(8,128)S(1)}, u32[]{:S(2)}, u32[]{:S(2)}) collective-permute-start(f32[176,32]{0,1:T(8,128)S(1)} %add.146), channel_id=1, source_target_pairs={{0,32},{1,33},{2,34},{3,35},{4,36},{5,37},{6,38},{7,39},{8,40},{9,... | collective-permute-start | bytes 67592 | tf_op jit(solution)/shard_map/ppermute | solution.py:55
  169.7 2.9 %collective-permute-done.23 = f32[176,32]{0,1:T(8,128)S(1)} collective-permute-done((f32[176,32]{0,1:T(8,128)S(1)}, f32[176,32]{0,1:T(8,128)S(1)}, u32[]{:S(2)}, u32[]{:S(2)}) %collective-permute-start.23) | collective-permute-done | bytes 22560 | tf_op jit(solution)/shard_map/ppermute | solution.py:55
  172.6 2.2 collective-permute-start.24
  174.8 3.7 %collective-permute-done.24 = f32[176,32]{0,1:T(8,128)S(1)} collective-permute-done((f32[176,32]{0,1:T(8,128)S(1)}, f32[176,32]{0,1:T(8,128)S(1)}, u32[]{:S(2)}, u32[]{:S(2)}) %collective-permute-start.24) | collective-permute-done | bytes 22560 | tf_op jit(solution)/shard_map/ppermute | solution.py:55
  178.5 4.0 %collective-permute-start.25 = (f32[176,32]{0,1:T(8,128)S(1)}, f32[176,32]{0,1:T(8,128)S(1)}, u32[]{:S(2)}, u32[]{:S(2)}) collective-permute-start(f32[176,32]{0,1:T(8,128)S(1)} %add.148), channel_id=1, source_target_pairs={{0,8},{1,9},{2,10},{3,11},{4,12},{5,13},{6,14},{7,15},{8,0},{9,1},... | collective-permute-start | bytes 67592 | tf_op jit(solution)/shard_map/ppermute | solution.py:55
  182.5 4.7 %collective-permute-done.25 = f32[176,32]{0,1:T(8,128)S(1)} collective-permute-done((f32[176,32]{0,1:T(8,128)S(1)}, f32[176,32]{0,1:T(8,128)S(1)}, u32[]{:S(2)}, u32[]{:S(2)}) %collective-permute-start.25) | collective-permute-done | bytes 22560 | tf_op jit(solution)/shard_map/ppermute | solution.py:55
  187.2 5.3 %collective-permute-start.26 = (f32[176,32]{0,1:T(8,128)S(1)}, f32[176,32]{0,1:T(8,128)S(1)}, u32[]{:S(2)}, u32[]{:S(2)}) collective-permute-start(f32[176,32]{0,1:T(8,128)S(1)} %add.149), channel_id=1, source_target_pairs={{0,64},{1,65},{2,66},{3,67},{4,68},{5,69},{6,70},{7,71},{8,72},{9,... | collective-permute-start | bytes 67592 | tf_op jit(solution)/shard_map/ppermute | solution.py:55
  192.5 3.3 %collective-permute-done.26 = f32[176,32]{0,1:T(8,128)S(1)} collective-permute-done((f32[176,32]{0,1:T(8,128)S(1)}, f32[176,32]{0,1:T(8,128)S(1)}, u32[]{:S(2)}, u32[]{:S(2)}) %collective-permute-start.26) | collective-permute-done | bytes 22560 | tf_op jit(solution)/shard_map/ppermute | solution.py:55
  195.8 5.8 %collective-permute-start.27 = (f32[176,32]{0,1:T(8,128)S(1)}, f32[176,32]{0,1:T(8,128)S(1)}, u32[]{:S(2)}, u32[]{:S(2)}) collective-permute-start(f32[176,32]{0,1:T(8,128)S(1)} %add.150), channel_id=1, source_target_pairs={{0,512},{1,513},{2,514},{3,515},{4,516},{5,517},{6,518},{7,519},{8... | collective-permute-start | bytes 67592 | tf_op jit(solution)/shard_map/ppermute | solution.py:55
  201.5 2.9 %collective-permute-done.27 = f32[176,32]{0,1:T(8,128)S(1)} collective-permute-done((f32[176,32]{0,1:T(8,128)S(1)}, f32[176,32]{0,1:T(8,128)S(1)}, u32[]{:S(2)}, u32[]{:S(2)}) %collective-permute-start.27) | collective-permute-done | bytes 22560 | tf_op jit(solution)/shard_map/ppermute | solution.py:55
  206.3 2.7 %collective-permute-done.28 = f32[176,32]{0,1:T(8,128)S(1)} collective-permute-done((f32[176,32]{0,1:T(8,128)S(1)}, f32[176,32]{0,1:T(8,128)S(1)}, u32[]{:S(2)}, u32[]{:S(2)}) %collective-permute-start.28) | collective-permute-done | bytes 22560 | tf_op jit(solution)/shard_map/ppermute | solution.py:58
  209.1 13.2 %collective-permute-start.29 = (f32[352,32]{0,1:T(8,128)S(1)}, f32[352,32]{0,1:T(8,128)S(1)}, u32[]{:S(2)}, u32[]{:S(2)}) collective-permute-start(f32[352,32]{0,1:T(8,128)S(1)} %maximum_select_fusion.3), channel_id=1, source_target_pairs={{0,1},{1,0},{2,3},{3,2},{4,5},{5,4},{6,7},{7,6},{8,9},{9,8},{10,11... | collective-permute-start | bytes 135176 | tf_op jit(solution)/shard_map/ppermute | solution.py:63
  222.3 3.8 %collective-permute-start.30 = (f32[352,32]{0,1:T(8,128)S(1)}, f32[352,32]{0,1:T(8,128)S(1)}, u32[]{:S(2)}, u32[]{:S(2)}) collective-permute-start(f32[352,32]{0,1:T(8,128)S(1)} %maximum_select_fusion.3), channel_id=1, source_target_pairs={{0,2},{1,3},{2,0},{3,1},{4,6},{5,7},{6,4},{7,5},{8,10},{9,11},{10,... | collective-permute-start | bytes 135176 | tf_op jit(solution)/shard_map/ppermute | solution.py:63
  232.4 3.2 %fusion.8 = f32[352,1408]{1,0:T(8,128)} fusion(f32[1408,32]{0,1:T(8,128)S(1)} %broadcast_multiply_fusion, f32[5632,32]{0,1:T(8,128)} %fusion.11, s32[]{:T(128)S(6)} %select_n.130), kind=kOutput, calls=%fused_computation.24 | convolution fusion | flops 95158272 | bytes 2211844 | tf_op jit(solution)/shard_map/dot_general | solution.py:93
  (72 shorter events, 39.8 us)
Async XLA Ops:
  0.6 1.6 copy-start
  4.3 21.2 %collective-permute-start = (f32[1408,32]{0,1:T(8,128)S(1)}, f32[1408,32]{0,1:T(8,128)}, u32[]{:S(2)}, u32[]{:S(2)}) collective-permute-start(f32[1408,32]{0,1:T(8,128)S(1)} %get-tuple-element.4), channel_id=1, source_target_pairs={{0,1},{1,0},{2,3},{3,2},{4,5},{5,4},{6,7},{7,6},{8,9},{9,8},{10,11... | collective-permute-start | bytes 540680 | tf_op jit(solution)/shard_map/ppermute | solution.py:41
  20.4 8.8 %collective-permute-start.2 = (f32[1408,32]{0,1:T(8,128)S(1)}, f32[1408,32]{0,1:T(8,128)}, u32[]{:S(2)}, u32[]{:S(2)}) collective-permute-start(f32[1408,32]{0,1:T(8,128)S(1)} %get-tuple-element.5), channel_id=1, source_target_pairs={{0,3},{1,2},{2,1},{3,0},{4,7},{5,6},{6,5},{7,4},{8,11},{9,10},{10,... | collective-permute-start | bytes 540680 | tf_op jit(solution)/shard_map/ppermute | solution.py:41
  22.3 9.7 %collective-permute-start.1 = (f32[1408,32]{0,1:T(8,128)S(1)}, f32[1408,32]{0,1:T(8,128)}, u32[]{:S(2)}, u32[]{:S(2)}) collective-permute-start(f32[1408,32]{0,1:T(8,128)S(1)} %get-tuple-element.6), channel_id=1, source_target_pairs={{0,2},{1,3},{2,0},{3,1},{4,6},{5,7},{6,4},{7,5},{8,10},{9,11},{10,... | collective-permute-start | bytes 540680 | tf_op jit(solution)/shard_map/ppermute | solution.py:41
  33.2 5.4 %collective-permute-start.3 = (f32[704,32]{0,1:T(8,128)S(1)}, f32[704,32]{0,1:T(8,128)S(1)}, u32[]{:S(2)}, u32[]{:S(2)}) collective-permute-start(f32[704,32]{0,1:T(8,128)S(1)} %slice_select_fusion), channel_id=1, source_target_pairs={{0,16},{1,17},{2,18},{3,19},{4,20},{5,21},{6,22},{7,23},{8,24},{9,... | collective-permute-start | bytes 270344 | tf_op jit(solution)/shard_map/ppermute | solution.py:52
  38.8 4.8 %collective-permute-start.4 = (f32[352,32]{0,1:T(8,128)S(1)}, f32[352,32]{0,1:T(8,128)S(1)}, u32[]{:S(2)}, u32[]{:S(2)}) collective-permute-start(f32[352,32]{0,1:T(8,128)S(1)} %slice_select_fusion.1), channel_id=1, source_target_pairs={{0,128},{1,129},{2,130},{3,131},{4,132},{5,133},{6,134},{7,135},{8... | collective-permute-start | bytes 135176 | tf_op jit(solution)/shard_map/ppermute | solution.py:52
  43.8 5.9 %collective-permute-start.5 = (f32[176,32]{0,1:T(8,128)S(1)}, f32[176,32]{0,1:T(8,128)S(1)}, u32[]{:S(2)}, u32[]{:S(2)}) collective-permute-start(f32[176,32]{0,1:T(8,128)S(1)} %slice_select_fusion.3), channel_id=1, source_target_pairs={{0,4},{1,5},{2,6},{3,7},{4,0},{5,1},{6,2},{7,3},{8,12},{9,13},{10,... | collective-permute-start | bytes 67592 | tf_op jit(solution)/shard_map/ppermute | solution.py:52
  49.8 5.5 %collective-permute-start.6 = (f32[176,32]{0,1:T(8,128)S(1)}, f32[176,32]{0,1:T(8,128)S(1)}, u32[]{:S(2)}, u32[]{:S(2)}) collective-permute-start(f32[176,32]{0,1:T(8,128)S(1)} %select_add_fusion.3), channel_id=1, source_target_pairs={{0,32},{1,33},{2,34},{3,35},{4,36},{5,37},{6,38},{7,39},{8,40},{9,... | collective-permute-start | bytes 67592 | tf_op jit(solution)/shard_map/ppermute | solution.py:55
  55.3 5.6 %collective-permute-start.7 = (f32[176,32]{0,1:T(8,128)S(1)}, f32[176,32]{0,1:T(8,128)S(1)}, u32[]{:S(2)}, u32[]{:S(2)}) collective-permute-start(f32[176,32]{0,1:T(8,128)S(1)} %add.130), channel_id=1, source_target_pairs={{0,256},{1,257},{2,258},{3,259},{4,260},{5,261},{6,262},{7,263},{8... | collective-permute-start | bytes 67592 | tf_op jit(solution)/shard_map/ppermute | solution.py:55
  60.9 8.6 %collective-permute-start.8 = (f32[176,32]{0,1:T(8,128)S(1)}, f32[176,32]{0,1:T(8,128)S(1)}, u32[]{:S(2)}, u32[]{:S(2)}) collective-permute-start(f32[176,32]{0,1:T(8,128)S(1)} %add.131), channel_id=1, source_target_pairs={{0,8},{1,9},{2,10},{3,11},{4,12},{5,13},{6,14},{7,15},{8,0},{9,1},... | collective-permute-start | bytes 67592 | tf_op jit(solution)/shard_map/ppermute | solution.py:55
  69.5 8.6 %collective-permute-start.9 = (f32[176,32]{0,1:T(8,128)S(1)}, f32[176,32]{0,1:T(8,128)S(1)}, u32[]{:S(2)}, u32[]{:S(2)}) collective-permute-start(f32[176,32]{0,1:T(8,128)S(1)} %add.132), channel_id=1, source_target_pairs={{0,64},{1,65},{2,66},{3,67},{4,68},{5,69},{6,70},{7,71},{8,72},{9,... | collective-permute-start | bytes 67592 | tf_op jit(solution)/shard_map/ppermute | solution.py:55
  78.1 8.6 %collective-permute-start.10 = (f32[176,32]{0,1:T(8,128)S(1)}, f32[176,32]{0,1:T(8,128)S(1)}, u32[]{:S(2)}, u32[]{:S(2)}) collective-permute-start(f32[176,32]{0,1:T(8,128)S(1)} %add.133), channel_id=1, source_target_pairs={{0,512},{1,513},{2,514},{3,515},{4,516},{5,517},{6,518},{7,519},{8... | collective-permute-start | bytes 67592 | tf_op jit(solution)/shard_map/ppermute | solution.py:55
  86.6 5.5 %collective-permute-start.11 = (f32[176,32]{0,1:T(8,128)S(1)}, f32[176,32]{0,1:T(8,128)S(1)}, u32[]{:S(2)}, u32[]{:S(2)}) collective-permute-start(f32[176,32]{0,1:T(8,128)S(1)} %add.134), channel_id=1, source_target_pairs={{0,4},{1,5},{2,6},{3,7},{4,0},{5,1},{6,2},{7,3},{8,12},{9,13},{10,... | collective-permute-start | bytes 67592 | tf_op jit(solution)/shard_map/ppermute | solution.py:58
  92.3 4.8 %collective-permute-start.12 = (f32[352,32]{0,1:T(8,128)S(1)}, f32[352,32]{0,1:T(8,128)S(1)}, u32[]{:S(2)}, u32[]{:S(2)}) collective-permute-start(f32[352,32]{0,1:T(8,128)S(1)} %maximum_select_fusion.2), channel_id=1, source_target_pairs={{0,128},{1,129},{2,130},{3,131},{4,132},{5,133},{6,134},{7,135},{8... | collective-permute-start | bytes 135176 | tf_op jit(solution)/shard_map/ppermute | solution.py:58
  97.2 5.7 %collective-permute-start.13 = (f32[704,32]{0,1:T(8,128)S(1)}, f32[704,32]{0,1:T(8,128)S(1)}, u32[]{:S(2)}, u32[]{:S(2)}) collective-permute-start(f32[704,32]{0,1:T(8,128)S(1)} %maximum_select_fusion.1), channel_id=1, source_target_pairs={{0,16},{1,17},{2,18},{3,19},{4,20},{5,21},{6,22},{7,23},{8,24},{9,... | collective-permute-start | bytes 270344 | tf_op jit(solution)/shard_map/ppermute | solution.py:58
  103.7 36.7 %copy-start.1 = (bf16[192,1408]{1,0:T(8,128)(2,1)S(1)}, bf16[192,1408]{1,0:T(8,128)(2,1)}, u32[]{:S(2)}) copy-start(bf16[192,1408]{1,0:T(8,128)(2,1)} %param.4) | copy-start | bytes 1622020
  103.7 21.0 %collective-permute-start.14 = (f32[1408,32]{0,1:T(8,128)}, f32[1408,32]{0,1:T(8,128)}, u32[]{:S(2)}, u32[]{:S(2)}) collective-permute-start(f32[1408,32]{0,1:T(8,128)} %get-tuple-element.3), channel_id=1, source_target_pairs={{0,1},{1,0},{2,3},{3,2},{4,5},{5,4},{6,7},{7,6},{8,9},{9,8},{10,11... | collective-permute-start | bytes 540680 | tf_op jit(solution)/shard_map/ppermute | solution.py:63
  119.3 8.2 %collective-permute-start.15 = (f32[1408,32]{0,1:T(8,128)}, f32[1408,32]{0,1:T(8,128)S(1)}, u32[]{:S(2)}, u32[]{:S(2)}) collective-permute-start(f32[1408,32]{0,1:T(8,128)} %get-tuple-element.3), channel_id=1, source_target_pairs={{0,2},{1,3},{2,0},{3,1},{4,6},{5,7},{6,4},{7,5},{8,10},{9,11},{10,... | collective-permute-start | bytes 540680 | tf_op jit(solution)/shard_map/ppermute | solution.py:63
  121.2 10.3 %collective-permute-start.16 = (f32[1408,32]{0,1:T(8,128)}, f32[1408,32]{0,1:T(8,128)S(1)}, u32[]{:S(2)}, u32[]{:S(2)}) collective-permute-start(f32[1408,32]{0,1:T(8,128)} %get-tuple-element.3), channel_id=1, source_target_pairs={{0,3},{1,2},{2,1},{3,0},{4,7},{5,6},{6,5},{7,4},{8,11},{9,10},{10,... | collective-permute-start | bytes 540680 | tf_op jit(solution)/shard_map/ppermute | solution.py:63
  142.7 7.6 %collective-permute-start.17 = (f32[352,32]{0,1:T(8,128)S(1)}, f32[352,32]{0,1:T(8,128)S(1)}, u32[]{:S(2)}, u32[]{:S(2)}) collective-permute-start(f32[352,32]{0,1:T(8,128)S(1)} %get-tuple-element.7), channel_id=1, source_target_pairs={{0,1},{1,0},{2,3},{3,2},{4,5},{5,4},{6,7},{7,6},{8,9},{9,8},{10,11... | collective-permute-start | bytes 135176 | tf_op jit(solution)/shard_map/ppermute | solution.py:41
  144.8 5.5 %collective-permute-start.19 = (f32[352,32]{0,1:T(8,128)S(1)}, f32[352,32]{0,1:T(8,128)S(1)}, u32[]{:S(2)}, u32[]{:S(2)}) collective-permute-start(f32[352,32]{0,1:T(8,128)S(1)} %get-tuple-element.8), channel_id=1, source_target_pairs={{0,3},{1,2},{2,1},{3,0},{4,7},{5,6},{6,5},{7,4},{8,11},{9,10},{10,... | collective-permute-start | bytes 135176 | tf_op jit(solution)/shard_map/ppermute | solution.py:41
  147.0 4.8 %collective-permute-start.18 = (f32[352,32]{0,1:T(8,128)S(1)}, f32[352,32]{0,1:T(8,128)S(1)}, u32[]{:S(2)}, u32[]{:S(2)}) collective-permute-start(f32[352,32]{0,1:T(8,128)S(1)} %get-tuple-element.9), channel_id=1, source_target_pairs={{0,2},{1,3},{2,0},{3,1},{4,6},{5,7},{6,4},{7,5},{8,10},{9,11},{10,... | collective-permute-start | bytes 135176 | tf_op jit(solution)/shard_map/ppermute | solution.py:41
  152.0 4.7 %collective-permute-start.20 = (f32[176,32]{0,1:T(8,128)S(1)}, f32[176,32]{0,1:T(8,128)S(1)}, u32[]{:S(2)}, u32[]{:S(2)}) collective-permute-start(f32[176,32]{0,1:T(8,128)S(1)} %slice_select_fusion.2), channel_id=1, source_target_pairs={{0,16},{1,17},{2,18},{3,19},{4,20},{5,21},{6,22},{7,23},{8,24},{9,... | collective-permute-start | bytes 67592 | tf_op jit(solution)/shard_map/ppermute | solution.py:52
  156.8 4.7 %collective-permute-start.21 = (f32[176,32]{0,1:T(8,128)S(1)}, f32[176,32]{0,1:T(8,128)S(1)}, u32[]{:S(2)}, u32[]{:S(2)}) collective-permute-start(f32[176,32]{0,1:T(8,128)S(1)} %select_add_fusion.2), channel_id=1, source_target_pairs={{0,128},{1,129},{2,130},{3,131},{4,132},{5,133},{6,134},{7,135},{8... | collective-permute-start | bytes 67592 | tf_op jit(solution)/shard_map/ppermute | solution.py:55
  161.4 5.5 %collective-permute-start.22 = (f32[176,32]{0,1:T(8,128)S(1)}, f32[176,32]{0,1:T(8,128)S(1)}, u32[]{:S(2)}, u32[]{:S(2)}) collective-permute-start(f32[176,32]{0,1:T(8,128)S(1)} %add.145), channel_id=1, source_target_pairs={{0,4},{1,5},{2,6},{3,7},{4,0},{5,1},{6,2},{7,3},{8,12},{9,13},{10,... | collective-permute-start | bytes 67592 | tf_op jit(solution)/shard_map/ppermute | solution.py:55
  167.0 5.6 %collective-permute-start.23 = (f32[176,32]{0,1:T(8,128)S(1)}, f32[176,32]{0,1:T(8,128)S(1)}, u32[]{:S(2)}, u32[]{:S(2)}) collective-permute-start(f32[176,32]{0,1:T(8,128)S(1)} %add.146), channel_id=1, source_target_pairs={{0,32},{1,33},{2,34},{3,35},{4,36},{5,37},{6,38},{7,39},{8,40},{9,... | collective-permute-start | bytes 67592 | tf_op jit(solution)/shard_map/ppermute | solution.py:55
  172.6 5.9 %collective-permute-start.24 = (f32[176,32]{0,1:T(8,128)S(1)}, f32[176,32]{0,1:T(8,128)S(1)}, u32[]{:S(2)}, u32[]{:S(2)}) collective-permute-start(f32[176,32]{0,1:T(8,128)S(1)} %add.147), channel_id=1, source_target_pairs={{0,256},{1,257},{2,258},{3,259},{4,260},{5,261},{6,262},{7,263},{8... | collective-permute-start | bytes 67592 | tf_op jit(solution)/shard_map/ppermute | solution.py:55
  178.5 8.7 %collective-permute-start.25 = (f32[176,32]{0,1:T(8,128)S(1)}, f32[176,32]{0,1:T(8,128)S(1)}, u32[]{:S(2)}, u32[]{:S(2)}) collective-permute-start(f32[176,32]{0,1:T(8,128)S(1)} %add.148), channel_id=1, source_target_pairs={{0,8},{1,9},{2,10},{3,11},{4,12},{5,13},{6,14},{7,15},{8,0},{9,1},... | collective-permute-start | bytes 67592 | tf_op jit(solution)/shard_map/ppermute | solution.py:55
  187.2 8.6 %collective-permute-start.26 = (f32[176,32]{0,1:T(8,128)S(1)}, f32[176,32]{0,1:T(8,128)S(1)}, u32[]{:S(2)}, u32[]{:S(2)}) collective-permute-start(f32[176,32]{0,1:T(8,128)S(1)} %add.149), channel_id=1, source_target_pairs={{0,64},{1,65},{2,66},{3,67},{4,68},{5,69},{6,70},{7,71},{8,72},{9,... | collective-permute-start | bytes 67592 | tf_op jit(solution)/shard_map/ppermute | solution.py:55
  195.8 8.6 %collective-permute-start.27 = (f32[176,32]{0,1:T(8,128)S(1)}, f32[176,32]{0,1:T(8,128)S(1)}, u32[]{:S(2)}, u32[]{:S(2)}) collective-permute-start(f32[176,32]{0,1:T(8,128)S(1)} %add.150), channel_id=1, source_target_pairs={{0,512},{1,513},{2,514},{3,515},{4,516},{5,517},{6,518},{7,519},{8... | collective-permute-start | bytes 67592 | tf_op jit(solution)/shard_map/ppermute | solution.py:55
  204.4 4.6 %collective-permute-start.28 = (f32[176,32]{0,1:T(8,128)S(1)}, f32[176,32]{0,1:T(8,128)S(1)}, u32[]{:S(2)}, u32[]{:S(2)}) collective-permute-start(f32[176,32]{0,1:T(8,128)S(1)} %add.151), channel_id=1, source_target_pairs={{0,16},{1,17},{2,18},{3,19},{4,20},{5,21},{6,22},{7,23},{8,24},{9,... | collective-permute-start | bytes 67592 | tf_op jit(solution)/shard_map/ppermute | solution.py:58
  209.1 19.7 %collective-permute-start.29 = (f32[352,32]{0,1:T(8,128)S(1)}, f32[352,32]{0,1:T(8,128)S(1)}, u32[]{:S(2)}, u32[]{:S(2)}) collective-permute-start(f32[352,32]{0,1:T(8,128)S(1)} %maximum_select_fusion.3), channel_id=1, source_target_pairs={{0,1},{1,0},{2,3},{3,2},{4,5},{5,4},{6,7},{7,6},{8,9},{9,8},{10,11... | collective-permute-start | bytes 135176 | tf_op jit(solution)/shard_map/ppermute | solution.py:63
  222.3 7.1 %collective-permute-start.30 = (f32[352,32]{0,1:T(8,128)S(1)}, f32[352,32]{0,1:T(8,128)S(1)}, u32[]{:S(2)}, u32[]{:S(2)}) collective-permute-start(f32[352,32]{0,1:T(8,128)S(1)} %maximum_select_fusion.3), channel_id=1, source_target_pairs={{0,2},{1,3},{2,0},{3,1},{4,6},{5,7},{6,4},{7,5},{8,10},{9,11},{10,... | collective-permute-start | bytes 135176 | tf_op jit(solution)/shard_map/ppermute | solution.py:63
  226.1 5.5 %collective-permute-start.31 = (f32[352,32]{0,1:T(8,128)S(1)}, f32[352,32]{0,1:T(8,128)S(1)}, u32[]{:S(2)}, u32[]{:S(2)}) collective-permute-start(f32[352,32]{0,1:T(8,128)S(1)} %maximum_select_fusion.3), channel_id=1, source_target_pairs={{0,3},{1,2},{2,1},{3,0},{4,7},{5,6},{6,5},{7,4},{8,11},{9,10},{10,... | collective-permute-start | bytes 135176 | tf_op jit(solution)/shard_map/ppermute | solution.py:63
  232.3 3.3 %copy-start.2 = (f32[1408,32]{0,1:T(8,128)}, f32[1408,32]{0,1:T(8,128)S(1)}, u32[]{:S(2)}) copy-start(f32[1408,32]{0,1:T(8,128)S(1)} %broadcast_multiply_fusion) | copy-start | bytes 540676

commit v4 on v2

--- a/solution.py
+++ b/solution.py
@@ -32,9 +32,8 @@
         if len(halved) < max_halvings and rows % 16 == 0:
             half = rows // 2
             mine = (idx >> bit) & 1
-            lo, hi = x[:half], x[half:]
-            send = jnp.where(mine == 1, lo, hi)
-            keep = jnp.where(mine == 1, hi, lo)
+            send = lax.dynamic_slice_in_dim(x, (1 - mine) * half, half, 0)
+            keep = lax.dynamic_slice_in_dim(x, mine * half, half, 0)
             x = keep + lax.ppermute(send, AXES, xor_pairs(n, bit))
             halved.append(bit)
         else:
@@ -42,7 +41,7 @@
     for bit in reversed(halved):
         mine = (idx >> bit) & 1
         other = lax.ppermute(x, AXES, xor_pairs(n, bit))
-        x = jnp.where(mine == 1, jnp.concatenate([other, x]), jnp.concatenate([x, other]))
+        x = lax.dynamic_update_slice_in_dim(jnp.concatenate([other, other]), x, mine * x.shape[0], 0)
     return x
 
 

time: 228 us -> 232 us (1.018)
  local copies, waits for them, and re-layouts: 2.42 us -> 6.78 us
    dynamic_update_slice x0 -> x8, local copies, waits for them, and re-layouts: none -> 4.51 us  [butterfly_sum(): lax.dynamic_update_slice_in_dim(jnp.concatenate([other, other]), x, mine...]
where the time goes in v4:
time: 232 us; the launch traced here: 230 us
  starting transfers between devices  108 us (47%)
  waiting for transfers between devices  95.1 us (41%)
  other arithmetic  9.96 us (4%)
  matrix products  9.53 us (4%)
  local copies, waits for them, and re-layouts  6.78 us (3%)
    ppermute x12, waiting for transfers between devices, butterfly_sum(): x = x + lax.ppermute(x, AXES, xor_pairs(n, bit))  49 us
    ppermute x8, starting transfers between devices, butterfly_sum(): other = lax.ppermute(x, AXES, xor_pairs(n, bit))  42.7 us
    ppermute x12, starting transfers between devices, butterfly_sum(): x = x + lax.ppermute(x, AXES, xor_pairs(n, bit))  35.4 us
    ppermute x8, starting transfers between devices, butterfly_sum(): x = keep + lax.ppermute(send, AXES, xor_pairs(n, bit))  29.8 us
    ppermute x8, waiting for transfers between devices, butterfly_sum(): x = keep + lax.ppermute(send, AXES, xor_pairs(n, bit))  24 us
    ppermute x8, waiting for transfers between devices, butterfly_sum(): other = lax.ppermute(x, AXES, xor_pairs(n, bit))  22.2 us
  transfers between devices with their start and end apart: 28, of which 28 were waited for; matrix products, arithmetic and copies ran while one was open for 0% of the time, Pallas kernels for 0%

profile of v4, /device:TPU:1, one launch (start us, length us, event | category | flops | bytes accessed | tf_op | source)
XLA Modules:
  0.0 230.4 jit_solution(9852318605485334428)
XLA Ops:
  2.2 2.0 fusion
  4.3 16.0 %collective-permute-start = (f32[2816,32]{0,1:T(8,128)S(1)}, f32[2816,32]{0,1:T(8,128)}, u32[]{:S(2)}, u32[]{:S(2)}) collective-permute-start(f32[2816,32]{0,1:T(8,128)S(1)} %dynamic-slice_bitcast_fusion), channel_id=1, source_target_pairs={{0,1},{1,0},{2,3},{3,2},{4,5},{5,4},{6,7},{7,6},{8,9},{9,8},{10,11... | collective-permute-start | bytes 1081352 | tf_op jit(solution)/shard_map/ppermute | solution.py:37
  22.8 1.9 collective-permute-start.1
  24.7 5.7 %collective-permute-done.1 = f32[1408,32]{0,1:T(8,128)S(1)} collective-permute-done((f32[1408,32]{0,1:T(8,128)S(1)}, f32[1408,32]{0,1:T(8,128)S(1)}, u32[]{:S(2)}, u32[]{:S(2)}) %collective-permute-start.1) | collective-permute-done | bytes 180256 | tf_op jit(solution)/shard_map/ppermute | solution.py:37
  30.6 1.9 collective-permute-start.2
  32.5 3.4 %collective-permute-done.2 = f32[704,32]{0,1:T(8,128)S(1)} collective-permute-done((f32[704,32]{0,1:T(8,128)S(1)}, f32[704,32]{0,1:T(8,128)S(1)}, u32[]{:S(2)}, u32[]{:S(2)}) %collective-permute-start.2) | collective-permute-done | bytes 90144 | tf_op jit(solution)/shard_map/ppermute | solution.py:37
  36.1 1.9 collective-permute-start.3
  38.1 2.9 %collective-permute-done.3 = f32[352,32]{0,1:T(8,128)S(1)} collective-permute-done((f32[352,32]{0,1:T(8,128)S(1)}, f32[352,32]{0,1:T(8,128)S(1)}, u32[]{:S(2)}, u32[]{:S(2)}) %collective-permute-start.3) | collective-permute-done | bytes 45088 | tf_op jit(solution)/shard_map/ppermute | solution.py:37
  41.1 1.9 collective-permute-start.4
  43.1 4.0 %collective-permute-done.4 = f32[176,32]{0,1:T(8,128)S(1)} collective-permute-done((f32[176,32]{0,1:T(8,128)S(1)}, f32[176,32]{0,1:T(8,128)S(1)}, u32[]{:S(2)}, u32[]{:S(2)}) %collective-permute-start.4) | collective-permute-done | bytes 22560 | tf_op jit(solution)/shard_map/ppermute | solution.py:37
  49.0 3.7 %collective-permute-done.5 = f32[176,32]{0,1:T(8,128)S(1)} collective-permute-done((f32[176,32]{0,1:T(8,128)S(1)}, f32[176,32]{0,1:T(8,128)S(1)}, u32[]{:S(2)}, u32[]{:S(2)}) %collective-permute-start.5) | collective-permute-done | bytes 22560 | tf_op jit(solution)/shard_map/ppermute | solution.py:40
  54.7 3.7 %collective-permute-done.6 = f32[176,32]{0,1:T(8,128)S(1)} collective-permute-done((f32[176,32]{0,1:T(8,128)S(1)}, f32[176,32]{0,1:T(8,128)S(1)}, u32[]{:S(2)}, u32[]{:S(2)}) %collective-permute-start.6) | collective-permute-done | bytes 22560 | tf_op jit(solution)/shard_map/ppermute | solution.py:40
  60.3 6.6 %collective-permute-done.7 = f32[176,32]{0,1:T(8,128)S(1)} collective-permute-done((f32[176,32]{0,1:T(8,128)S(1)}, f32[176,32]{0,1:T(8,128)S(1)}, u32[]{:S(2)}, u32[]{:S(2)}) %collective-permute-start.7) | collective-permute-done | bytes 22560 | tf_op jit(solution)/shard_map/ppermute | solution.py:40
  66.9 3.8 %collective-permute-start.8 = (f32[176,32]{0,1:T(8,128)S(1)}, f32[176,32]{0,1:T(8,128)S(1)}, u32[]{:S(2)}, u32[]{:S(2)}) collective-permute-start(f32[176,32]{0,1:T(8,128)S(1)} %add.150), channel_id=1, source_target_pairs={{0,64},{1,65},{2,66},{3,67},{4,68},{5,69},{6,70},{7,71},{8,72},{9,... | collective-permute-start | bytes 67592 | tf_op jit(solution)/shard_map/ppermute | solution.py:40
  70.8 4.7 %collective-permute-done.8 = f32[176,32]{0,1:T(8,128)S(1)} collective-permute-done((f32[176,32]{0,1:T(8,128)S(1)}, f32[176,32]{0,1:T(8,128)S(1)}, u32[]{:S(2)}, u32[]{:S(2)}) %collective-permute-start.8) | collective-permute-done | bytes 22560 | tf_op jit(solution)/shard_map/ppermute | solution.py:40
  75.5 4.6 %collective-permute-start.9 = (f32[176,32]{0,1:T(8,128)S(1)}, f32[176,32]{0,1:T(8,128)S(1)}, u32[]{:S(2)}, u32[]{:S(2)}) collective-permute-start(f32[176,32]{0,1:T(8,128)S(1)} %add.151), channel_id=1, source_target_pairs={{0,512},{1,513},{2,514},{3,515},{4,516},{5,517},{6,518},{7,519},{8... | collective-permute-start | bytes 67592 | tf_op jit(solution)/shard_map/ppermute | solution.py:40
  80.1 3.9 %collective-permute-done.9 = f32[176,32]{0,1:T(8,128)S(1)} collective-permute-done((f32[176,32]{0,1:T(8,128)S(1)}, f32[176,32]{0,1:T(8,128)S(1)}, u32[]{:S(2)}, u32[]{:S(2)}) %collective-permute-start.9) | collective-permute-done | bytes 22560 | tf_op jit(solution)/shard_map/ppermute | solution.py:40
  86.0 3.9 %collective-permute-done.10 = f32[176,32]{0,1:T(8,128)S(1)} collective-permute-done((f32[176,32]{0,1:T(8,128)S(1)}, f32[176,32]{0,1:T(8,128)S(1)}, u32[]{:S(2)}, u32[]{:S(2)}) %collective-permute-start.10) | collective-permute-done | bytes 22560 | tf_op jit(solution)/shard_map/ppermute | solution.py:43
  90.3 1.9 collective-permute-start.11
  92.3 2.9 %collective-permute-done.11 = f32[352,32]{0,1:T(8,128)S(1)} collective-permute-done((f32[352,32]{0,1:T(8,128)S(1)}, f32[352,32]{0,1:T(8,128)S(1)}, u32[]{:S(2)}, u32[]{:S(2)}) %collective-permute-start.11) | collective-permute-done | bytes 45088 | tf_op jit(solution)/shard_map/ppermute | solution.py:43
  95.8 1.9 collective-permute-start.12
  97.8 3.4 %collective-permute-done.12 = f32[704,32]{0,1:T(8,128)S(1)} collective-permute-done((f32[704,32]{0,1:T(8,128)S(1)}, f32[704,32]{0,1:T(8,128)S(1)}, u32[]{:S(2)}, u32[]{:S(2)}) %collective-permute-start.12) | collective-permute-done | bytes 90144 | tf_op jit(solution)/shard_map/ppermute | solution.py:43
  102.1 1.9 collective-permute-start.13
  104.1 4.3 %collective-permute-done.13 = f32[1408,32]{0,1:T(8,128)S(1)} collective-permute-done((f32[1408,32]{0,1:T(8,128)S(1)}, f32[1408,32]{0,1:T(8,128)S(1)}, u32[]{:S(2)}, u32[]{:S(2)}) %collective-permute-start.13) | collective-permute-done | bytes 180256 | tf_op jit(solution)/shard_map/ppermute | solution.py:43
  108.4 16.6 %collective-permute-start.14 = (f32[2816,32]{0,1:T(8,128)S(1)}, f32[2816,32]{0,1:T(8,128)}, u32[]{:S(2)}, u32[]{:S(2)}) collective-permute-start(f32[2816,32]{0,1:T(8,128)S(1)} %constant_dynamic-update-slice_fusion.1), channel_id=1, source_target_pairs={{0,1},{1,0},{2,3},{3,2},{4,5},{5,4},{6,7},{7,6},{8,9},{9,8},{10,11... | collective-permute-start | bytes 1081352 | tf_op jit(solution)/shard_map/ppermute | solution.py:43
  129.1 2.9 %cholesky.16 = f32[32,32]{1,0:T(8,128)S(1)} custom-call(f32[32,32]{1,0:T(8,128)S(1)} %fusion.9), custom_call_target="Cholesky" | custom-call | tf_op jit(solution)/shard_map/cholesky | solution.py:49
  133.4 2.4 %custom-call.5 = f32[1,32,32]{1,2,0:T(8,128)S(1)} custom-call(f32[1,32,32]{2,1,0:T(8,128)S(1)} %fusion.6), custom_call_target="InvertDiagBlocksLowerTriangular" | custom-call | tf_op jit(solution)/shard_map/triangular_solve | solution.py:50
  137.5 2.2 fusion.1
  139.8 2.3 collective-permute-start.15
  143.2 1.9 collective-permute-start.16
  145.1 2.9 %collective-permute-done.16 = f32[352,32]{0,1:T(8,128)S(1)} collective-permute-done((f32[352,32]{0,1:T(8,128)S(1)}, f32[352,32]{0,1:T(8,128)S(1)}, u32[]{:S(2)}, u32[]{:S(2)}) %collective-permute-start.16) | collective-permute-done | bytes 45088 | tf_op jit(solution)/shard_map/ppermute | solution.py:37
  150.1 2.7 %collective-permute-done.17 = f32[176,32]{0,1:T(8,128)S(1)} collective-permute-done((f32[176,32]{0,1:T(8,128)S(1)}, f32[176,32]{0,1:T(8,128)S(1)}, u32[]{:S(2)}, u32[]{:S(2)}) %collective-permute-start.17) | collective-permute-done | bytes 22560 | tf_op jit(solution)/shard_map/ppermute | solution.py:37
  152.9 1.9 collective-permute-start.18
  154.8 2.7 %collective-permute-done.18 = f32[176,32]{0,1:T(8,128)S(1)} collective-permute-done((f32[176,32]{0,1:T(8,128)S(1)}, f32[176,32]{0,1:T(8,128)S(1)}, u32[]{:S(2)}, u32[]{:S(2)}) %collective-permute-start.18) | collective-permute-done | bytes 22560 | tf_op jit(solution)/shard_map/ppermute | solution.py:40
  159.5 3.7 %collective-permute-done.19 = f32[176,32]{0,1:T(8,128)S(1)} collective-permute-done((f32[176,32]{0,1:T(8,128)S(1)}, f32[176,32]{0,1:T(8,128)S(1)}, u32[]{:S(2)}, u32[]{:S(2)}) %collective-permute-start.19) | collective-permute-done | bytes 22560 | tf_op jit(solution)/shard_map/ppermute | solution.py:40
  165.1 3.7 %collective-permute-done.20 = f32[176,32]{0,1:T(8,128)S(1)} collective-permute-done((f32[176,32]{0,1:T(8,128)S(1)}, f32[176,32]{0,1:T(8,128)S(1)}, u32[]{:S(2)}, u32[]{:S(2)}) %collective-permute-start.20) | collective-permute-done | bytes 22560 | tf_op jit(solution)/shard_map/ppermute | solution.py:40
  170.7 3.8 %collective-permute-done.21 = f32[176,32]{0,1:T(8,128)S(1)} collective-permute-done((f32[176,32]{0,1:T(8,128)S(1)}, f32[176,32]{0,1:T(8,128)S(1)}, u32[]{:S(2)}, u32[]{:S(2)}) %collective-permute-start.21) | collective-permute-done | bytes 22560 | tf_op jit(solution)/shard_map/ppermute | solution.py:40
  174.5 4.3 %collective-permute-start.22 = (f32[176,32]{0,1:T(8,128)S(1)}, f32[176,32]{0,1:T(8,128)S(1)}, u32[]{:S(2)}, u32[]{:S(2)}) collective-permute-start(f32[176,32]{0,1:T(8,128)S(1)} %add.167), channel_id=1, source_target_pairs={{0,8},{1,9},{2,10},{3,11},{4,12},{5,13},{6,14},{7,15},{8,0},{9,1},... | collective-permute-start | bytes 67592 | tf_op jit(solution)/shard_map/ppermute | solution.py:40
  178.8 4.6 %collective-permute-done.22 = f32[176,32]{0,1:T(8,128)S(1)} collective-permute-done((f32[176,32]{0,1:T(8,128)S(1)}, f32[176,32]{0,1:T(8,128)S(1)}, u32[]{:S(2)}, u32[]{:S(2)}) %collective-permute-start.22) | collective-permute-done | bytes 22560 | tf_op jit(solution)/shard_map/ppermute | solution.py:40
  183.3 4.4 %collective-permute-start.23 = (f32[176,32]{0,1:T(8,128)S(1)}, f32[176,32]{0,1:T(8,128)S(1)}, u32[]{:S(2)}, u32[]{:S(2)}) collective-permute-start(f32[176,32]{0,1:T(8,128)S(1)} %add.168), channel_id=1, source_target_pairs={{0,64},{1,65},{2,66},{3,67},{4,68},{5,69},{6,70},{7,71},{8,72},{9,... | collective-permute-start | bytes 67592 | tf_op jit(solution)/shard_map/ppermute | solution.py:40
  187.7 4.2 %collective-permute-done.23 = f32[176,32]{0,1:T(8,128)S(1)} collective-permute-done((f32[176,32]{0,1:T(8,128)S(1)}, f32[176,32]{0,1:T(8,128)S(1)}, u32[]{:S(2)}, u32[]{:S(2)}) %collective-permute-start.23) | collective-permute-done | bytes 22560 | tf_op jit(solution)/shard_map/ppermute | solution.py:40
  191.9 4.9 %collective-permute-start.24 = (f32[176,32]{0,1:T(8,128)S(1)}, f32[176,32]{0,1:T(8,128)S(1)}, u32[]{:S(2)}, u32[]{:S(2)}) collective-permute-start(f32[176,32]{0,1:T(8,128)S(1)} %add.169), channel_id=1, source_target_pairs={{0,512},{1,513},{2,514},{3,515},{4,516},{5,517},{6,518},{7,519},{8... | collective-permute-start | bytes 67592 | tf_op jit(solution)/shard_map/ppermute | solution.py:40
  196.8 3.7 %collective-permute-done.24 = f32[176,32]{0,1:T(8,128)S(1)} collective-permute-done((f32[176,32]{0,1:T(8,128)S(1)}, f32[176,32]{0,1:T(8,128)S(1)}, u32[]{:S(2)}, u32[]{:S(2)}) %collective-permute-start.24) | collective-permute-done | bytes 22560 | tf_op jit(solution)/shard_map/ppermute | solution.py:40
  202.4 2.7 %collective-permute-done.25 = f32[176,32]{0,1:T(8,128)S(1)} collective-permute-done((f32[176,32]{0,1:T(8,128)S(1)}, f32[176,32]{0,1:T(8,128)S(1)}, u32[]{:S(2)}, u32[]{:S(2)}) %collective-permute-start.25) | collective-permute-done | bytes 22560 | tf_op jit(solution)/shard_map/ppermute | solution.py:43
  205.6 2.2 collective-permute-start.26
  207.8 2.6 %collective-permute-done.26 = f32[352,32]{0,1:T(8,128)S(1)} collective-permute-done((f32[352,32]{0,1:T(8,128)S(1)}, f32[352,32]{0,1:T(8,128)S(1)}, u32[]{:S(2)}, u32[]{:S(2)}) %collective-permute-start.26) | collective-permute-done | bytes 45088 | tf_op jit(solution)/shard_map/ppermute | solution.py:43
  211.1 14.3 %collective-permute-start.27 = (f32[704,32]{0,1:T(8,128)S(1)}, f32[704,32]{0,1:T(8,128)S(1)}, u32[]{:S(2)}, u32[]{:S(2)}) collective-permute-start(f32[704,32]{0,1:T(8,128)S(1)} %dynamic_update_slice.30), channel_id=1, source_target_pairs={{0,1},{1,0},{2,3},{3,2},{4,5},{5,4},{6,7},{7,6},{8,9},{9,8},{10,11... | collective-permute-start | bytes 270344 | tf_op jit(solution)/shard_map/ppermute | solution.py:43
  227.2 3.2 %fusion.4 = f32[352,1408]{1,0:T(8,128)} fusion(f32[1408,32]{0,1:T(8,128)S(1)} %broadcast_multiply_fusion, f32[5632,32]{0,1:T(8,128)} %fusion.7, s32[]{:T(128)S(6)} %select_n.73), kind=kOutput, calls=%fused_computation.21 | convolution fusion | flops 95158272 | bytes 2211844 | tf_op jit(solution)/shard_map/dot_general | solution.py:73
  (73 shorter events, 35.3 us)
Async XLA Ops:
  0.6 1.6 copy-start
  4.3 17.4 %collective-permute-start = (f32[2816,32]{0,1:T(8,128)S(1)}, f32[2816,32]{0,1:T(8,128)}, u32[]{:S(2)}, u32[]{:S(2)}) collective-permute-start(f32[2816,32]{0,1:T(8,128)S(1)} %dynamic-slice_bitcast_fusion), channel_id=1, source_target_pairs={{0,1},{1,0},{2,3},{3,2},{4,5},{5,4},{6,7},{7,6},{8,9},{9,8},{10,11... | collective-permute-start | bytes 1081352 | tf_op jit(solution)/shard_map/ppermute | solution.py:37
  22.8 7.6 %collective-permute-start.1 = (f32[1408,32]{0,1:T(8,128)S(1)}, f32[1408,32]{0,1:T(8,128)S(1)}, u32[]{:S(2)}, u32[]{:S(2)}) collective-permute-start(f32[1408,32]{0,1:T(8,128)S(1)} %constant_dynamic-slice_fusion.5), channel_id=1, source_target_pairs={{0,2},{1,3},{2,0},{3,1},{4,6},{5,7},{6,4},{7,5},{8,10},{9,11},{10,... | collective-permute-start | bytes 540680 | tf_op jit(solution)/shard_map/ppermute | solution.py:37
  30.6 5.4 %collective-permute-start.2 = (f32[704,32]{0,1:T(8,128)S(1)}, f32[704,32]{0,1:T(8,128)S(1)}, u32[]{:S(2)}, u32[]{:S(2)}) collective-permute-start(f32[704,32]{0,1:T(8,128)S(1)} %constant_dynamic-slice_fusion.4), channel_id=1, source_target_pairs={{0,16},{1,17},{2,18},{3,19},{4,20},{5,21},{6,22},{7,23},{8,24},{9,... | collective-permute-start | bytes 270344 | tf_op jit(solution)/shard_map/ppermute | solution.py:37
  36.1 4.8 %collective-permute-start.3 = (f32[352,32]{0,1:T(8,128)S(1)}, f32[352,32]{0,1:T(8,128)S(1)}, u32[]{:S(2)}, u32[]{:S(2)}) collective-permute-start(f32[352,32]{0,1:T(8,128)S(1)} %constant_dynamic-slice_fusion.3), channel_id=1, source_target_pairs={{0,128},{1,129},{2,130},{3,131},{4,132},{5,133},{6,134},{7,135},{8... | collective-permute-start | bytes 135176 | tf_op jit(solution)/shard_map/ppermute | solution.py:37
  41.1 5.9 %collective-permute-start.4 = (f32[176,32]{0,1:T(8,128)S(1)}, f32[176,32]{0,1:T(8,128)S(1)}, u32[]{:S(2)}, u32[]{:S(2)}) collective-permute-start(f32[176,32]{0,1:T(8,128)S(1)} %constant_dynamic-slice_fusion.2), channel_id=1, source_target_pairs={{0,4},{1,5},{2,6},{3,7},{4,0},{5,1},{6,2},{7,3},{8,12},{9,13},{10,... | collective-permute-start | bytes 67592 | tf_op jit(solution)/shard_map/ppermute | solution.py:37
  47.1 5.6 %collective-permute-start.5 = (f32[176,32]{0,1:T(8,128)S(1)}, f32[176,32]{0,1:T(8,128)S(1)}, u32[]{:S(2)}, u32[]{:S(2)}) collective-permute-start(f32[176,32]{0,1:T(8,128)S(1)} %dynamic-slice_add_fusion.5), channel_id=1, source_target_pairs={{0,32},{1,33},{2,34},{3,35},{4,36},{5,37},{6,38},{7,39},{8,40},{9,... | collective-permute-start | bytes 67592 | tf_op jit(solution)/shard_map/ppermute | solution.py:40
  52.7 5.6 %collective-permute-start.6 = (f32[176,32]{0,1:T(8,128)S(1)}, f32[176,32]{0,1:T(8,128)S(1)}, u32[]{:S(2)}, u32[]{:S(2)}) collective-permute-start(f32[176,32]{0,1:T(8,128)S(1)} %add.148), channel_id=1, source_target_pairs={{0,256},{1,257},{2,258},{3,259},{4,260},{5,261},{6,262},{7,263},{8... | collective-permute-start | bytes 67592 | tf_op jit(solution)/shard_map/ppermute | solution.py:40
  58.4 8.6 %collective-permute-start.7 = (f32[176,32]{0,1:T(8,128)S(1)}, f32[176,32]{0,1:T(8,128)S(1)}, u32[]{:S(2)}, u32[]{:S(2)}) collective-permute-start(f32[176,32]{0,1:T(8,128)S(1)} %add.149), channel_id=1, source_target_pairs={{0,8},{1,9},{2,10},{3,11},{4,12},{5,13},{6,14},{7,15},{8,0},{9,1},... | collective-permute-start | bytes 67592 | tf_op jit(solution)/shard_map/ppermute | solution.py:40
  66.9 8.6 %collective-permute-start.8 = (f32[176,32]{0,1:T(8,128)S(1)}, f32[176,32]{0,1:T(8,128)S(1)}, u32[]{:S(2)}, u32[]{:S(2)}) collective-permute-start(f32[176,32]{0,1:T(8,128)S(1)} %add.150), channel_id=1, source_target_pairs={{0,64},{1,65},{2,66},{3,67},{4,68},{5,69},{6,70},{7,71},{8,72},{9,... | collective-permute-start | bytes 67592 | tf_op jit(solution)/shard_map/ppermute | solution.py:40
  75.5 8.6 %collective-permute-start.9 = (f32[176,32]{0,1:T(8,128)S(1)}, f32[176,32]{0,1:T(8,128)S(1)}, u32[]{:S(2)}, u32[]{:S(2)}) collective-permute-start(f32[176,32]{0,1:T(8,128)S(1)} %add.151), channel_id=1, source_target_pairs={{0,512},{1,513},{2,514},{3,515},{4,516},{5,517},{6,518},{7,519},{8... | collective-permute-start | bytes 67592 | tf_op jit(solution)/shard_map/ppermute | solution.py:40
  84.1 5.8 %collective-permute-start.10 = (f32[176,32]{0,1:T(8,128)S(1)}, f32[176,32]{0,1:T(8,128)S(1)}, u32[]{:S(2)}, u32[]{:S(2)}) collective-permute-start(f32[176,32]{0,1:T(8,128)S(1)} %add.152), channel_id=1, source_target_pairs={{0,4},{1,5},{2,6},{3,7},{4,0},{5,1},{6,2},{7,3},{8,12},{9,13},{10,... | collective-permute-start | bytes 67592 | tf_op jit(solution)/shard_map/ppermute | solution.py:43
  90.3 4.8 %collective-permute-start.11 = (f32[352,32]{0,1:T(8,128)S(1)}, f32[352,32]{0,1:T(8,128)S(1)}, u32[]{:S(2)}, u32[]{:S(2)}) collective-permute-start(f32[352,32]{0,1:T(8,128)S(1)} %dynamic_update_slice.24), channel_id=1, source_target_pairs={{0,128},{1,129},{2,130},{3,131},{4,132},{5,133},{6,134},{7,135},{8... | collective-permute-start | bytes 135176 | tf_op jit(solution)/shard_map/ppermute | solution.py:43
  95.8 5.4 %collective-permute-start.12 = (f32[704,32]{0,1:T(8,128)S(1)}, f32[704,32]{0,1:T(8,128)S(1)}, u32[]{:S(2)}, u32[]{:S(2)}) collective-permute-start(f32[704,32]{0,1:T(8,128)S(1)} %dynamic_update_slice.25), channel_id=1, source_target_pairs={{0,16},{1,17},{2,18},{3,19},{4,20},{5,21},{6,22},{7,23},{8,24},{9,... | collective-permute-start | bytes 270344 | tf_op jit(solution)/shard_map/ppermute | solution.py:43
  102.1 6.2 %collective-permute-start.13 = (f32[1408,32]{0,1:T(8,128)S(1)}, f32[1408,32]{0,1:T(8,128)S(1)}, u32[]{:S(2)}, u32[]{:S(2)}) collective-permute-start(f32[1408,32]{0,1:T(8,128)S(1)} %dynamic_update_slice.26), channel_id=1, source_target_pairs={{0,2},{1,3},{2,0},{3,1},{4,6},{5,7},{6,4},{7,5},{8,10},{9,11},{10,... | collective-permute-start | bytes 540680 | tf_op jit(solution)/shard_map/ppermute | solution.py:43
  108.4 16.6 %copy-start.2 = (f32[2816,32]{0,1:T(8,128)}, f32[2816,32]{0,1:T(8,128)S(1)}, u32[]{:S(2)}) copy-start(f32[2816,32]{0,1:T(8,128)S(1)} %constant_dynamic-update-slice_fusion.1) | copy-start | bytes 1081348
  108.4 18.0 %collective-permute-start.14 = (f32[2816,32]{0,1:T(8,128)S(1)}, f32[2816,32]{0,1:T(8,128)}, u32[]{:S(2)}, u32[]{:S(2)}) collective-permute-start(f32[2816,32]{0,1:T(8,128)S(1)} %constant_dynamic-update-slice_fusion.1), channel_id=1, source_target_pairs={{0,1},{1,0},{2,3},{3,2},{4,5},{5,4},{6,7},{7,6},{8,9},{9,8},{10,11... | collective-permute-start | bytes 1081352 | tf_op jit(solution)/shard_map/ppermute | solution.py:43
  125.0 12.4 %copy-start.1 = (bf16[192,1408]{1,0:T(8,128)(2,1)S(1)}, bf16[192,1408]{1,0:T(8,128)(2,1)}, u32[]{:S(2)}) copy-start(bf16[192,1408]{1,0:T(8,128)(2,1)} %param.4) | copy-start | bytes 1622020
  139.8 3.2 %collective-permute-start.15 = (f32[704,32]{0,1:T(8,128)S(1)}, f32[704,32]{0,1:T(8,128)S(1)}, u32[]{:S(2)}, u32[]{:S(2)}) collective-permute-start(f32[704,32]{0,1:T(8,128)S(1)} %dynamic-slice_bitcast_fusion.1), channel_id=1, source_target_pairs={{0,1},{1,0},{2,3},{3,2},{4,5},{5,4},{6,7},{7,6},{8,9},{9,8},{10,11... | collective-permute-start | bytes 270344 | tf_op jit(solution)/shard_map/ppermute | solution.py:37
  143.2 4.8 %collective-permute-start.16 = (f32[352,32]{0,1:T(8,128)S(1)}, f32[352,32]{0,1:T(8,128)S(1)}, u32[]{:S(2)}, u32[]{:S(2)}) collective-permute-start(f32[352,32]{0,1:T(8,128)S(1)} %constant_dynamic-slice_fusion.1), channel_id=1, source_target_pairs={{0,2},{1,3},{2,0},{3,1},{4,6},{5,7},{6,4},{7,5},{8,10},{9,11},{10,... | collective-permute-start | bytes 135176 | tf_op jit(solution)/shard_map/ppermute | solution.py:37
  148.2 4.6 %collective-permute-start.17 = (f32[176,32]{0,1:T(8,128)S(1)}, f32[176,32]{0,1:T(8,128)S(1)}, u32[]{:S(2)}, u32[]{:S(2)}) collective-permute-start(f32[176,32]{0,1:T(8,128)S(1)} %constant_dynamic-slice_fusion), channel_id=1, source_target_pairs={{0,16},{1,17},{2,18},{3,19},{4,20},{5,21},{6,22},{7,23},{8,24},{9,... | collective-permute-start | bytes 67592 | tf_op jit(solution)/shard_map/ppermute | solution.py:37
  152.9 4.6 %collective-permute-start.18 = (f32[176,32]{0,1:T(8,128)S(1)}, f32[176,32]{0,1:T(8,128)S(1)}, u32[]{:S(2)}, u32[]{:S(2)}) collective-permute-start(f32[176,32]{0,1:T(8,128)S(1)} %dynamic-slice_add_fusion.4), channel_id=1, source_target_pairs={{0,128},{1,129},{2,130},{3,131},{4,132},{5,133},{6,134},{7,135},{8... | collective-permute-start | bytes 67592 | tf_op jit(solution)/shard_map/ppermute | solution.py:40
  157.6 5.6 %collective-permute-start.19 = (f32[176,32]{0,1:T(8,128)S(1)}, f32[176,32]{0,1:T(8,128)S(1)}, u32[]{:S(2)}, u32[]{:S(2)}) collective-permute-start(f32[176,32]{0,1:T(8,128)S(1)} %add.164), channel_id=1, source_target_pairs={{0,4},{1,5},{2,6},{3,7},{4,0},{5,1},{6,2},{7,3},{8,12},{9,13},{10,... | collective-permute-start | bytes 67592 | tf_op jit(solution)/shard_map/ppermute | solution.py:40
  163.2 5.6 %collective-permute-start.20 = (f32[176,32]{0,1:T(8,128)S(1)}, f32[176,32]{0,1:T(8,128)S(1)}, u32[]{:S(2)}, u32[]{:S(2)}) collective-permute-start(f32[176,32]{0,1:T(8,128)S(1)} %add.165), channel_id=1, source_target_pairs={{0,32},{1,33},{2,34},{3,35},{4,36},{5,37},{6,38},{7,39},{8,40},{9,... | collective-permute-start | bytes 67592 | tf_op jit(solution)/shard_map/ppermute | solution.py:40
  168.8 5.7 %collective-permute-start.21 = (f32[176,32]{0,1:T(8,128)S(1)}, f32[176,32]{0,1:T(8,128)S(1)}, u32[]{:S(2)}, u32[]{:S(2)}) collective-permute-start(f32[176,32]{0,1:T(8,128)S(1)} %add.166), channel_id=1, source_target_pairs={{0,256},{1,257},{2,258},{3,259},{4,260},{5,261},{6,262},{7,263},{8... | collective-permute-start | bytes 67592 | tf_op jit(solution)/shard_map/ppermute | solution.py:40
  174.5 8.8 %collective-permute-start.22 = (f32[176,32]{0,1:T(8,128)S(1)}, f32[176,32]{0,1:T(8,128)S(1)}, u32[]{:S(2)}, u32[]{:S(2)}) collective-permute-start(f32[176,32]{0,1:T(8,128)S(1)} %add.167), channel_id=1, source_target_pairs={{0,8},{1,9},{2,10},{3,11},{4,12},{5,13},{6,14},{7,15},{8,0},{9,1},... | collective-permute-start | bytes 67592 | tf_op jit(solution)/shard_map/ppermute | solution.py:40
  183.3 8.6 %collective-permute-start.23 = (f32[176,32]{0,1:T(8,128)S(1)}, f32[176,32]{0,1:T(8,128)S(1)}, u32[]{:S(2)}, u32[]{:S(2)}) collective-permute-start(f32[176,32]{0,1:T(8,128)S(1)} %add.168), channel_id=1, source_target_pairs={{0,64},{1,65},{2,66},{3,67},{4,68},{5,69},{6,70},{7,71},{8,72},{9,... | collective-permute-start | bytes 67592 | tf_op jit(solution)/shard_map/ppermute | solution.py:40
  191.9 8.6 %collective-permute-start.24 = (f32[176,32]{0,1:T(8,128)S(1)}, f32[176,32]{0,1:T(8,128)S(1)}, u32[]{:S(2)}, u32[]{:S(2)}) collective-permute-start(f32[176,32]{0,1:T(8,128)S(1)} %add.169), channel_id=1, source_target_pairs={{0,512},{1,513},{2,514},{3,515},{4,516},{5,517},{6,518},{7,519},{8... | collective-permute-start | bytes 67592 | tf_op jit(solution)/shard_map/ppermute | solution.py:40
  200.5 4.6 %collective-permute-start.25 = (f32[176,32]{0,1:T(8,128)S(1)}, f32[176,32]{0,1:T(8,128)S(1)}, u32[]{:S(2)}, u32[]{:S(2)}) collective-permute-start(f32[176,32]{0,1:T(8,128)S(1)} %add.170), channel_id=1, source_target_pairs={{0,16},{1,17},{2,18},{3,19},{4,20},{5,21},{6,22},{7,23},{8,24},{9,... | collective-permute-start | bytes 67592 | tf_op jit(solution)/shard_map/ppermute | solution.py:43
  205.6 4.8 %collective-permute-start.26 = (f32[352,32]{0,1:T(8,128)S(1)}, f32[352,32]{0,1:T(8,128)S(1)}, u32[]{:S(2)}, u32[]{:S(2)}) collective-permute-start(f32[352,32]{0,1:T(8,128)S(1)} %dynamic_update_slice.29), channel_id=1, source_target_pairs={{0,2},{1,3},{2,0},{3,1},{4,6},{5,7},{6,4},{7,5},{8,10},{9,11},{10,... | collective-permute-start | bytes 135176 | tf_op jit(solution)/shard_map/ppermute | solution.py:43
  211.1 15.2 %collective-permute-start.27 = (f32[704,32]{0,1:T(8,128)S(1)}, f32[704,32]{0,1:T(8,128)S(1)}, u32[]{:S(2)}, u32[]{:S(2)}) collective-permute-start(f32[704,32]{0,1:T(8,128)S(1)} %dynamic_update_slice.30), channel_id=1, source_target_pairs={{0,1},{1,0},{2,3},{3,2},{4,5},{5,4},{6,7},{7,6},{8,9},{9,8},{10,11... | collective-permute-start | bytes 270344 | tf_op jit(solution)/shard_map/ppermute | solution.py:43
  227.2 3.3 %copy-start.3 = (f32[1408,32]{0,1:T(8,128)}, f32[1408,32]{0,1:T(8,128)S(1)}, u32[]{:S(2)}) copy-start(f32[1408,32]{0,1:T(8,128)S(1)} %broadcast_multiply_fusion) | copy-start | bytes 540676

commit v5 on v2

--- a/solution.py
+++ b/solution.py
@@ -69,7 +69,7 @@
         my_hat = lax.dynamic_slice_in_dim(p_hat, lax.axis_index("sub") * block_rows, block_rows, 0)
         v_low = jnp.dot(activations, p_low, preferred_element_type=jnp.float32).astype(jnp.bfloat16)
         q_local = jnp.einsum("tc,tr->cr", grad_out, v_low, preferred_element_type=jnp.float32)
-        q_sum = butterfly_sum(q_local, order, n, 3)
+        q_sum = butterfly_sum(q_local, order, n, 4)
         q_new = q_sum / n
         grad_approx = jnp.dot(my_hat, q_new.T, precision=lax.Precision.HIGH)
         return (grad_approx, q_new)

time: 228 us -> 232 us (1.018)
    ppermute x12 -> x11, waiting for transfers between devices: 48.9 us -> 45.2 us  [butterfly_sum(): x = x + lax.ppermute(x, AXES, xor_pairs(n, bit))]
    ppermute x8 -> x9, waiting for transfers between devices: 22.6 us -> 25.5 us  [butterfly_sum(): other = lax.ppermute(x, AXES, xor_pairs(n, bit))]
    ppermute x8 -> x9, starting transfers between devices: 42.3 us -> 44.9 us  [butterfly_sum(): other = lax.ppermute(x, AXES, xor_pairs(n, bit))]
    ppermute x8 -> x9, waiting for transfers between devices: 24 us -> 26.5 us  [butterfly_sum(): x = keep + lax.ppermute(send, AXES, xor_pairs(n, bit))]
    ppermute x8 -> x9, starting transfers between devices: 29.8 us -> 31.7 us  [butterfly_sum(): x = keep + lax.ppermute(send, AXES, xor_pairs(n, bit))]
    ppermute x12 -> x11, starting transfers between devices: 35.5 us -> 33.7 us  [butterfly_sum(): x = x + lax.ppermute(x, AXES, xor_pairs(n, bit))]
  transfers between devices with their start and end apart: 28 -> 29, of which waited for: 28 -> 29; matrix products, arithmetic and copies ran while one was open for 0% -> 0% of each run, Pallas kernels for 0% -> 0%
where the time goes in v5:
time: 232 us; the launch traced here: 231 us
  starting transfers between devices  110 us (47%)
  waiting for transfers between devices  97.2 us (42%)
  other arithmetic  11.6 us (5%)
  matrix products  8.74 us (4%)
  local copies, waits for them, and re-layouts  2.44 us (1%)
    ppermute x11, waiting for transfers between devices, butterfly_sum(): x = x + lax.ppermute(x, AXES, xor_pairs(n, bit))  45.2 us
    ppermute x9, starting transfers between devices, butterfly_sum(): other = lax.ppermute(x, AXES, xor_pairs(n, bit))  44.9 us
    ppermute x11, starting transfers between devices, butterfly_sum(): x = x + lax.ppermute(x, AXES, xor_pairs(n, bit))  33.7 us
    ppermute x9, starting transfers between devices, butterfly_sum(): x = keep + lax.ppermute(send, AXES, xor_pairs(n, bit))  31.7 us
    ppermute x9, waiting for transfers between devices, butterfly_sum(): x = keep + lax.ppermute(send, AXES, xor_pairs(n, bit))  26.5 us
    ppermute x9, waiting for transfers between devices, butterfly_sum(): other = lax.ppermute(x, AXES, xor_pairs(n, bit))  25.5 us
  transfers between devices with their start and end apart: 29, of which 29 were waited for; matrix products, arithmetic and copies ran while one was open for 0% of the time, Pallas kernels for 0%

profile of v5, /device:TPU:1, one launch (start us, length us, event | category | flops | bytes accessed | tf_op | source)
XLA Modules:
  0.0 231.4 jit_solution(10593149996551975180)
XLA Ops:
  2.2 2.0 convolution_bitcast_fusion
  4.3 16.0 %collective-permute-start = (f32[2816,32]{0,1:T(8,128)S(1)}, f32[2816,32]{0,1:T(8,128)}, u32[]{:S(2)}, u32[]{:S(2)}) collective-permute-start(f32[2816,32]{0,1:T(8,128)S(1)} %slice_select_fusion), channel_id=1, source_target_pairs={{0,1},{1,0},{2,3},{3,2},{4,5},{5,4},{6,7},{7,6},{8,9},{9,8},{10,11... | collective-permute-start | bytes 1081352 | tf_op jit(solution)/shard_map/ppermute | solution.py:38
  22.8 1.9 collective-permute-start.1
  24.8 5.7 %collective-permute-done.1 = f32[1408,32]{0,1:T(8,128)S(1)} collective-permute-done((f32[1408,32]{0,1:T(8,128)S(1)}, f32[1408,32]{0,1:T(8,128)S(1)}, u32[]{:S(2)}, u32[]{:S(2)}) %collective-permute-start.1) | collective-permute-done | bytes 180256 | tf_op jit(solution)/shard_map/ppermute | solution.py:38
  30.6 1.9 collective-permute-start.2
  32.5 3.4 %collective-permute-done.2 = f32[704,32]{0,1:T(8,128)S(1)} collective-permute-done((f32[704,32]{0,1:T(8,128)S(1)}, f32[704,32]{0,1:T(8,128)S(1)}, u32[]{:S(2)}, u32[]{:S(2)}) %collective-permute-start.2) | collective-permute-done | bytes 90144 | tf_op jit(solution)/shard_map/ppermute | solution.py:38
  36.1 1.9 collective-permute-start.3
  38.1 2.9 %collective-permute-done.3 = f32[352,32]{0,1:T(8,128)S(1)} collective-permute-done((f32[352,32]{0,1:T(8,128)S(1)}, f32[352,32]{0,1:T(8,128)S(1)}, u32[]{:S(2)}, u32[]{:S(2)}) %collective-permute-start.3) | collective-permute-done | bytes 45088 | tf_op jit(solution)/shard_map/ppermute | solution.py:38
  43.0 4.0 %collective-permute-done.4 = f32[176,32]{0,1:T(8,128)S(1)} collective-permute-done((f32[176,32]{0,1:T(8,128)S(1)}, f32[176,32]{0,1:T(8,128)S(1)}, u32[]{:S(2)}, u32[]{:S(2)}) %collective-permute-start.4) | collective-permute-done | bytes 22560 | tf_op jit(solution)/shard_map/ppermute | solution.py:38
  49.0 3.7 %collective-permute-done.5 = f32[176,32]{0,1:T(8,128)S(1)} collective-permute-done((f32[176,32]{0,1:T(8,128)S(1)}, f32[176,32]{0,1:T(8,128)S(1)}, u32[]{:S(2)}, u32[]{:S(2)}) %collective-permute-start.5) | collective-permute-done | bytes 22560 | tf_op jit(solution)/shard_map/ppermute | solution.py:41
  54.6 3.7 %collective-permute-done.6 = f32[176,32]{0,1:T(8,128)S(1)} collective-permute-done((f32[176,32]{0,1:T(8,128)S(1)}, f32[176,32]{0,1:T(8,128)S(1)}, u32[]{:S(2)}, u32[]{:S(2)}) %collective-permute-start.6) | collective-permute-done | bytes 22560 | tf_op jit(solution)/shard_map/ppermute | solution.py:41
  60.3 6.6 %collective-permute-done.7 = f32[176,32]{0,1:T(8,128)S(1)} collective-permute-done((f32[176,32]{0,1:T(8,128)S(1)}, f32[176,32]{0,1:T(8,128)S(1)}, u32[]{:S(2)}, u32[]{:S(2)}) %collective-permute-start.7) | collective-permute-done | bytes 22560 | tf_op jit(solution)/shard_map/ppermute | solution.py:41
  66.9 3.8 %collective-permute-start.8 = (f32[176,32]{0,1:T(8,128)S(1)}, f32[176,32]{0,1:T(8,128)S(1)}, u32[]{:S(2)}, u32[]{:S(2)}) collective-permute-start(f32[176,32]{0,1:T(8,128)S(1)} %add.84), channel_id=1, source_target_pairs={{0,64},{1,65},{2,66},{3,67},{4,68},{5,69},{6,70},{7,71},{8,72},{9,... | collective-permute-start | bytes 67592 | tf_op jit(solution)/shard_map/ppermute | solution.py:41
  70.8 4.7 %collective-permute-done.8 = f32[176,32]{0,1:T(8,128)S(1)} collective-permute-done((f32[176,32]{0,1:T(8,128)S(1)}, f32[176,32]{0,1:T(8,128)S(1)}, u32[]{:S(2)}, u32[]{:S(2)}) %collective-permute-start.8) | collective-permute-done | bytes 22560 | tf_op jit(solution)/shard_map/ppermute | solution.py:41
  75.5 4.6 %collective-permute-start.9 = (f32[176,32]{0,1:T(8,128)S(1)}, f32[176,32]{0,1:T(8,128)S(1)}, u32[]{:S(2)}, u32[]{:S(2)}) collective-permute-start(f32[176,32]{0,1:T(8,128)S(1)} %add.85), channel_id=1, source_target_pairs={{0,512},{1,513},{2,514},{3,515},{4,516},{5,517},{6,518},{7,519},{8... | collective-permute-start | bytes 67592 | tf_op jit(solution)/shard_map/ppermute | solution.py:41
  80.1 3.9 %collective-permute-done.9 = f32[176,32]{0,1:T(8,128)S(1)} collective-permute-done((f32[176,32]{0,1:T(8,128)S(1)}, f32[176,32]{0,1:T(8,128)S(1)}, u32[]{:S(2)}, u32[]{:S(2)}) %collective-permute-start.9) | collective-permute-done | bytes 22560 | tf_op jit(solution)/shard_map/ppermute | solution.py:41
  86.0 3.9 %collective-permute-done.10 = f32[176,32]{0,1:T(8,128)S(1)} collective-permute-done((f32[176,32]{0,1:T(8,128)S(1)}, f32[176,32]{0,1:T(8,128)S(1)}, u32[]{:S(2)}, u32[]{:S(2)}) %collective-permute-start.10) | collective-permute-done | bytes 22560 | tf_op jit(solution)/shard_map/ppermute | solution.py:44
  89.9 1.9 collective-permute-start.11
  91.9 2.9 %collective-permute-done.11 = f32[352,32]{0,1:T(8,128)S(1)} collective-permute-done((f32[352,32]{0,1:T(8,128)S(1)}, f32[352,32]{0,1:T(8,128)S(1)}, u32[]{:S(2)}, u32[]{:S(2)}) %collective-permute-start.11) | collective-permute-done | bytes 45088 | tf_op jit(solution)/shard_map/ppermute | solution.py:44
  94.9 2.1 collective-permute-start.12
  97.0 3.7 %collective-permute-done.12 = f32[704,32]{0,1:T(8,128)S(1)} collective-permute-done((f32[704,32]{0,1:T(8,128)S(1)}, f32[704,32]{0,1:T(8,128)S(1)}, u32[]{:S(2)}, u32[]{:S(2)}) %collective-permute-start.12) | collective-permute-done | bytes 90144 | tf_op jit(solution)/shard_map/ppermute | solution.py:44
  100.8 1.9 collective-permute-start.13
  102.7 4.3 %collective-permute-done.13 = f32[1408,32]{0,1:T(8,128)S(1)} collective-permute-done((f32[1408,32]{0,1:T(8,128)S(1)}, f32[1408,32]{0,1:T(8,128)S(1)}, u32[]{:S(2)}, u32[]{:S(2)}) %collective-permute-start.13) | collective-permute-done | bytes 180256 | tf_op jit(solution)/shard_map/ppermute | solution.py:44
  107.1 16.3 %collective-permute-start.14 = (f32[2816,32]{0,1:T(8,128)S(1)}, f32[2816,32]{0,1:T(8,128)S(1)}, u32[]{:S(2)}, u32[]{:S(2)}) collective-permute-start(f32[2816,32]{0,1:T(8,128)S(1)} %maximum_select_fusion.3), channel_id=1, source_target_pairs={{0,1},{1,0},{2,3},{3,2},{4,5},{5,4},{6,7},{7,6},{8,9},{9,8},{10,11... | collective-permute-start | bytes 1081352 | tf_op jit(solution)/shard_map/ppermute | solution.py:44
  125.9 2.9 %cholesky.16 = f32[32,32]{1,0:T(8,128)S(1)} custom-call(f32[32,32]{1,0:T(8,128)S(1)} %fusion.11), custom_call_target="Cholesky" | custom-call | tf_op jit(solution)/shard_map/cholesky | solution.py:50
  130.2 2.4 %custom-call.5 = f32[1,32,32]{1,2,0:T(8,128)S(1)} custom-call(f32[1,32,32]{2,1,0:T(8,128)S(1)} %fusion.9), custom_call_target="InvertDiagBlocksLowerTriangular" | custom-call | tf_op jit(solution)/shard_map/triangular_solve | solution.py:51
  132.6 2.2 fusion
  137.7 2.3 collective-permute-start.15
  142.0 1.9 collective-permute-start.16
  144.0 2.9 %collective-permute-done.16 = f32[352,32]{0,1:T(8,128)S(1)} collective-permute-done((f32[352,32]{0,1:T(8,128)S(1)}, f32[352,32]{0,1:T(8,128)S(1)}, u32[]{:S(2)}, u32[]{:S(2)}) %collective-permute-start.16) | collective-permute-done | bytes 45088 | tf_op jit(solution)/shard_map/ppermute | solution.py:38
  149.0 2.7 %collective-permute-done.17 = f32[176,32]{0,1:T(8,128)S(1)} collective-permute-done((f32[176,32]{0,1:T(8,128)S(1)}, f32[176,32]{0,1:T(8,128)S(1)}, u32[]{:S(2)}, u32[]{:S(2)}) %collective-permute-start.17) | collective-permute-done | bytes 22560 | tf_op jit(solution)/shard_map/ppermute | solution.py:38
  153.8 2.6 %collective-permute-done.18 = f32[88,32]{0,1:T(8,128)S(1)} collective-permute-done((f32[88,32]{0,1:T(8,128)S(1)}, f32[88,32]{0,1:T(8,128)S(1)}, u32[]{:S(2)}, u32[]{:S(2)}) %collective-permute-start.18) | collective-permute-done | bytes 11296 | tf_op jit(solution)/shard_map/ppermute | solution.py:38
  158.3 3.5 %collective-permute-done.19 = f32[88,32]{0,1:T(8,128)S(1)} collective-permute-done((f32[88,32]{0,1:T(8,128)S(1)}, f32[88,32]{0,1:T(8,128)S(1)}, u32[]{:S(2)}, u32[]{:S(2)}) %collective-permute-start.19) | collective-permute-done | bytes 11296 | tf_op jit(solution)/shard_map/ppermute | solution.py:41
  163.7 3.5 %collective-permute-done.20 = f32[88,32]{0,1:T(8,128)S(1)} collective-permute-done((f32[88,32]{0,1:T(8,128)S(1)}, f32[88,32]{0,1:T(8,128)S(1)}, u32[]{:S(2)}, u32[]{:S(2)}) %collective-permute-start.20) | collective-permute-done | bytes 11296 | tf_op jit(solution)/shard_map/ppermute | solution.py:41
  169.1 3.7 %collective-permute-done.21 = f32[88,32]{0,1:T(8,128)S(1)} collective-permute-done((f32[88,32]{0,1:T(8,128)S(1)}, f32[88,32]{0,1:T(8,128)S(1)}, u32[]{:S(2)}, u32[]{:S(2)}) %collective-permute-start.21) | collective-permute-done | bytes 11296 | tf_op jit(solution)/shard_map/ppermute | solution.py:41
  172.8 4.3 %collective-permute-start.22 = (f32[88,32]{0,1:T(8,128)S(1)}, f32[88,32]{0,1:T(8,128)S(1)}, u32[]{:S(2)}, u32[]{:S(2)}) collective-permute-start(f32[88,32]{0,1:T(8,128)S(1)} %add.95), channel_id=1, source_target_pairs={{0,8},{1,9},{2,10},{3,11},{4,12},{5,13},{6,14},{7,15},{8,0},{9,1},... | collective-permute-start | bytes 33800 | tf_op jit(solution)/shard_map/ppermute | solution.py:41
  177.1 4.3 %collective-permute-done.22 = f32[88,32]{0,1:T(8,128)S(1)} collective-permute-done((f32[88,32]{0,1:T(8,128)S(1)}, f32[88,32]{0,1:T(8,128)S(1)}, u32[]{:S(2)}, u32[]{:S(2)}) %collective-permute-start.22) | collective-permute-done | bytes 11296 | tf_op jit(solution)/shard_map/ppermute | solution.py:41
  181.4 4.5 %collective-permute-start.23 = (f32[88,32]{0,1:T(8,128)S(1)}, f32[88,32]{0,1:T(8,128)S(1)}, u32[]{:S(2)}, u32[]{:S(2)}) collective-permute-start(f32[88,32]{0,1:T(8,128)S(1)} %add.96), channel_id=1, source_target_pairs={{0,64},{1,65},{2,66},{3,67},{4,68},{5,69},{6,70},{7,71},{8,72},{9,... | collective-permute-start | bytes 33800 | tf_op jit(solution)/shard_map/ppermute | solution.py:41
  185.9 3.8 %collective-permute-done.23 = f32[88,32]{0,1:T(8,128)S(1)} collective-permute-done((f32[88,32]{0,1:T(8,128)S(1)}, f32[88,32]{0,1:T(8,128)S(1)}, u32[]{:S(2)}, u32[]{:S(2)}) %collective-permute-start.23) | collective-permute-done | bytes 11296 | tf_op jit(solution)/shard_map/ppermute | solution.py:41
  189.8 4.9 %collective-permute-start.24 = (f32[88,32]{0,1:T(8,128)S(1)}, f32[88,32]{0,1:T(8,128)S(1)}, u32[]{:S(2)}, u32[]{:S(2)}) collective-permute-start(f32[88,32]{0,1:T(8,128)S(1)} %add.97), channel_id=1, source_target_pairs={{0,512},{1,513},{2,514},{3,515},{4,516},{5,517},{6,518},{7,519},{8... | collective-permute-start | bytes 33800 | tf_op jit(solution)/shard_map/ppermute | solution.py:41
  194.7 3.7 %collective-permute-done.24 = f32[88,32]{0,1:T(8,128)S(1)} collective-permute-done((f32[88,32]{0,1:T(8,128)S(1)}, f32[88,32]{0,1:T(8,128)S(1)}, u32[]{:S(2)}, u32[]{:S(2)}) %collective-permute-start.24) | collective-permute-done | bytes 11296 | tf_op jit(solution)/shard_map/ppermute | solution.py:41
  200.4 2.6 %collective-permute-done.25 = f32[88,32]{0,1:T(8,128)S(1)} collective-permute-done((f32[88,32]{0,1:T(8,128)S(1)}, f32[88,32]{0,1:T(8,128)S(1)}, u32[]{:S(2)}, u32[]{:S(2)}) %collective-permute-start.25) | collective-permute-done | bytes 11296 | tf_op jit(solution)/shard_map/ppermute | solution.py:44
  203.0 1.9 collective-permute-start.26
  204.9 3.0 %collective-permute-done.26 = f32[176,32]{0,1:T(8,128)S(1)} collective-permute-done((f32[176,32]{0,1:T(8,128)S(1)}, f32[176,32]{0,1:T(8,128)S(1)}, u32[]{:S(2)}, u32[]{:S(2)}) %collective-permute-start.26) | collective-permute-done | bytes 22560 | tf_op jit(solution)/shard_map/ppermute | solution.py:44
  208.0 1.9 collective-permute-start.27
  210.0 2.9 %collective-permute-done.27 = f32[352,32]{0,1:T(8,128)S(1)} collective-permute-done((f32[352,32]{0,1:T(8,128)S(1)}, f32[352,32]{0,1:T(8,128)S(1)}, u32[]{:S(2)}, u32[]{:S(2)}) %collective-permute-start.27) | collective-permute-done | bytes 45088 | tf_op jit(solution)/shard_map/ppermute | solution.py:44
  213.0 15.0 %collective-permute-start.28 = (f32[704,32]{0,1:T(8,128)S(1)}, f32[704,32]{0,1:T(8,128)S(1)}, u32[]{:S(2)}, u32[]{:S(2)}) collective-permute-start(f32[704,32]{0,1:T(8,128)S(1)} %maximum_select_fusion.7), channel_id=1, source_target_pairs={{0,1},{1,0},{2,3},{3,2},{4,5},{5,4},{6,7},{7,6},{8,9},{9,8},{10,11... | collective-permute-start | bytes 270344 | tf_op jit(solution)/shard_map/ppermute | solution.py:44
  229.0 2.3 %fusion.7 = f32[352,1408]{1,0:T(8,128)} fusion(f32[1408,32]{0,1:T(8,128)S(1)} %fusion.6, f32[5632,32]{0,1:T(8,128)S(1)} %fusion, s32[]{:T(128)S(6)} %select_n.190), kind=kOutput, calls=%fused_computation.27 | convolution fusion | flops 95158272 | bytes 2211844 | tf_op jit(solution)/shard_map/dot_general | solution.py:74
  (69 shorter events, 36.5 us)
Async XLA Ops:
  0.6 1.6 copy-start
  4.3 17.4 %collective-permute-start = (f32[2816,32]{0,1:T(8,128)S(1)}, f32[2816,32]{0,1:T(8,128)}, u32[]{:S(2)}, u32[]{:S(2)}) collective-permute-start(f32[2816,32]{0,1:T(8,128)S(1)} %slice_select_fusion), channel_id=1, source_target_pairs={{0,1},{1,0},{2,3},{3,2},{4,5},{5,4},{6,7},{7,6},{8,9},{9,8},{10,11... | collective-permute-start | bytes 1081352 | tf_op jit(solution)/shard_map/ppermute | solution.py:38
  22.8 7.6 %collective-permute-start.1 = (f32[1408,32]{0,1:T(8,128)S(1)}, f32[1408,32]{0,1:T(8,128)S(1)}, u32[]{:S(2)}, u32[]{:S(2)}) collective-permute-start(f32[1408,32]{0,1:T(8,128)S(1)} %slice_select_fusion.1), channel_id=1, source_target_pairs={{0,2},{1,3},{2,0},{3,1},{4,6},{5,7},{6,4},{7,5},{8,10},{9,11},{10,... | collective-permute-start | bytes 540680 | tf_op jit(solution)/shard_map/ppermute | solution.py:38
  30.6 5.4 %collective-permute-start.2 = (f32[704,32]{0,1:T(8,128)S(1)}, f32[704,32]{0,1:T(8,128)S(1)}, u32[]{:S(2)}, u32[]{:S(2)}) collective-permute-start(f32[704,32]{0,1:T(8,128)S(1)} %slice_select_fusion.3), channel_id=1, source_target_pairs={{0,16},{1,17},{2,18},{3,19},{4,20},{5,21},{6,22},{7,23},{8,24},{9,... | collective-permute-start | bytes 270344 | tf_op jit(solution)/shard_map/ppermute | solution.py:38
  36.1 4.8 %collective-permute-start.3 = (f32[352,32]{0,1:T(8,128)S(1)}, f32[352,32]{0,1:T(8,128)S(1)}, u32[]{:S(2)}, u32[]{:S(2)}) collective-permute-start(f32[352,32]{0,1:T(8,128)S(1)} %slice_select_fusion.5), channel_id=1, source_target_pairs={{0,128},{1,129},{2,130},{3,131},{4,132},{5,133},{6,134},{7,135},{8... | collective-permute-start | bytes 135176 | tf_op jit(solution)/shard_map/ppermute | solution.py:38
  41.1 5.9 %collective-permute-start.4 = (f32[176,32]{0,1:T(8,128)S(1)}, f32[176,32]{0,1:T(8,128)S(1)}, u32[]{:S(2)}, u32[]{:S(2)}) collective-permute-start(f32[176,32]{0,1:T(8,128)S(1)} %slice_select_fusion.7), channel_id=1, source_target_pairs={{0,4},{1,5},{2,6},{3,7},{4,0},{5,1},{6,2},{7,3},{8,12},{9,13},{10,... | collective-permute-start | bytes 67592 | tf_op jit(solution)/shard_map/ppermute | solution.py:38
  47.1 5.6 %collective-permute-start.5 = (f32[176,32]{0,1:T(8,128)S(1)}, f32[176,32]{0,1:T(8,128)S(1)}, u32[]{:S(2)}, u32[]{:S(2)}) collective-permute-start(f32[176,32]{0,1:T(8,128)S(1)} %select_add_fusion.7), channel_id=1, source_target_pairs={{0,32},{1,33},{2,34},{3,35},{4,36},{5,37},{6,38},{7,39},{8,40},{9,... | collective-permute-start | bytes 67592 | tf_op jit(solution)/shard_map/ppermute | solution.py:41
  52.7 5.6 %collective-permute-start.6 = (f32[176,32]{0,1:T(8,128)S(1)}, f32[176,32]{0,1:T(8,128)S(1)}, u32[]{:S(2)}, u32[]{:S(2)}) collective-permute-start(f32[176,32]{0,1:T(8,128)S(1)} %add.82), channel_id=1, source_target_pairs={{0,256},{1,257},{2,258},{3,259},{4,260},{5,261},{6,262},{7,263},{8... | collective-permute-start | bytes 67592 | tf_op jit(solution)/shard_map/ppermute | solution.py:41
  58.4 8.6 %collective-permute-start.7 = (f32[176,32]{0,1:T(8,128)S(1)}, f32[176,32]{0,1:T(8,128)S(1)}, u32[]{:S(2)}, u32[]{:S(2)}) collective-permute-start(f32[176,32]{0,1:T(8,128)S(1)} %add.83), channel_id=1, source_target_pairs={{0,8},{1,9},{2,10},{3,11},{4,12},{5,13},{6,14},{7,15},{8,0},{9,1},... | collective-permute-start | bytes 67592 | tf_op jit(solution)/shard_map/ppermute | solution.py:41
  66.9 8.6 %collective-permute-start.8 = (f32[176,32]{0,1:T(8,128)S(1)}, f32[176,32]{0,1:T(8,128)S(1)}, u32[]{:S(2)}, u32[]{:S(2)}) collective-permute-start(f32[176,32]{0,1:T(8,128)S(1)} %add.84), channel_id=1, source_target_pairs={{0,64},{1,65},{2,66},{3,67},{4,68},{5,69},{6,70},{7,71},{8,72},{9,... | collective-permute-start | bytes 67592 | tf_op jit(solution)/shard_map/ppermute | solution.py:41
  75.5 8.6 %collective-permute-start.9 = (f32[176,32]{0,1:T(8,128)S(1)}, f32[176,32]{0,1:T(8,128)S(1)}, u32[]{:S(2)}, u32[]{:S(2)}) collective-permute-start(f32[176,32]{0,1:T(8,128)S(1)} %add.85), channel_id=1, source_target_pairs={{0,512},{1,513},{2,514},{3,515},{4,516},{5,517},{6,518},{7,519},{8... | collective-permute-start | bytes 67592 | tf_op jit(solution)/shard_map/ppermute | solution.py:41
  84.0 5.8 %collective-permute-start.10 = (f32[176,32]{0,1:T(8,128)S(1)}, f32[176,32]{0,1:T(8,128)S(1)}, u32[]{:S(2)}, u32[]{:S(2)}) collective-permute-start(f32[176,32]{0,1:T(8,128)S(1)} %add.86), channel_id=1, source_target_pairs={{0,4},{1,5},{2,6},{3,7},{4,0},{5,1},{6,2},{7,3},{8,12},{9,13},{10,... | collective-permute-start | bytes 67592 | tf_op jit(solution)/shard_map/ppermute | solution.py:44
  89.9 4.8 %collective-permute-start.11 = (f32[352,32]{0,1:T(8,128)S(1)}, f32[352,32]{0,1:T(8,128)S(1)}, u32[]{:S(2)}, u32[]{:S(2)}) collective-permute-start(f32[352,32]{0,1:T(8,128)S(1)} %maximum_select_fusion.8), channel_id=1, source_target_pairs={{0,128},{1,129},{2,130},{3,131},{4,132},{5,133},{6,134},{7,135},{8... | collective-permute-start | bytes 135176 | tf_op jit(solution)/shard_map/ppermute | solution.py:44
  94.9 40.0 %copy-start.1 = (bf16[192,1408]{1,0:T(8,128)(2,1)S(1)}, bf16[192,1408]{1,0:T(8,128)(2,1)}, u32[]{:S(2)}) copy-start(bf16[192,1408]{1,0:T(8,128)(2,1)} %param.4) | copy-start | bytes 1622020
  94.9 5.8 %collective-permute-start.12 = (f32[704,32]{0,1:T(8,128)S(1)}, f32[704,32]{0,1:T(8,128)S(1)}, u32[]{:S(2)}, u32[]{:S(2)}) collective-permute-start(f32[704,32]{0,1:T(8,128)S(1)} %maximum_select_fusion.6), channel_id=1, source_target_pairs={{0,16},{1,17},{2,18},{3,19},{4,20},{5,21},{6,22},{7,23},{8,24},{9,... | collective-permute-start | bytes 270344 | tf_op jit(solution)/shard_map/ppermute | solution.py:44
  100.8 6.2 %collective-permute-start.13 = (f32[1408,32]{0,1:T(8,128)S(1)}, f32[1408,32]{0,1:T(8,128)S(1)}, u32[]{:S(2)}, u32[]{:S(2)}) collective-permute-start(f32[1408,32]{0,1:T(8,128)S(1)} %maximum_select_fusion.4), channel_id=1, source_target_pairs={{0,2},{1,3},{2,0},{3,1},{4,6},{5,7},{6,4},{7,5},{8,10},{9,11},{10,... | collective-permute-start | bytes 540680 | tf_op jit(solution)/shard_map/ppermute | solution.py:44
  107.1 17.6 %copy-start.2 = (f32[2816,32]{0,1:T(8,128)}, f32[2816,32]{0,1:T(8,128)S(1)}, u32[]{:S(2)}) copy-start(f32[2816,32]{0,1:T(8,128)S(1)} %maximum_select_fusion.3) | copy-start | bytes 1081348
  107.1 17.6 %collective-permute-start.14 = (f32[2816,32]{0,1:T(8,128)S(1)}, f32[2816,32]{0,1:T(8,128)S(1)}, u32[]{:S(2)}, u32[]{:S(2)}) collective-permute-start(f32[2816,32]{0,1:T(8,128)S(1)} %maximum_select_fusion.3), channel_id=1, source_target_pairs={{0,1},{1,0},{2,3},{3,2},{4,5},{5,4},{6,7},{7,6},{8,9},{9,8},{10,11... | collective-permute-start | bytes 1081352 | tf_op jit(solution)/shard_map/ppermute | solution.py:44
  124.7 0.8 copy-start.4
  137.7 3.2 %collective-permute-start.15 = (f32[704,32]{0,1:T(8,128)S(1)}, f32[704,32]{0,1:T(8,128)S(1)}, u32[]{:S(2)}, u32[]{:S(2)}) collective-permute-start(f32[704,32]{0,1:T(8,128)S(1)} %slice_select_fusion.2), channel_id=1, source_target_pairs={{0,1},{1,0},{2,3},{3,2},{4,5},{5,4},{6,7},{7,6},{8,9},{9,8},{10,11... | collective-permute-start | bytes 270344 | tf_op jit(solution)/shard_map/ppermute | solution.py:38
  142.0 4.8 %collective-permute-start.16 = (f32[352,32]{0,1:T(8,128)S(1)}, f32[352,32]{0,1:T(8,128)S(1)}, u32[]{:S(2)}, u32[]{:S(2)}) collective-permute-start(f32[352,32]{0,1:T(8,128)S(1)} %slice_select_fusion.4), channel_id=1, source_target_pairs={{0,2},{1,3},{2,0},{3,1},{4,6},{5,7},{6,4},{7,5},{8,10},{9,11},{10,... | collective-permute-start | bytes 135176 | tf_op jit(solution)/shard_map/ppermute | solution.py:38
  147.0 4.7 %collective-permute-start.17 = (f32[176,32]{0,1:T(8,128)S(1)}, f32[176,32]{0,1:T(8,128)S(1)}, u32[]{:S(2)}, u32[]{:S(2)}) collective-permute-start(f32[176,32]{0,1:T(8,128)S(1)} %slice_select_fusion.6), channel_id=1, source_target_pairs={{0,16},{1,17},{2,18},{3,19},{4,20},{5,21},{6,22},{7,23},{8,24},{9,... | collective-permute-start | bytes 67592 | tf_op jit(solution)/shard_map/ppermute | solution.py:38
  151.8 4.5 %collective-permute-start.18 = (f32[88,32]{0,1:T(8,128)S(1)}, f32[88,32]{0,1:T(8,128)S(1)}, u32[]{:S(2)}, u32[]{:S(2)}) collective-permute-start(f32[88,32]{0,1:T(8,128)S(1)} %slice_select_fusion.8), channel_id=1, source_target_pairs={{0,128},{1,129},{2,130},{3,131},{4,132},{5,133},{6,134},{7,135},{8... | collective-permute-start | bytes 33800 | tf_op jit(solution)/shard_map/ppermute | solution.py:38
  156.4 5.4 %collective-permute-start.19 = (f32[88,32]{0,1:T(8,128)S(1)}, f32[88,32]{0,1:T(8,128)S(1)}, u32[]{:S(2)}, u32[]{:S(2)}) collective-permute-start(f32[88,32]{0,1:T(8,128)S(1)} %select_add_fusion.8), channel_id=1, source_target_pairs={{0,4},{1,5},{2,6},{3,7},{4,0},{5,1},{6,2},{7,3},{8,12},{9,13},{10,... | collective-permute-start | bytes 33800 | tf_op jit(solution)/shard_map/ppermute | solution.py:41
  161.8 5.4 %collective-permute-start.20 = (f32[88,32]{0,1:T(8,128)S(1)}, f32[88,32]{0,1:T(8,128)S(1)}, u32[]{:S(2)}, u32[]{:S(2)}) collective-permute-start(f32[88,32]{0,1:T(8,128)S(1)} %add.93), channel_id=1, source_target_pairs={{0,32},{1,33},{2,34},{3,35},{4,36},{5,37},{6,38},{7,39},{8,40},{9,... | collective-permute-start | bytes 33800 | tf_op jit(solution)/shard_map/ppermute | solution.py:41
  167.1 5.7 %collective-permute-start.21 = (f32[88,32]{0,1:T(8,128)S(1)}, f32[88,32]{0,1:T(8,128)S(1)}, u32[]{:S(2)}, u32[]{:S(2)}) collective-permute-start(f32[88,32]{0,1:T(8,128)S(1)} %add.94), channel_id=1, source_target_pairs={{0,256},{1,257},{2,258},{3,259},{4,260},{5,261},{6,262},{7,263},{8... | collective-permute-start | bytes 33800 | tf_op jit(solution)/shard_map/ppermute | solution.py:41
  172.8 8.6 %collective-permute-start.22 = (f32[88,32]{0,1:T(8,128)S(1)}, f32[88,32]{0,1:T(8,128)S(1)}, u32[]{:S(2)}, u32[]{:S(2)}) collective-permute-start(f32[88,32]{0,1:T(8,128)S(1)} %add.95), channel_id=1, source_target_pairs={{0,8},{1,9},{2,10},{3,11},{4,12},{5,13},{6,14},{7,15},{8,0},{9,1},... | collective-permute-start | bytes 33800 | tf_op jit(solution)/shard_map/ppermute | solution.py:41
  181.4 8.4 %collective-permute-start.23 = (f32[88,32]{0,1:T(8,128)S(1)}, f32[88,32]{0,1:T(8,128)S(1)}, u32[]{:S(2)}, u32[]{:S(2)}) collective-permute-start(f32[88,32]{0,1:T(8,128)S(1)} %add.96), channel_id=1, source_target_pairs={{0,64},{1,65},{2,66},{3,67},{4,68},{5,69},{6,70},{7,71},{8,72},{9,... | collective-permute-start | bytes 33800 | tf_op jit(solution)/shard_map/ppermute | solution.py:41
  189.8 8.7 %collective-permute-start.24 = (f32[88,32]{0,1:T(8,128)S(1)}, f32[88,32]{0,1:T(8,128)S(1)}, u32[]{:S(2)}, u32[]{:S(2)}) collective-permute-start(f32[88,32]{0,1:T(8,128)S(1)} %add.97), channel_id=1, source_target_pairs={{0,512},{1,513},{2,514},{3,515},{4,516},{5,517},{6,518},{7,519},{8... | collective-permute-start | bytes 33800 | tf_op jit(solution)/shard_map/ppermute | solution.py:41
  198.4 4.5 %collective-permute-start.25 = (f32[88,32]{0,1:T(8,128)S(1)}, f32[88,32]{0,1:T(8,128)S(1)}, u32[]{:S(2)}, u32[]{:S(2)}) collective-permute-start(f32[88,32]{0,1:T(8,128)S(1)} %add.98), channel_id=1, source_target_pairs={{0,128},{1,129},{2,130},{3,131},{4,132},{5,133},{6,134},{7,135},{8... | collective-permute-start | bytes 33800 | tf_op jit(solution)/shard_map/ppermute | solution.py:44
  203.0 5.0 %collective-permute-start.26 = (f32[176,32]{0,1:T(8,128)S(1)}, f32[176,32]{0,1:T(8,128)S(1)}, u32[]{:S(2)}, u32[]{:S(2)}) collective-permute-start(f32[176,32]{0,1:T(8,128)S(1)} %maximum_select_fusion.10), channel_id=1, source_target_pairs={{0,16},{1,17},{2,18},{3,19},{4,20},{5,21},{6,22},{7,23},{8,24},{9,... | collective-permute-start | bytes 67592 | tf_op jit(solution)/shard_map/ppermute | solution.py:44
  208.0 4.8 %collective-permute-start.27 = (f32[352,32]{0,1:T(8,128)S(1)}, f32[352,32]{0,1:T(8,128)S(1)}, u32[]{:S(2)}, u32[]{:S(2)}) collective-permute-start(f32[352,32]{0,1:T(8,128)S(1)} %maximum_select_fusion.9), channel_id=1, source_target_pairs={{0,2},{1,3},{2,0},{3,1},{4,6},{5,7},{6,4},{7,5},{8,10},{9,11},{10,... | collective-permute-start | bytes 135176 | tf_op jit(solution)/shard_map/ppermute | solution.py:44
  213.0 15.9 %collective-permute-start.28 = (f32[704,32]{0,1:T(8,128)S(1)}, f32[704,32]{0,1:T(8,128)S(1)}, u32[]{:S(2)}, u32[]{:S(2)}) collective-permute-start(f32[704,32]{0,1:T(8,128)S(1)} %maximum_select_fusion.7), channel_id=1, source_target_pairs={{0,1},{1,0},{2,3},{3,2},{4,5},{5,4},{6,7},{7,6},{8,9},{9,8},{10,11... | collective-permute-start | bytes 270344 | tf_op jit(solution)/shard_map/ppermute | solution.py:44
  229.0 2.4 %copy-start.3 = (f32[1408,32]{0,1:T(8,128)}, f32[1408,32]{0,1:T(8,128)S(1)}, u32[]{:S(2)}) copy-start(f32[1408,32]{0,1:T(8,128)S(1)} %fusion.6) | copy-start | bytes 540676

commit v6 on v2

--- a/solution.py
+++ b/solution.py
@@ -62,7 +62,7 @@
         p_local = jnp.einsum("tf,tr->fr", activations, u_low, preferred_element_type=jnp.float32)
         hidden = activations.shape[1]
         block_rows = hidden // n_sub
-        p_sum = butterfly_sum(p_local, order, n, 5)
+        p_sum = butterfly_sum(p_local, order, n, 4)
         gram = jnp.dot(p_sum.T, p_sum, precision=lax.Precision.HIGH)
         p_hat = orthonormal(p_sum, gram)
         p_low = p_hat.astype(jnp.bfloat16)

time: 228 us -> 222 us (0.974)
  waiting for transfers between devices: 95.4 us -> 91.1 us
    ppermute x8 -> x7, waiting for transfers between devices: 22.6 us -> 18 us  [butterfly_sum(): other = lax.ppermute(x, AXES, xor_pairs(n, bit))]
    ppermute x12 -> x13, waiting for transfers between devices: 48.9 us -> 53.1 us  [butterfly_sum(): x = x + lax.ppermute(x, AXES, xor_pairs(n, bit))]
    ppermute x8 -> x7, waiting for transfers between devices: 24 us -> 20 us  [butterfly_sum(): x = keep + lax.ppermute(send, AXES, xor_pairs(n, bit))]
    ppermute x12 -> x13, starting transfers between devices: 35.5 us -> 38.8 us  [butterfly_sum(): x = x + lax.ppermute(x, AXES, xor_pairs(n, bit))]
    ppermute x8 -> x7, starting transfers between devices: 42.3 us -> 40.1 us  [butterfly_sum(): other = lax.ppermute(x, AXES, xor_pairs(n, bit))]
    ppermute x8 -> x7, starting transfers between devices: 29.8 us -> 27.9 us  [butterfly_sum(): x = keep + lax.ppermute(send, AXES, xor_pairs(n, bit))]
  transfers between devices with their start and end apart: 28 -> 27, of which waited for: 28 -> 27; matrix products, arithmetic and copies ran while one was open for 0% -> 0% of each run, Pallas kernels for 0% -> 0%
where the time goes in v6:
time: 222 us; the launch traced here: 221 us
  starting transfers between devices  107 us (48%)
  waiting for transfers between devices  91.1 us (41%)
  other arithmetic  11.2 us (5%)
  matrix products  8.73 us (4%)
  local copies, waits for them, and re-layouts  2.42 us (1%)
    ppermute x13, waiting for transfers between devices, butterfly_sum(): x = x + lax.ppermute(x, AXES, xor_pairs(n, bit))  53.1 us
    ppermute x7, starting transfers between devices, butterfly_sum(): other = lax.ppermute(x, AXES, xor_pairs(n, bit))  40.1 us
    ppermute x13, starting transfers between devices, butterfly_sum(): x = x + lax.ppermute(x, AXES, xor_pairs(n, bit))  38.8 us
    ppermute x7, starting transfers between devices, butterfly_sum(): x = keep + lax.ppermute(send, AXES, xor_pairs(n, bit))  27.9 us
    ppermute x7, waiting for transfers between devices, butterfly_sum(): x = keep + lax.ppermute(send, AXES, xor_pairs(n, bit))  20 us
    ppermute x7, waiting for transfers between devices, butterfly_sum(): other = lax.ppermute(x, AXES, xor_pairs(n, bit))  18 us
  transfers between devices with their start and end apart: 27, of which 27 were waited for; matrix products, arithmetic and copies ran while one was open for 0% of the time, Pallas kernels for 0%

profile of v6, /device:TPU:1, one launch (start us, length us, event | category | flops | bytes accessed | tf_op | source)
XLA Modules:
  0.0 221.3 jit_solution(742457507950410347)
XLA Ops:
  2.2 2.0 convolution_bitcast_fusion
  4.3 16.0 %collective-permute-start = (f32[2816,32]{0,1:T(8,128)S(1)}, f32[2816,32]{0,1:T(8,128)}, u32[]{:S(2)}, u32[]{:S(2)}) collective-permute-start(f32[2816,32]{0,1:T(8,128)S(1)} %slice_select_fusion), channel_id=1, source_target_pairs={{0,1},{1,0},{2,3},{3,2},{4,5},{5,4},{6,7},{7,6},{8,9},{9,8},{10,11... | collective-permute-start | bytes 1081352 | tf_op jit(solution)/shard_map/ppermute | solution.py:38
  22.8 1.9 collective-permute-start.1
  24.8 5.7 %collective-permute-done.1 = f32[1408,32]{0,1:T(8,128)S(1)} collective-permute-done((f32[1408,32]{0,1:T(8,128)S(1)}, f32[1408,32]{0,1:T(8,128)S(1)}, u32[]{:S(2)}, u32[]{:S(2)}) %collective-permute-start.1) | collective-permute-done | bytes 180256 | tf_op jit(solution)/shard_map/ppermute | solution.py:38
  30.6 1.9 collective-permute-start.2
  32.5 3.4 %collective-permute-done.2 = f32[704,32]{0,1:T(8,128)S(1)} collective-permute-done((f32[704,32]{0,1:T(8,128)S(1)}, f32[704,32]{0,1:T(8,128)S(1)}, u32[]{:S(2)}, u32[]{:S(2)}) %collective-permute-start.2) | collective-permute-done | bytes 90144 | tf_op jit(solution)/shard_map/ppermute | solution.py:38
  36.1 1.9 collective-permute-start.3
  38.0 2.9 %collective-permute-done.3 = f32[352,32]{0,1:T(8,128)S(1)} collective-permute-done((f32[352,32]{0,1:T(8,128)S(1)}, f32[352,32]{0,1:T(8,128)S(1)}, u32[]{:S(2)}, u32[]{:S(2)}) %collective-permute-start.3) | collective-permute-done | bytes 45088 | tf_op jit(solution)/shard_map/ppermute | solution.py:38
  41.0 1.9 collective-permute-start.4
  43.0 4.3 %collective-permute-done.4 = f32[352,32]{0,1:T(8,128)S(1)} collective-permute-done((f32[352,32]{0,1:T(8,128)S(1)}, f32[352,32]{0,1:T(8,128)S(1)}, u32[]{:S(2)}, u32[]{:S(2)}) %collective-permute-start.4) | collective-permute-done | bytes 45088 | tf_op jit(solution)/shard_map/ppermute | solution.py:41
  47.3 1.9 collective-permute-start.5
  49.2 4.1 %collective-permute-done.5 = f32[352,32]{0,1:T(8,128)S(1)} collective-permute-done((f32[352,32]{0,1:T(8,128)S(1)}, f32[352,32]{0,1:T(8,128)S(1)}, u32[]{:S(2)}, u32[]{:S(2)}) %collective-permute-start.5) | collective-permute-done | bytes 45088 | tf_op jit(solution)/shard_map/ppermute | solution.py:41
  53.3 1.9 collective-permute-start.6
  55.2 4.1 %collective-permute-done.6 = f32[352,32]{0,1:T(8,128)S(1)} collective-permute-done((f32[352,32]{0,1:T(8,128)S(1)}, f32[352,32]{0,1:T(8,128)S(1)}, u32[]{:S(2)}, u32[]{:S(2)}) %collective-permute-start.6) | collective-permute-done | bytes 45088 | tf_op jit(solution)/shard_map/ppermute | solution.py:41
  59.3 1.9 collective-permute-start.7
  61.2 6.8 %collective-permute-done.7 = f32[352,32]{0,1:T(8,128)S(1)} collective-permute-done((f32[352,32]{0,1:T(8,128)S(1)}, f32[352,32]{0,1:T(8,128)S(1)}, u32[]{:S(2)}, u32[]{:S(2)}) %collective-permute-start.7) | collective-permute-done | bytes 45088 | tf_op jit(solution)/shard_map/ppermute | solution.py:41
  68.1 3.5 %collective-permute-start.8 = (f32[352,32]{0,1:T(8,128)S(1)}, f32[352,32]{0,1:T(8,128)S(1)}, u32[]{:S(2)}, u32[]{:S(2)}) collective-permute-start(f32[352,32]{0,1:T(8,128)S(1)} %add.84), channel_id=1, source_target_pairs={{0,64},{1,65},{2,66},{3,67},{4,68},{5,69},{6,70},{7,71},{8,72},{9,... | collective-permute-start | bytes 135176 | tf_op jit(solution)/shard_map/ppermute | solution.py:41
  71.6 5.2 %collective-permute-done.8 = f32[352,32]{0,1:T(8,128)S(1)} collective-permute-done((f32[352,32]{0,1:T(8,128)S(1)}, f32[352,32]{0,1:T(8,128)S(1)}, u32[]{:S(2)}, u32[]{:S(2)}) %collective-permute-start.8) | collective-permute-done | bytes 45088 | tf_op jit(solution)/shard_map/ppermute | solution.py:41
  76.8 4.5 %collective-permute-start.9 = (f32[352,32]{0,1:T(8,128)S(1)}, f32[352,32]{0,1:T(8,128)S(1)}, u32[]{:S(2)}, u32[]{:S(2)}) collective-permute-start(f32[352,32]{0,1:T(8,128)S(1)} %add.85), channel_id=1, source_target_pairs={{0,512},{1,513},{2,514},{3,515},{4,516},{5,517},{6,518},{7,519},{8... | collective-permute-start | bytes 135176 | tf_op jit(solution)/shard_map/ppermute | solution.py:41
  81.3 4.3 %collective-permute-done.9 = f32[352,32]{0,1:T(8,128)S(1)} collective-permute-done((f32[352,32]{0,1:T(8,128)S(1)}, f32[352,32]{0,1:T(8,128)S(1)}, u32[]{:S(2)}, u32[]{:S(2)}) %collective-permute-start.9) | collective-permute-done | bytes 45088 | tf_op jit(solution)/shard_map/ppermute | solution.py:41
  85.6 2.2 collective-permute-start.10
  87.8 2.6 %collective-permute-done.10 = f32[352,32]{0,1:T(8,128)S(1)} collective-permute-done((f32[352,32]{0,1:T(8,128)S(1)}, f32[352,32]{0,1:T(8,128)S(1)}, u32[]{:S(2)}, u32[]{:S(2)}) %collective-permute-start.10) | collective-permute-done | bytes 45088 | tf_op jit(solution)/shard_map/ppermute | solution.py:44
  90.5 2.4 %collective-permute-start.11 = (f32[704,32]{0,1:T(8,128)S(1)}, f32[704,32]{0,1:T(8,128)S(1)}, u32[]{:S(2)}, u32[]{:S(2)}) collective-permute-start(f32[704,32]{0,1:T(8,128)S(1)} %maximum_select_fusion.6), channel_id=1, source_target_pairs={{0,16},{1,17},{2,18},{3,19},{4,20},{5,21},{6,22},{7,23},{8,24},{9,... | collective-permute-start | bytes 270344 | tf_op jit(solution)/shard_map/ppermute | solution.py:44
  93.0 3.0 %collective-permute-done.11 = f32[704,32]{0,1:T(8,128)S(1)} collective-permute-done((f32[704,32]{0,1:T(8,128)S(1)}, f32[704,32]{0,1:T(8,128)S(1)}, u32[]{:S(2)}, u32[]{:S(2)}) %collective-permute-start.11) | collective-permute-done | bytes 90144 | tf_op jit(solution)/shard_map/ppermute | solution.py:44
  96.1 1.9 collective-permute-start.12
  98.1 4.3 %collective-permute-done.12 = f32[1408,32]{0,1:T(8,128)S(1)} collective-permute-done((f32[1408,32]{0,1:T(8,128)S(1)}, f32[1408,32]{0,1:T(8,128)S(1)}, u32[]{:S(2)}, u32[]{:S(2)}) %collective-permute-start.12) | collective-permute-done | bytes 180256 | tf_op jit(solution)/shard_map/ppermute | solution.py:44
  102.4 15.5 %collective-permute-start.13 = (f32[2816,32]{0,1:T(8,128)S(1)}, f32[2816,32]{0,1:T(8,128)S(1)}, u32[]{:S(2)}, u32[]{:S(2)}) collective-permute-start(f32[2816,32]{0,1:T(8,128)S(1)} %maximum_select_fusion.3), channel_id=1, source_target_pairs={{0,1},{1,0},{2,3},{3,2},{4,5},{5,4},{6,7},{7,6},{8,9},{9,8},{10,11... | collective-permute-start | bytes 1081352 | tf_op jit(solution)/shard_map/ppermute | solution.py:44
  120.5 2.9 %cholesky.16 = f32[32,32]{1,0:T(8,128)S(1)} custom-call(f32[32,32]{1,0:T(8,128)S(1)} %fusion.11), custom_call_target="Cholesky" | custom-call | tf_op jit(solution)/shard_map/cholesky | solution.py:50
  124.7 2.4 %custom-call.5 = f32[1,32,32]{1,2,0:T(8,128)S(1)} custom-call(f32[1,32,32]{2,1,0:T(8,128)S(1)} %fusion.9), custom_call_target="InvertDiagBlocksLowerTriangular" | custom-call | tf_op jit(solution)/shard_map/triangular_solve | solution.py:51
  127.2 2.2 fusion
  132.2 2.3 %collective-permute-start.14 = (f32[704,32]{0,1:T(8,128)S(1)}, f32[704,32]{0,1:T(8,128)S(1)}, u32[]{:S(2)}, u32[]{:S(2)}) collective-permute-start(f32[704,32]{0,1:T(8,128)S(1)} %slice_select_fusion.2), channel_id=1, source_target_pairs={{0,1},{1,0},{2,3},{3,2},{4,5},{5,4},{6,7},{7,6},{8,9},{9,8},{10,11... | collective-permute-start | bytes 270344 | tf_op jit(solution)/shard_map/ppermute | solution.py:38
  138.5 2.9 %collective-permute-done.15 = f32[352,32]{0,1:T(8,128)S(1)} collective-permute-done((f32[352,32]{0,1:T(8,128)S(1)}, f32[352,32]{0,1:T(8,128)S(1)}, u32[]{:S(2)}, u32[]{:S(2)}) %collective-permute-start.15) | collective-permute-done | bytes 45088 | tf_op jit(solution)/shard_map/ppermute | solution.py:38
  143.5 2.7 %collective-permute-done.16 = f32[176,32]{0,1:T(8,128)S(1)} collective-permute-done((f32[176,32]{0,1:T(8,128)S(1)}, f32[176,32]{0,1:T(8,128)S(1)}, u32[]{:S(2)}, u32[]{:S(2)}) %collective-permute-start.16) | collective-permute-done | bytes 22560 | tf_op jit(solution)/shard_map/ppermute | solution.py:38
  148.2 2.7 %collective-permute-done.17 = f32[176,32]{0,1:T(8,128)S(1)} collective-permute-done((f32[176,32]{0,1:T(8,128)S(1)}, f32[176,32]{0,1:T(8,128)S(1)}, u32[]{:S(2)}, u32[]{:S(2)}) %collective-permute-start.17) | collective-permute-done | bytes 22560 | tf_op jit(solution)/shard_map/ppermute | solution.py:41
  152.9 3.7 %collective-permute-done.18 = f32[176,32]{0,1:T(8,128)S(1)} collective-permute-done((f32[176,32]{0,1:T(8,128)S(1)}, f32[176,32]{0,1:T(8,128)S(1)}, u32[]{:S(2)}, u32[]{:S(2)}) %collective-permute-start.18) | collective-permute-done | bytes 22560 | tf_op jit(solution)/shard_map/ppermute | solution.py:41
  158.5 3.7 %collective-permute-done.19 = f32[176,32]{0,1:T(8,128)S(1)} collective-permute-done((f32[176,32]{0,1:T(8,128)S(1)}, f32[176,32]{0,1:T(8,128)S(1)}, u32[]{:S(2)}, u32[]{:S(2)}) %collective-permute-start.19) | collective-permute-done | bytes 22560 | tf_op jit(solution)/shard_map/ppermute | solution.py:41
  164.1 3.7 %collective-permute-done.20 = f32[176,32]{0,1:T(8,128)S(1)} collective-permute-done((f32[176,32]{0,1:T(8,128)S(1)}, f32[176,32]{0,1:T(8,128)S(1)}, u32[]{:S(2)}, u32[]{:S(2)}) %collective-permute-start.20) | collective-permute-done | bytes 22560 | tf_op jit(solution)/shard_map/ppermute | solution.py:41
  167.8 4.7 %collective-permute-start.21 = (f32[176,32]{0,1:T(8,128)S(1)}, f32[176,32]{0,1:T(8,128)S(1)}, u32[]{:S(2)}, u32[]{:S(2)}) collective-permute-start(f32[176,32]{0,1:T(8,128)S(1)} %add.95), channel_id=1, source_target_pairs={{0,8},{1,9},{2,10},{3,11},{4,12},{5,13},{6,14},{7,15},{8,0},{9,1},... | collective-permute-start | bytes 67592 | tf_op jit(solution)/shard_map/ppermute | solution.py:41
  172.6 3.9 %collective-permute-done.21 = f32[176,32]{0,1:T(8,128)S(1)} collective-permute-done((f32[176,32]{0,1:T(8,128)S(1)}, f32[176,32]{0,1:T(8,128)S(1)}, u32[]{:S(2)}, u32[]{:S(2)}) %collective-permute-start.21) | collective-permute-done | bytes 22560 | tf_op jit(solution)/shard_map/ppermute | solution.py:41
  176.4 5.2 %collective-permute-start.22 = (f32[176,32]{0,1:T(8,128)S(1)}, f32[176,32]{0,1:T(8,128)S(1)}, u32[]{:S(2)}, u32[]{:S(2)}) collective-permute-start(f32[176,32]{0,1:T(8,128)S(1)} %add.96), channel_id=1, source_target_pairs={{0,64},{1,65},{2,66},{3,67},{4,68},{5,69},{6,70},{7,71},{8,72},{9,... | collective-permute-start | bytes 67592 | tf_op jit(solution)/shard_map/ppermute | solution.py:41
  181.6 3.4 %collective-permute-done.22 = f32[176,32]{0,1:T(8,128)S(1)} collective-permute-done((f32[176,32]{0,1:T(8,128)S(1)}, f32[176,32]{0,1:T(8,128)S(1)}, u32[]{:S(2)}, u32[]{:S(2)}) %collective-permute-start.22) | collective-permute-done | bytes 22560 | tf_op jit(solution)/shard_map/ppermute | solution.py:41
  185.0 5.6 %collective-permute-start.23 = (f32[176,32]{0,1:T(8,128)S(1)}, f32[176,32]{0,1:T(8,128)S(1)}, u32[]{:S(2)}, u32[]{:S(2)}) collective-permute-start(f32[176,32]{0,1:T(8,128)S(1)} %add.97), channel_id=1, source_target_pairs={{0,512},{1,513},{2,514},{3,515},{4,516},{5,517},{6,518},{7,519},{8... | collective-permute-start | bytes 67592 | tf_op jit(solution)/shard_map/ppermute | solution.py:41
  190.6 3.2 %collective-permute-done.23 = f32[176,32]{0,1:T(8,128)S(1)} collective-permute-done((f32[176,32]{0,1:T(8,128)S(1)}, f32[176,32]{0,1:T(8,128)S(1)}, u32[]{:S(2)}, u32[]{:S(2)}) %collective-permute-start.23) | collective-permute-done | bytes 22560 | tf_op jit(solution)/shard_map/ppermute | solution.py:41
  195.8 2.7 %collective-permute-done.24 = f32[176,32]{0,1:T(8,128)S(1)} collective-permute-done((f32[176,32]{0,1:T(8,128)S(1)}, f32[176,32]{0,1:T(8,128)S(1)}, u32[]{:S(2)}, u32[]{:S(2)}) %collective-permute-start.24) | collective-permute-done | bytes 22560 | tf_op jit(solution)/shard_map/ppermute | solution.py:44
  198.6 1.9 collective-permute-start.25
  200.5 3.1 %collective-permute-done.25 = f32[352,32]{0,1:T(8,128)S(1)} collective-permute-done((f32[352,32]{0,1:T(8,128)S(1)}, f32[352,32]{0,1:T(8,128)S(1)}, u32[]{:S(2)}, u32[]{:S(2)}) %collective-permute-start.25) | collective-permute-done | bytes 45088 | tf_op jit(solution)/shard_map/ppermute | solution.py:44
  203.7 14.2 %collective-permute-start.26 = (f32[704,32]{0,1:T(8,128)S(1)}, f32[704,32]{0,1:T(8,128)S(1)}, u32[]{:S(2)}, u32[]{:S(2)}) collective-permute-start(f32[704,32]{0,1:T(8,128)S(1)} %maximum_select_fusion.7), channel_id=1, source_target_pairs={{0,1},{1,0},{2,3},{3,2},{4,5},{5,4},{6,7},{7,6},{8,9},{9,8},{10,11... | collective-permute-start | bytes 270344 | tf_op jit(solution)/shard_map/ppermute | solution.py:44
  219.0 2.3 %fusion.7 = f32[352,1408]{1,0:T(8,128)} fusion(f32[1408,32]{0,1:T(8,128)S(1)} %fusion.6, f32[5632,32]{0,1:T(8,128)S(1)} %fusion, s32[]{:T(128)S(6)} %select_n.151), kind=kOutput, calls=%fused_computation.26 | convolution fusion | flops 95158272 | bytes 2211844 | tf_op jit(solution)/shard_map/dot_general | solution.py:74
  (61 shorter events, 28.4 us)
Async XLA Ops:
  0.6 1.6 copy-start
  4.3 17.4 %collective-permute-start = (f32[2816,32]{0,1:T(8,128)S(1)}, f32[2816,32]{0,1:T(8,128)}, u32[]{:S(2)}, u32[]{:S(2)}) collective-permute-start(f32[2816,32]{0,1:T(8,128)S(1)} %slice_select_fusion), channel_id=1, source_target_pairs={{0,1},{1,0},{2,3},{3,2},{4,5},{5,4},{6,7},{7,6},{8,9},{9,8},{10,11... | collective-permute-start | bytes 1081352 | tf_op jit(solution)/shard_map/ppermute | solution.py:38
  22.8 7.6 %collective-permute-start.1 = (f32[1408,32]{0,1:T(8,128)S(1)}, f32[1408,32]{0,1:T(8,128)S(1)}, u32[]{:S(2)}, u32[]{:S(2)}) collective-permute-start(f32[1408,32]{0,1:T(8,128)S(1)} %slice_select_fusion.1), channel_id=1, source_target_pairs={{0,2},{1,3},{2,0},{3,1},{4,6},{5,7},{6,4},{7,5},{8,10},{9,11},{10,... | collective-permute-start | bytes 540680 | tf_op jit(solution)/shard_map/ppermute | solution.py:38
  30.6 5.4 %collective-permute-start.2 = (f32[704,32]{0,1:T(8,128)S(1)}, f32[704,32]{0,1:T(8,128)S(1)}, u32[]{:S(2)}, u32[]{:S(2)}) collective-permute-start(f32[704,32]{0,1:T(8,128)S(1)} %slice_select_fusion.3), channel_id=1, source_target_pairs={{0,16},{1,17},{2,18},{3,19},{4,20},{5,21},{6,22},{7,23},{8,24},{9,... | collective-permute-start | bytes 270344 | tf_op jit(solution)/shard_map/ppermute | solution.py:38
  36.1 4.8 %collective-permute-start.3 = (f32[352,32]{0,1:T(8,128)S(1)}, f32[352,32]{0,1:T(8,128)S(1)}, u32[]{:S(2)}, u32[]{:S(2)}) collective-permute-start(f32[352,32]{0,1:T(8,128)S(1)} %slice_select_fusion.5), channel_id=1, source_target_pairs={{0,128},{1,129},{2,130},{3,131},{4,132},{5,133},{6,134},{7,135},{8... | collective-permute-start | bytes 135176 | tf_op jit(solution)/shard_map/ppermute | solution.py:38
  41.0 6.3 %collective-permute-start.4 = (f32[352,32]{0,1:T(8,128)S(1)}, f32[352,32]{0,1:T(8,128)S(1)}, u32[]{:S(2)}, u32[]{:S(2)}) collective-permute-start(f32[352,32]{0,1:T(8,128)S(1)} %select_add_fusion.5), channel_id=1, source_target_pairs={{0,4},{1,5},{2,6},{3,7},{4,0},{5,1},{6,2},{7,3},{8,12},{9,13},{10,... | collective-permute-start | bytes 135176 | tf_op jit(solution)/shard_map/ppermute | solution.py:41
  47.3 6.0 %collective-permute-start.5 = (f32[352,32]{0,1:T(8,128)S(1)}, f32[352,32]{0,1:T(8,128)S(1)}, u32[]{:S(2)}, u32[]{:S(2)}) collective-permute-start(f32[352,32]{0,1:T(8,128)S(1)} %add.81), channel_id=1, source_target_pairs={{0,32},{1,33},{2,34},{3,35},{4,36},{5,37},{6,38},{7,39},{8,40},{9,... | collective-permute-start | bytes 135176 | tf_op jit(solution)/shard_map/ppermute | solution.py:41
  53.3 6.0 %collective-permute-start.6 = (f32[352,32]{0,1:T(8,128)S(1)}, f32[352,32]{0,1:T(8,128)S(1)}, u32[]{:S(2)}, u32[]{:S(2)}) collective-permute-start(f32[352,32]{0,1:T(8,128)S(1)} %add.82), channel_id=1, source_target_pairs={{0,256},{1,257},{2,258},{3,259},{4,260},{5,261},{6,262},{7,263},{8... | collective-permute-start | bytes 135176 | tf_op jit(solution)/shard_map/ppermute | solution.py:41
  59.3 8.7 %collective-permute-start.7 = (f32[352,32]{0,1:T(8,128)S(1)}, f32[352,32]{0,1:T(8,128)S(1)}, u32[]{:S(2)}, u32[]{:S(2)}) collective-permute-start(f32[352,32]{0,1:T(8,128)S(1)} %add.83), channel_id=1, source_target_pairs={{0,8},{1,9},{2,10},{3,11},{4,12},{5,13},{6,14},{7,15},{8,0},{9,1},... | collective-permute-start | bytes 135176 | tf_op jit(solution)/shard_map/ppermute | solution.py:41
  68.1 8.7 %collective-permute-start.8 = (f32[352,32]{0,1:T(8,128)S(1)}, f32[352,32]{0,1:T(8,128)S(1)}, u32[]{:S(2)}, u32[]{:S(2)}) collective-permute-start(f32[352,32]{0,1:T(8,128)S(1)} %add.84), channel_id=1, source_target_pairs={{0,64},{1,65},{2,66},{3,67},{4,68},{5,69},{6,70},{7,71},{8,72},{9,... | collective-permute-start | bytes 135176 | tf_op jit(solution)/shard_map/ppermute | solution.py:41
  76.8 8.8 %collective-permute-start.9 = (f32[352,32]{0,1:T(8,128)S(1)}, f32[352,32]{0,1:T(8,128)S(1)}, u32[]{:S(2)}, u32[]{:S(2)}) collective-permute-start(f32[352,32]{0,1:T(8,128)S(1)} %add.85), channel_id=1, source_target_pairs={{0,512},{1,513},{2,514},{3,515},{4,516},{5,517},{6,518},{7,519},{8... | collective-permute-start | bytes 135176 | tf_op jit(solution)/shard_map/ppermute | solution.py:41
  85.6 4.8 %collective-permute-start.10 = (f32[352,32]{0,1:T(8,128)S(1)}, f32[352,32]{0,1:T(8,128)S(1)}, u32[]{:S(2)}, u32[]{:S(2)}) collective-permute-start(f32[352,32]{0,1:T(8,128)S(1)} %add.86), channel_id=1, source_target_pairs={{0,128},{1,129},{2,130},{3,131},{4,132},{5,133},{6,134},{7,135},{8... | collective-permute-start | bytes 135176 | tf_op jit(solution)/shard_map/ppermute | solution.py:44
  90.5 38.9 %copy-start.1 = (bf16[192,1408]{1,0:T(8,128)(2,1)S(1)}, bf16[192,1408]{1,0:T(8,128)(2,1)}, u32[]{:S(2)}) copy-start(bf16[192,1408]{1,0:T(8,128)(2,1)} %param.4) | copy-start | bytes 1622020
  90.5 5.5 %collective-permute-start.11 = (f32[704,32]{0,1:T(8,128)S(1)}, f32[704,32]{0,1:T(8,128)S(1)}, u32[]{:S(2)}, u32[]{:S(2)}) collective-permute-start(f32[704,32]{0,1:T(8,128)S(1)} %maximum_select_fusion.6), channel_id=1, source_target_pairs={{0,16},{1,17},{2,18},{3,19},{4,20},{5,21},{6,22},{7,23},{8,24},{9,... | collective-permute-start | bytes 270344 | tf_op jit(solution)/shard_map/ppermute | solution.py:44
  96.1 6.2 %collective-permute-start.12 = (f32[1408,32]{0,1:T(8,128)S(1)}, f32[1408,32]{0,1:T(8,128)S(1)}, u32[]{:S(2)}, u32[]{:S(2)}) collective-permute-start(f32[1408,32]{0,1:T(8,128)S(1)} %maximum_select_fusion.4), channel_id=1, source_target_pairs={{0,2},{1,3},{2,0},{3,1},{4,6},{5,7},{6,4},{7,5},{8,10},{9,11},{10,... | collective-permute-start | bytes 540680 | tf_op jit(solution)/shard_map/ppermute | solution.py:44
  102.4 16.8 %copy-start.2 = (f32[2816,32]{0,1:T(8,128)}, f32[2816,32]{0,1:T(8,128)S(1)}, u32[]{:S(2)}) copy-start(f32[2816,32]{0,1:T(8,128)S(1)} %maximum_select_fusion.3) | copy-start | bytes 1081348
  102.4 16.8 %collective-permute-start.13 = (f32[2816,32]{0,1:T(8,128)S(1)}, f32[2816,32]{0,1:T(8,128)S(1)}, u32[]{:S(2)}, u32[]{:S(2)}) collective-permute-start(f32[2816,32]{0,1:T(8,128)S(1)} %maximum_select_fusion.3), channel_id=1, source_target_pairs={{0,1},{1,0},{2,3},{3,2},{4,5},{5,4},{6,7},{7,6},{8,9},{9,8},{10,11... | collective-permute-start | bytes 1081352 | tf_op jit(solution)/shard_map/ppermute | solution.py:44
  119.2 0.7 copy-start.4
  132.2 3.2 %collective-permute-start.14 = (f32[704,32]{0,1:T(8,128)S(1)}, f32[704,32]{0,1:T(8,128)S(1)}, u32[]{:S(2)}, u32[]{:S(2)}) collective-permute-start(f32[704,32]{0,1:T(8,128)S(1)} %slice_select_fusion.2), channel_id=1, source_target_pairs={{0,1},{1,0},{2,3},{3,2},{4,5},{5,4},{6,7},{7,6},{8,9},{9,8},{10,11... | collective-permute-start | bytes 270344 | tf_op jit(solution)/shard_map/ppermute | solution.py:38
  136.6 4.8 %collective-permute-start.15 = (f32[352,32]{0,1:T(8,128)S(1)}, f32[352,32]{0,1:T(8,128)S(1)}, u32[]{:S(2)}, u32[]{:S(2)}) collective-permute-start(f32[352,32]{0,1:T(8,128)S(1)} %slice_select_fusion.4), channel_id=1, source_target_pairs={{0,2},{1,3},{2,0},{3,1},{4,6},{5,7},{6,4},{7,5},{8,10},{9,11},{10,... | collective-permute-start | bytes 135176 | tf_op jit(solution)/shard_map/ppermute | solution.py:38
  141.6 4.7 %collective-permute-start.16 = (f32[176,32]{0,1:T(8,128)S(1)}, f32[176,32]{0,1:T(8,128)S(1)}, u32[]{:S(2)}, u32[]{:S(2)}) collective-permute-start(f32[176,32]{0,1:T(8,128)S(1)} %slice_select_fusion.6), channel_id=1, source_target_pairs={{0,16},{1,17},{2,18},{3,19},{4,20},{5,21},{6,22},{7,23},{8,24},{9,... | collective-permute-start | bytes 67592 | tf_op jit(solution)/shard_map/ppermute | solution.py:38
  146.3 4.7 %collective-permute-start.17 = (f32[176,32]{0,1:T(8,128)S(1)}, f32[176,32]{0,1:T(8,128)S(1)}, u32[]{:S(2)}, u32[]{:S(2)}) collective-permute-start(f32[176,32]{0,1:T(8,128)S(1)} %select_add_fusion.6), channel_id=1, source_target_pairs={{0,128},{1,129},{2,130},{3,131},{4,132},{5,133},{6,134},{7,135},{8... | collective-permute-start | bytes 67592 | tf_op jit(solution)/shard_map/ppermute | solution.py:41
  151.0 5.6 %collective-permute-start.18 = (f32[176,32]{0,1:T(8,128)S(1)}, f32[176,32]{0,1:T(8,128)S(1)}, u32[]{:S(2)}, u32[]{:S(2)}) collective-permute-start(f32[176,32]{0,1:T(8,128)S(1)} %add.92), channel_id=1, source_target_pairs={{0,4},{1,5},{2,6},{3,7},{4,0},{5,1},{6,2},{7,3},{8,12},{9,13},{10,... | collective-permute-start | bytes 67592 | tf_op jit(solution)/shard_map/ppermute | solution.py:41
  156.6 5.6 %collective-permute-start.19 = (f32[176,32]{0,1:T(8,128)S(1)}, f32[176,32]{0,1:T(8,128)S(1)}, u32[]{:S(2)}, u32[]{:S(2)}) collective-permute-start(f32[176,32]{0,1:T(8,128)S(1)} %add.93), channel_id=1, source_target_pairs={{0,32},{1,33},{2,34},{3,35},{4,36},{5,37},{6,38},{7,39},{8,40},{9,... | collective-permute-start | bytes 67592 | tf_op jit(solution)/shard_map/ppermute | solution.py:41
  162.2 5.6 %collective-permute-start.20 = (f32[176,32]{0,1:T(8,128)S(1)}, f32[176,32]{0,1:T(8,128)S(1)}, u32[]{:S(2)}, u32[]{:S(2)}) collective-permute-start(f32[176,32]{0,1:T(8,128)S(1)} %add.94), channel_id=1, source_target_pairs={{0,256},{1,257},{2,258},{3,259},{4,260},{5,261},{6,262},{7,263},{8... | collective-permute-start | bytes 67592 | tf_op jit(solution)/shard_map/ppermute | solution.py:41
  167.8 8.6 %collective-permute-start.21 = (f32[176,32]{0,1:T(8,128)S(1)}, f32[176,32]{0,1:T(8,128)S(1)}, u32[]{:S(2)}, u32[]{:S(2)}) collective-permute-start(f32[176,32]{0,1:T(8,128)S(1)} %add.95), channel_id=1, source_target_pairs={{0,8},{1,9},{2,10},{3,11},{4,12},{5,13},{6,14},{7,15},{8,0},{9,1},... | collective-permute-start | bytes 67592 | tf_op jit(solution)/shard_map/ppermute | solution.py:41
  176.4 8.6 %collective-permute-start.22 = (f32[176,32]{0,1:T(8,128)S(1)}, f32[176,32]{0,1:T(8,128)S(1)}, u32[]{:S(2)}, u32[]{:S(2)}) collective-permute-start(f32[176,32]{0,1:T(8,128)S(1)} %add.96), channel_id=1, source_target_pairs={{0,64},{1,65},{2,66},{3,67},{4,68},{5,69},{6,70},{7,71},{8,72},{9,... | collective-permute-start | bytes 67592 | tf_op jit(solution)/shard_map/ppermute | solution.py:41
  185.0 8.8 %collective-permute-start.23 = (f32[176,32]{0,1:T(8,128)S(1)}, f32[176,32]{0,1:T(8,128)S(1)}, u32[]{:S(2)}, u32[]{:S(2)}) collective-permute-start(f32[176,32]{0,1:T(8,128)S(1)} %add.97), channel_id=1, source_target_pairs={{0,512},{1,513},{2,514},{3,515},{4,516},{5,517},{6,518},{7,519},{8... | collective-permute-start | bytes 67592 | tf_op jit(solution)/shard_map/ppermute | solution.py:41
  193.8 4.6 %collective-permute-start.24 = (f32[176,32]{0,1:T(8,128)S(1)}, f32[176,32]{0,1:T(8,128)S(1)}, u32[]{:S(2)}, u32[]{:S(2)}) collective-permute-start(f32[176,32]{0,1:T(8,128)S(1)} %add.98), channel_id=1, source_target_pairs={{0,16},{1,17},{2,18},{3,19},{4,20},{5,21},{6,22},{7,23},{8,24},{9,... | collective-permute-start | bytes 67592 | tf_op jit(solution)/shard_map/ppermute | solution.py:44
  198.6 5.0 %collective-permute-start.25 = (f32[352,32]{0,1:T(8,128)S(1)}, f32[352,32]{0,1:T(8,128)S(1)}, u32[]{:S(2)}, u32[]{:S(2)}) collective-permute-start(f32[352,32]{0,1:T(8,128)S(1)} %maximum_select_fusion.8), channel_id=1, source_target_pairs={{0,2},{1,3},{2,0},{3,1},{4,6},{5,7},{6,4},{7,5},{8,10},{9,11},{10,... | collective-permute-start | bytes 135176 | tf_op jit(solution)/shard_map/ppermute | solution.py:44
  203.7 15.1 %collective-permute-start.26 = (f32[704,32]{0,1:T(8,128)S(1)}, f32[704,32]{0,1:T(8,128)S(1)}, u32[]{:S(2)}, u32[]{:S(2)}) collective-permute-start(f32[704,32]{0,1:T(8,128)S(1)} %maximum_select_fusion.7), channel_id=1, source_target_pairs={{0,1},{1,0},{2,3},{3,2},{4,5},{5,4},{6,7},{7,6},{8,9},{9,8},{10,11... | collective-permute-start | bytes 270344 | tf_op jit(solution)/shard_map/ppermute | solution.py:44
  218.9 2.4 %copy-start.3 = (f32[1408,32]{0,1:T(8,128)}, f32[1408,32]{0,1:T(8,128)S(1)}, u32[]{:S(2)}) copy-start(f32[1408,32]{0,1:T(8,128)S(1)} %fusion.6) | copy-start | bytes 540676

commit v7 on v6

--- a/solution.py
+++ b/solution.py
@@ -69,7 +69,7 @@
         my_hat = lax.dynamic_slice_in_dim(p_hat, lax.axis_index("sub") * block_rows, block_rows, 0)
         v_low = jnp.dot(activations, p_low, preferred_element_type=jnp.float32).astype(jnp.bfloat16)
         q_local = jnp.einsum("tc,tr->cr", grad_out, v_low, preferred_element_type=jnp.float32)
-        q_sum = butterfly_sum(q_local, order, n, 3)
+        q_sum = butterfly_sum(q_local, order, n, 2)
         q_new = q_sum / n
         grad_approx = jnp.dot(my_hat, q_new.T, precision=lax.Precision.HIGH)
         return (grad_approx, q_new)

time: 222 us -> 219 us (0.986)
  starting transfers between devices: 107 us -> 104 us
    ppermute x13 -> x14, waiting for transfers between devices: 53.1 us -> 58.7 us  [butterfly_sum(): x = x + lax.ppermute(x, AXES, xor_pairs(n, bit))]
    ppermute x7 -> x6, waiting for transfers between devices: 18 us -> 15.1 us  [butterfly_sum(): other = lax.ppermute(x, AXES, xor_pairs(n, bit))]
    ppermute x7 -> x6, waiting for transfers between devices: 20 us -> 17.3 us  [butterfly_sum(): x = keep + lax.ppermute(send, AXES, xor_pairs(n, bit))]
    ppermute x7 -> x6, starting transfers between devices: 40.1 us -> 37.8 us  [butterfly_sum(): other = lax.ppermute(x, AXES, xor_pairs(n, bit))]
    ppermute x7 -> x6, starting transfers between devices: 27.9 us -> 26 us  [butterfly_sum(): x = keep + lax.ppermute(send, AXES, xor_pairs(n, bit))]
    ppermute x13 -> x14, starting transfers between devices: 38.8 us -> 39.8 us  [butterfly_sum(): x = x + lax.ppermute(x, AXES, xor_pairs(n, bit))]
  transfers between devices with their start and end apart: 27 -> 26, of which waited for: 27 -> 26; matrix products, arithmetic and copies ran while one was open for 0% -> 0% of each run, Pallas kernels for 0% -> 0%
where the time goes in v7:
time: 219 us; the launch traced here: 218 us
  starting transfers between devices  104 us (47%)
  waiting for transfers between devices  91.1 us (42%)
  other arithmetic  11 us (5%)
  matrix products  8.74 us (4%)
  local copies, waits for them, and re-layouts  2.43 us (1%)
    ppermute x14, waiting for transfers between devices, butterfly_sum(): x = x + lax.ppermute(x, AXES, xor_pairs(n, bit))  58.7 us
    ppermute x14, starting transfers between devices, butterfly_sum(): x = x + lax.ppermute(x, AXES, xor_pairs(n, bit))  39.8 us
    ppermute x6, starting transfers between devices, butterfly_sum(): other = lax.ppermute(x, AXES, xor_pairs(n, bit))  37.8 us
    ppermute x6, starting transfers between devices, butterfly_sum(): x = keep + lax.ppermute(send, AXES, xor_pairs(n, bit))  26 us
    ppermute x6, waiting for transfers between devices, butterfly_sum(): x = keep + lax.ppermute(send, AXES, xor_pairs(n, bit))  17.3 us
    ppermute x6, waiting for transfers between devices, butterfly_sum(): other = lax.ppermute(x, AXES, xor_pairs(n, bit))  15.1 us
  transfers between devices with their start and end apart: 26, of which 26 were waited for; matrix products, arithmetic and copies ran while one was open for 0% of the time, Pallas kernels for 0%

profile of v7, /device:TPU:1, one launch (start us, length us, event | category | flops | bytes accessed | tf_op | source)
XLA Modules:
  0.0 217.9 jit_solution(18409099828002306628)
XLA Ops:
  2.2 2.0 convolution_bitcast_fusion
  4.3 16.0 %collective-permute-start = (f32[2816,32]{0,1:T(8,128)S(1)}, f32[2816,32]{0,1:T(8,128)}, u32[]{:S(2)}, u32[]{:S(2)}) collective-permute-start(f32[2816,32]{0,1:T(8,128)S(1)} %slice_select_fusion), channel_id=1, source_target_pairs={{0,1},{1,0},{2,3},{3,2},{4,5},{5,4},{6,7},{7,6},{8,9},{9,8},{10,11... | collective-permute-start | bytes 1081352 | tf_op jit(solution)/shard_map/ppermute | solution.py:38
  22.8 1.9 collective-permute-start.1
  24.8 5.7 %collective-permute-done.1 = f32[1408,32]{0,1:T(8,128)S(1)} collective-permute-done((f32[1408,32]{0,1:T(8,128)S(1)}, f32[1408,32]{0,1:T(8,128)S(1)}, u32[]{:S(2)}, u32[]{:S(2)}) %collective-permute-start.1) | collective-permute-done | bytes 180256 | tf_op jit(solution)/shard_map/ppermute | solution.py:38
  30.6 1.9 collective-permute-start.2
  32.5 3.4 %collective-permute-done.2 = f32[704,32]{0,1:T(8,128)S(1)} collective-permute-done((f32[704,32]{0,1:T(8,128)S(1)}, f32[704,32]{0,1:T(8,128)S(1)}, u32[]{:S(2)}, u32[]{:S(2)}) %collective-permute-start.2) | collective-permute-done | bytes 90144 | tf_op jit(solution)/shard_map/ppermute | solution.py:38
  38.0 2.9 %collective-permute-done.3 = f32[352,32]{0,1:T(8,128)S(1)} collective-permute-done((f32[352,32]{0,1:T(8,128)S(1)}, f32[352,32]{0,1:T(8,128)S(1)}, u32[]{:S(2)}, u32[]{:S(2)}) %collective-permute-start.3) | collective-permute-done | bytes 45088 | tf_op jit(solution)/shard_map/ppermute | solution.py:38
  41.0 1.9 collective-permute-start.4
  43.0 4.3 %collective-permute-done.4 = f32[352,32]{0,1:T(8,128)S(1)} collective-permute-done((f32[352,32]{0,1:T(8,128)S(1)}, f32[352,32]{0,1:T(8,128)S(1)}, u32[]{:S(2)}, u32[]{:S(2)}) %collective-permute-start.4) | collective-permute-done | bytes 45088 | tf_op jit(solution)/shard_map/ppermute | solution.py:41
  47.3 1.9 collective-permute-start.5
  49.2 4.1 %collective-permute-done.5 = f32[352,32]{0,1:T(8,128)S(1)} collective-permute-done((f32[352,32]{0,1:T(8,128)S(1)}, f32[352,32]{0,1:T(8,128)S(1)}, u32[]{:S(2)}, u32[]{:S(2)}) %collective-permute-start.5) | collective-permute-done | bytes 45088 | tf_op jit(solution)/shard_map/ppermute | solution.py:41
  53.3 1.9 collective-permute-start.6
  55.2 4.1 %collective-permute-done.6 = f32[352,32]{0,1:T(8,128)S(1)} collective-permute-done((f32[352,32]{0,1:T(8,128)S(1)}, f32[352,32]{0,1:T(8,128)S(1)}, u32[]{:S(2)}, u32[]{:S(2)}) %collective-permute-start.6) | collective-permute-done | bytes 45088 | tf_op jit(solution)/shard_map/ppermute | solution.py:41
  59.3 1.9 collective-permute-start.7
  61.2 6.8 %collective-permute-done.7 = f32[352,32]{0,1:T(8,128)S(1)} collective-permute-done((f32[352,32]{0,1:T(8,128)S(1)}, f32[352,32]{0,1:T(8,128)S(1)}, u32[]{:S(2)}, u32[]{:S(2)}) %collective-permute-start.7) | collective-permute-done | bytes 45088 | tf_op jit(solution)/shard_map/ppermute | solution.py:41
  68.1 3.5 %collective-permute-start.8 = (f32[352,32]{0,1:T(8,128)S(1)}, f32[352,32]{0,1:T(8,128)S(1)}, u32[]{:S(2)}, u32[]{:S(2)}) collective-permute-start(f32[352,32]{0,1:T(8,128)S(1)} %add.84), channel_id=1, source_target_pairs={{0,64},{1,65},{2,66},{3,67},{4,68},{5,69},{6,70},{7,71},{8,72},{9,... | collective-permute-start | bytes 135176 | tf_op jit(solution)/shard_map/ppermute | solution.py:41
  71.6 5.2 %collective-permute-done.8 = f32[352,32]{0,1:T(8,128)S(1)} collective-permute-done((f32[352,32]{0,1:T(8,128)S(1)}, f32[352,32]{0,1:T(8,128)S(1)}, u32[]{:S(2)}, u32[]{:S(2)}) %collective-permute-start.8) | collective-permute-done | bytes 45088 | tf_op jit(solution)/shard_map/ppermute | solution.py:41
  76.8 4.5 %collective-permute-start.9 = (f32[352,32]{0,1:T(8,128)S(1)}, f32[352,32]{0,1:T(8,128)S(1)}, u32[]{:S(2)}, u32[]{:S(2)}) collective-permute-start(f32[352,32]{0,1:T(8,128)S(1)} %add.85), channel_id=1, source_target_pairs={{0,512},{1,513},{2,514},{3,515},{4,516},{5,517},{6,518},{7,519},{8... | collective-permute-start | bytes 135176 | tf_op jit(solution)/shard_map/ppermute | solution.py:41
  81.3 4.3 %collective-permute-done.9 = f32[352,32]{0,1:T(8,128)S(1)} collective-permute-done((f32[352,32]{0,1:T(8,128)S(1)}, f32[352,32]{0,1:T(8,128)S(1)}, u32[]{:S(2)}, u32[]{:S(2)}) %collective-permute-start.9) | collective-permute-done | bytes 45088 | tf_op jit(solution)/shard_map/ppermute | solution.py:41
  85.6 2.2 %collective-permute-start.10 = (f32[352,32]{0,1:T(8,128)S(1)}, f32[352,32]{0,1:T(8,128)S(1)}, u32[]{:S(2)}, u32[]{:S(2)}) collective-permute-start(f32[352,32]{0,1:T(8,128)S(1)} %add.86), channel_id=1, source_target_pairs={{0,128},{1,129},{2,130},{3,131},{4,132},{5,133},{6,134},{7,135},{8... | collective-permute-start | bytes 135176 | tf_op jit(solution)/shard_map/ppermute | solution.py:44
  87.8 2.6 %collective-permute-done.10 = f32[352,32]{0,1:T(8,128)S(1)} collective-permute-done((f32[352,32]{0,1:T(8,128)S(1)}, f32[352,32]{0,1:T(8,128)S(1)}, u32[]{:S(2)}, u32[]{:S(2)}) %collective-permute-start.10) | collective-permute-done | bytes 45088 | tf_op jit(solution)/shard_map/ppermute | solution.py:44
  90.5 2.4 %collective-permute-start.11 = (f32[704,32]{0,1:T(8,128)S(1)}, f32[704,32]{0,1:T(8,128)S(1)}, u32[]{:S(2)}, u32[]{:S(2)}) collective-permute-start(f32[704,32]{0,1:T(8,128)S(1)} %maximum_select_fusion.6), channel_id=1, source_target_pairs={{0,16},{1,17},{2,18},{3,19},{4,20},{5,21},{6,22},{7,23},{8,24},{9,... | collective-permute-start | bytes 270344 | tf_op jit(solution)/shard_map/ppermute | solution.py:44
  93.0 3.0 %collective-permute-done.11 = f32[704,32]{0,1:T(8,128)S(1)} collective-permute-done((f32[704,32]{0,1:T(8,128)S(1)}, f32[704,32]{0,1:T(8,128)S(1)}, u32[]{:S(2)}, u32[]{:S(2)}) %collective-permute-start.11) | collective-permute-done | bytes 90144 | tf_op jit(solution)/shard_map/ppermute | solution.py:44
  96.1 1.9 collective-permute-start.12
  98.1 4.3 %collective-permute-done.12 = f32[1408,32]{0,1:T(8,128)S(1)} collective-permute-done((f32[1408,32]{0,1:T(8,128)S(1)}, f32[1408,32]{0,1:T(8,128)S(1)}, u32[]{:S(2)}, u32[]{:S(2)}) %collective-permute-start.12) | collective-permute-done | bytes 180256 | tf_op jit(solution)/shard_map/ppermute | solution.py:44
  102.4 15.5 %collective-permute-start.13 = (f32[2816,32]{0,1:T(8,128)S(1)}, f32[2816,32]{0,1:T(8,128)S(1)}, u32[]{:S(2)}, u32[]{:S(2)}) collective-permute-start(f32[2816,32]{0,1:T(8,128)S(1)} %maximum_select_fusion.3), channel_id=1, source_target_pairs={{0,1},{1,0},{2,3},{3,2},{4,5},{5,4},{6,7},{7,6},{8,9},{9,8},{10,11... | collective-permute-start | bytes 1081352 | tf_op jit(solution)/shard_map/ppermute | solution.py:44
  120.5 2.9 %cholesky.16 = f32[32,32]{1,0:T(8,128)S(1)} custom-call(f32[32,32]{1,0:T(8,128)S(1)} %fusion.11), custom_call_target="Cholesky" | custom-call | tf_op jit(solution)/shard_map/cholesky | solution.py:50
  124.8 2.4 %custom-call.5 = f32[1,32,32]{1,2,0:T(8,128)S(1)} custom-call(f32[1,32,32]{2,1,0:T(8,128)S(1)} %fusion.9), custom_call_target="InvertDiagBlocksLowerTriangular" | custom-call | tf_op jit(solution)/shard_map/triangular_solve | solution.py:51
  127.2 2.2 %fusion = f32[5632,32]{0,1:T(8,128)S(1)} fusion(f32[2816,32]{0,1:T(8,128)} %copy-done.2, f32[2816,32]{0,1:T(8,128)} %copy-done.4, pred[]{:T(512)S(6)} %eq.8, f32[1,32,32]{1,2,0:T(8,128)S(1)} %custom-call.5), kind=kOutput, calls=%fused_computation.5 | convolution fusion | flops 69746688 | bytes 1445889 | tf_op jit(solution)/shard_map/triangular_solve | solution.py:51
  132.2 2.3 %collective-permute-start.14 = (f32[704,32]{0,1:T(8,128)S(1)}, f32[704,32]{0,1:T(8,128)S(1)}, u32[]{:S(2)}, u32[]{:S(2)}) collective-permute-start(f32[704,32]{0,1:T(8,128)S(1)} %slice_select_fusion.2), channel_id=1, source_target_pairs={{0,1},{1,0},{2,3},{3,2},{4,5},{5,4},{6,7},{7,6},{8,9},{9,8},{10,11... | collective-permute-start | bytes 270344 | tf_op jit(solution)/shard_map/ppermute | solution.py:38
  138.5 2.9 %collective-permute-done.15 = f32[352,32]{0,1:T(8,128)S(1)} collective-permute-done((f32[352,32]{0,1:T(8,128)S(1)}, f32[352,32]{0,1:T(8,128)S(1)}, u32[]{:S(2)}, u32[]{:S(2)}) %collective-permute-start.15) | collective-permute-done | bytes 45088 | tf_op jit(solution)/shard_map/ppermute | solution.py:38
  141.5 1.9 collective-permute-start.16
  143.4 2.9 %collective-permute-done.16 = f32[352,32]{0,1:T(8,128)S(1)} collective-permute-done((f32[352,32]{0,1:T(8,128)S(1)}, f32[352,32]{0,1:T(8,128)S(1)}, u32[]{:S(2)}, u32[]{:S(2)}) %collective-permute-start.16) | collective-permute-done | bytes 45088 | tf_op jit(solution)/shard_map/ppermute | solution.py:41
  146.3 1.9 collective-permute-start.17
  148.3 2.9 %collective-permute-done.17 = f32[352,32]{0,1:T(8,128)S(1)} collective-permute-done((f32[352,32]{0,1:T(8,128)S(1)}, f32[352,32]{0,1:T(8,128)S(1)}, u32[]{:S(2)}, u32[]{:S(2)}) %collective-permute-start.17) | collective-permute-done | bytes 45088 | tf_op jit(solution)/shard_map/ppermute | solution.py:41
  153.1 4.1 %collective-permute-done.18 = f32[352,32]{0,1:T(8,128)S(1)} collective-permute-done((f32[352,32]{0,1:T(8,128)S(1)}, f32[352,32]{0,1:T(8,128)S(1)}, u32[]{:S(2)}, u32[]{:S(2)}) %collective-permute-start.18) | collective-permute-done | bytes 45088 | tf_op jit(solution)/shard_map/ppermute | solution.py:41
  157.2 1.9 collective-permute-start.19
  159.1 4.1 %collective-permute-done.19 = f32[352,32]{0,1:T(8,128)S(1)} collective-permute-done((f32[352,32]{0,1:T(8,128)S(1)}, f32[352,32]{0,1:T(8,128)S(1)}, u32[]{:S(2)}, u32[]{:S(2)}) %collective-permute-start.19) | collective-permute-done | bytes 45088 | tf_op jit(solution)/shard_map/ppermute | solution.py:41
  165.1 4.1 %collective-permute-done.20 = f32[352,32]{0,1:T(8,128)S(1)} collective-permute-done((f32[352,32]{0,1:T(8,128)S(1)}, f32[352,32]{0,1:T(8,128)S(1)}, u32[]{:S(2)}, u32[]{:S(2)}) %collective-permute-start.20) | collective-permute-done | bytes 45088 | tf_op jit(solution)/shard_map/ppermute | solution.py:41
  169.2 4.9 %collective-permute-start.21 = (f32[352,32]{0,1:T(8,128)S(1)}, f32[352,32]{0,1:T(8,128)S(1)}, u32[]{:S(2)}, u32[]{:S(2)}) collective-permute-start(f32[352,32]{0,1:T(8,128)S(1)} %add.95), channel_id=1, source_target_pairs={{0,8},{1,9},{2,10},{3,11},{4,12},{5,13},{6,14},{7,15},{8,0},{9,1},... | collective-permute-start | bytes 135176 | tf_op jit(solution)/shard_map/ppermute | solution.py:41
  174.1 4.1 %collective-permute-done.21 = f32[352,32]{0,1:T(8,128)S(1)} collective-permute-done((f32[352,32]{0,1:T(8,128)S(1)}, f32[352,32]{0,1:T(8,128)S(1)}, u32[]{:S(2)}, u32[]{:S(2)}) %collective-permute-start.21) | collective-permute-done | bytes 45088 | tf_op jit(solution)/shard_map/ppermute | solution.py:41
  178.2 4.5 %collective-permute-start.22 = (f32[352,32]{0,1:T(8,128)S(1)}, f32[352,32]{0,1:T(8,128)S(1)}, u32[]{:S(2)}, u32[]{:S(2)}) collective-permute-start(f32[352,32]{0,1:T(8,128)S(1)} %add.96), channel_id=1, source_target_pairs={{0,64},{1,65},{2,66},{3,67},{4,68},{5,69},{6,70},{7,71},{8,72},{9,... | collective-permute-start | bytes 135176 | tf_op jit(solution)/shard_map/ppermute | solution.py:41
  182.7 4.3 %collective-permute-done.22 = f32[352,32]{0,1:T(8,128)S(1)} collective-permute-done((f32[352,32]{0,1:T(8,128)S(1)}, f32[352,32]{0,1:T(8,128)S(1)}, u32[]{:S(2)}, u32[]{:S(2)}) %collective-permute-start.22) | collective-permute-done | bytes 45088 | tf_op jit(solution)/shard_map/ppermute | solution.py:41
  187.0 5.2 %collective-permute-start.23 = (f32[352,32]{0,1:T(8,128)S(1)}, f32[352,32]{0,1:T(8,128)S(1)}, u32[]{:S(2)}, u32[]{:S(2)}) collective-permute-start(f32[352,32]{0,1:T(8,128)S(1)} %add.97), channel_id=1, source_target_pairs={{0,512},{1,513},{2,514},{3,515},{4,516},{5,517},{6,518},{7,519},{8... | collective-permute-start | bytes 135176 | tf_op jit(solution)/shard_map/ppermute | solution.py:41
  192.2 3.6 %collective-permute-done.23 = f32[352,32]{0,1:T(8,128)S(1)} collective-permute-done((f32[352,32]{0,1:T(8,128)S(1)}, f32[352,32]{0,1:T(8,128)S(1)}, u32[]{:S(2)}, u32[]{:S(2)}) %collective-permute-start.23) | collective-permute-done | bytes 45088 | tf_op jit(solution)/shard_map/ppermute | solution.py:41
  197.7 2.9 %collective-permute-done.24 = f32[352,32]{0,1:T(8,128)S(1)} collective-permute-done((f32[352,32]{0,1:T(8,128)S(1)}, f32[352,32]{0,1:T(8,128)S(1)}, u32[]{:S(2)}, u32[]{:S(2)}) %collective-permute-start.24) | collective-permute-done | bytes 45088 | tf_op jit(solution)/shard_map/ppermute | solution.py:44
  200.7 13.8 %collective-permute-start.25 = (f32[704,32]{0,1:T(8,128)S(1)}, f32[704,32]{0,1:T(8,128)S(1)}, u32[]{:S(2)}, u32[]{:S(2)}) collective-permute-start(f32[704,32]{0,1:T(8,128)S(1)} %maximum_select_fusion.7), channel_id=1, source_target_pairs={{0,1},{1,0},{2,3},{3,2},{4,5},{5,4},{6,7},{7,6},{8,9},{9,8},{10,11... | collective-permute-start | bytes 270344 | tf_op jit(solution)/shard_map/ppermute | solution.py:44
  215.6 2.3 %fusion.7 = f32[352,1408]{1,0:T(8,128)} fusion(f32[1408,32]{0,1:T(8,128)S(1)} %fusion.6, f32[5632,32]{0,1:T(8,128)S(1)} %fusion, s32[]{:T(128)S(6)} %select_n.133), kind=kOutput, calls=%fused_computation.25 | convolution fusion | flops 95158272 | bytes 2211844 | tf_op jit(solution)/shard_map/dot_general | solution.py:74
  (57 shorter events, 24.4 us)
Async XLA Ops:
  0.6 1.6 copy-start
  4.3 17.4 %collective-permute-start = (f32[2816,32]{0,1:T(8,128)S(1)}, f32[2816,32]{0,1:T(8,128)}, u32[]{:S(2)}, u32[]{:S(2)}) collective-permute-start(f32[2816,32]{0,1:T(8,128)S(1)} %slice_select_fusion), channel_id=1, source_target_pairs={{0,1},{1,0},{2,3},{3,2},{4,5},{5,4},{6,7},{7,6},{8,9},{9,8},{10,11... | collective-permute-start | bytes 1081352 | tf_op jit(solution)/shard_map/ppermute | solution.py:38
  22.8 7.6 %collective-permute-start.1 = (f32[1408,32]{0,1:T(8,128)S(1)}, f32[1408,32]{0,1:T(8,128)S(1)}, u32[]{:S(2)}, u32[]{:S(2)}) collective-permute-start(f32[1408,32]{0,1:T(8,128)S(1)} %slice_select_fusion.1), channel_id=1, source_target_pairs={{0,2},{1,3},{2,0},{3,1},{4,6},{5,7},{6,4},{7,5},{8,10},{9,11},{10,... | collective-permute-start | bytes 540680 | tf_op jit(solution)/shard_map/ppermute | solution.py:38
  30.6 5.4 %collective-permute-start.2 = (f32[704,32]{0,1:T(8,128)S(1)}, f32[704,32]{0,1:T(8,128)S(1)}, u32[]{:S(2)}, u32[]{:S(2)}) collective-permute-start(f32[704,32]{0,1:T(8,128)S(1)} %slice_select_fusion.3), channel_id=1, source_target_pairs={{0,16},{1,17},{2,18},{3,19},{4,20},{5,21},{6,22},{7,23},{8,24},{9,... | collective-permute-start | bytes 270344 | tf_op jit(solution)/shard_map/ppermute | solution.py:38
  36.1 4.8 %collective-permute-start.3 = (f32[352,32]{0,1:T(8,128)S(1)}, f32[352,32]{0,1:T(8,128)S(1)}, u32[]{:S(2)}, u32[]{:S(2)}) collective-permute-start(f32[352,32]{0,1:T(8,128)S(1)} %slice_select_fusion.5), channel_id=1, source_target_pairs={{0,128},{1,129},{2,130},{3,131},{4,132},{5,133},{6,134},{7,135},{8... | collective-permute-start | bytes 135176 | tf_op jit(solution)/shard_map/ppermute | solution.py:38
  41.0 6.3 %collective-permute-start.4 = (f32[352,32]{0,1:T(8,128)S(1)}, f32[352,32]{0,1:T(8,128)S(1)}, u32[]{:S(2)}, u32[]{:S(2)}) collective-permute-start(f32[352,32]{0,1:T(8,128)S(1)} %select_add_fusion.5), channel_id=1, source_target_pairs={{0,4},{1,5},{2,6},{3,7},{4,0},{5,1},{6,2},{7,3},{8,12},{9,13},{10,... | collective-permute-start | bytes 135176 | tf_op jit(solution)/shard_map/ppermute | solution.py:41
  47.3 6.0 %collective-permute-start.5 = (f32[352,32]{0,1:T(8,128)S(1)}, f32[352,32]{0,1:T(8,128)S(1)}, u32[]{:S(2)}, u32[]{:S(2)}) collective-permute-start(f32[352,32]{0,1:T(8,128)S(1)} %add.81), channel_id=1, source_target_pairs={{0,32},{1,33},{2,34},{3,35},{4,36},{5,37},{6,38},{7,39},{8,40},{9,... | collective-permute-start | bytes 135176 | tf_op jit(solution)/shard_map/ppermute | solution.py:41
  53.3 6.0 %collective-permute-start.6 = (f32[352,32]{0,1:T(8,128)S(1)}, f32[352,32]{0,1:T(8,128)S(1)}, u32[]{:S(2)}, u32[]{:S(2)}) collective-permute-start(f32[352,32]{0,1:T(8,128)S(1)} %add.82), channel_id=1, source_target_pairs={{0,256},{1,257},{2,258},{3,259},{4,260},{5,261},{6,262},{7,263},{8... | collective-permute-start | bytes 135176 | tf_op jit(solution)/shard_map/ppermute | solution.py:41
  59.3 8.7 %collective-permute-start.7 = (f32[352,32]{0,1:T(8,128)S(1)}, f32[352,32]{0,1:T(8,128)S(1)}, u32[]{:S(2)}, u32[]{:S(2)}) collective-permute-start(f32[352,32]{0,1:T(8,128)S(1)} %add.83), channel_id=1, source_target_pairs={{0,8},{1,9},{2,10},{3,11},{4,12},{5,13},{6,14},{7,15},{8,0},{9,1},... | collective-permute-start | bytes 135176 | tf_op jit(solution)/shard_map/ppermute | solution.py:41
  68.1 8.7 %collective-permute-start.8 = (f32[352,32]{0,1:T(8,128)S(1)}, f32[352,32]{0,1:T(8,128)S(1)}, u32[]{:S(2)}, u32[]{:S(2)}) collective-permute-start(f32[352,32]{0,1:T(8,128)S(1)} %add.84), channel_id=1, source_target_pairs={{0,64},{1,65},{2,66},{3,67},{4,68},{5,69},{6,70},{7,71},{8,72},{9,... | collective-permute-start | bytes 135176 | tf_op jit(solution)/shard_map/ppermute | solution.py:41
  76.8 8.8 %collective-permute-start.9 = (f32[352,32]{0,1:T(8,128)S(1)}, f32[352,32]{0,1:T(8,128)S(1)}, u32[]{:S(2)}, u32[]{:S(2)}) collective-permute-start(f32[352,32]{0,1:T(8,128)S(1)} %add.85), channel_id=1, source_target_pairs={{0,512},{1,513},{2,514},{3,515},{4,516},{5,517},{6,518},{7,519},{8... | collective-permute-start | bytes 135176 | tf_op jit(solution)/shard_map/ppermute | solution.py:41
  85.6 4.8 %collective-permute-start.10 = (f32[352,32]{0,1:T(8,128)S(1)}, f32[352,32]{0,1:T(8,128)S(1)}, u32[]{:S(2)}, u32[]{:S(2)}) collective-permute-start(f32[352,32]{0,1:T(8,128)S(1)} %add.86), channel_id=1, source_target_pairs={{0,128},{1,129},{2,130},{3,131},{4,132},{5,133},{6,134},{7,135},{8... | collective-permute-start | bytes 135176 | tf_op jit(solution)/shard_map/ppermute | solution.py:44
  90.5 38.9 %copy-start.1 = (bf16[192,1408]{1,0:T(8,128)(2,1)S(1)}, bf16[192,1408]{1,0:T(8,128)(2,1)}, u32[]{:S(2)}) copy-start(bf16[192,1408]{1,0:T(8,128)(2,1)} %param.4) | copy-start | bytes 1622020
  90.5 5.5 %collective-permute-start.11 = (f32[704,32]{0,1:T(8,128)S(1)}, f32[704,32]{0,1:T(8,128)S(1)}, u32[]{:S(2)}, u32[]{:S(2)}) collective-permute-start(f32[704,32]{0,1:T(8,128)S(1)} %maximum_select_fusion.6), channel_id=1, source_target_pairs={{0,16},{1,17},{2,18},{3,19},{4,20},{5,21},{6,22},{7,23},{8,24},{9,... | collective-permute-start | bytes 270344 | tf_op jit(solution)/shard_map/ppermute | solution.py:44
  96.1 6.2 %collective-permute-start.12 = (f32[1408,32]{0,1:T(8,128)S(1)}, f32[1408,32]{0,1:T(8,128)S(1)}, u32[]{:S(2)}, u32[]{:S(2)}) collective-permute-start(f32[1408,32]{0,1:T(8,128)S(1)} %maximum_select_fusion.4), channel_id=1, source_target_pairs={{0,2},{1,3},{2,0},{3,1},{4,6},{5,7},{6,4},{7,5},{8,10},{9,11},{10,... | collective-permute-start | bytes 540680 | tf_op jit(solution)/shard_map/ppermute | solution.py:44
  102.4 16.8 %copy-start.2 = (f32[2816,32]{0,1:T(8,128)}, f32[2816,32]{0,1:T(8,128)S(1)}, u32[]{:S(2)}) copy-start(f32[2816,32]{0,1:T(8,128)S(1)} %maximum_select_fusion.3) | copy-start | bytes 1081348
  102.4 16.8 %collective-permute-start.13 = (f32[2816,32]{0,1:T(8,128)S(1)}, f32[2816,32]{0,1:T(8,128)S(1)}, u32[]{:S(2)}, u32[]{:S(2)}) collective-permute-start(f32[2816,32]{0,1:T(8,128)S(1)} %maximum_select_fusion.3), channel_id=1, source_target_pairs={{0,1},{1,0},{2,3},{3,2},{4,5},{5,4},{6,7},{7,6},{8,9},{9,8},{10,11... | collective-permute-start | bytes 1081352 | tf_op jit(solution)/shard_map/ppermute | solution.py:44
  119.2 0.7 copy-start.4
  132.2 3.2 %collective-permute-start.14 = (f32[704,32]{0,1:T(8,128)S(1)}, f32[704,32]{0,1:T(8,128)S(1)}, u32[]{:S(2)}, u32[]{:S(2)}) collective-permute-start(f32[704,32]{0,1:T(8,128)S(1)} %slice_select_fusion.2), channel_id=1, source_target_pairs={{0,1},{1,0},{2,3},{3,2},{4,5},{5,4},{6,7},{7,6},{8,9},{9,8},{10,11... | collective-permute-start | bytes 270344 | tf_op jit(solution)/shard_map/ppermute | solution.py:38
  136.6 4.8 %collective-permute-start.15 = (f32[352,32]{0,1:T(8,128)S(1)}, f32[352,32]{0,1:T(8,128)S(1)}, u32[]{:S(2)}, u32[]{:S(2)}) collective-permute-start(f32[352,32]{0,1:T(8,128)S(1)} %slice_select_fusion.4), channel_id=1, source_target_pairs={{0,2},{1,3},{2,0},{3,1},{4,6},{5,7},{6,4},{7,5},{8,10},{9,11},{10,... | collective-permute-start | bytes 135176 | tf_op jit(solution)/shard_map/ppermute | solution.py:38
  141.5 4.8 %collective-permute-start.16 = (f32[352,32]{0,1:T(8,128)S(1)}, f32[352,32]{0,1:T(8,128)S(1)}, u32[]{:S(2)}, u32[]{:S(2)}) collective-permute-start(f32[352,32]{0,1:T(8,128)S(1)} %select_add_fusion.4), channel_id=1, source_target_pairs={{0,16},{1,17},{2,18},{3,19},{4,20},{5,21},{6,22},{7,23},{8,24},{9,... | collective-permute-start | bytes 135176 | tf_op jit(solution)/shard_map/ppermute | solution.py:41
  146.3 4.8 %collective-permute-start.17 = (f32[352,32]{0,1:T(8,128)S(1)}, f32[352,32]{0,1:T(8,128)S(1)}, u32[]{:S(2)}, u32[]{:S(2)}) collective-permute-start(f32[352,32]{0,1:T(8,128)S(1)} %add.91), channel_id=1, source_target_pairs={{0,128},{1,129},{2,130},{3,131},{4,132},{5,133},{6,134},{7,135},{8... | collective-permute-start | bytes 135176 | tf_op jit(solution)/shard_map/ppermute | solution.py:41
  151.2 6.0 %collective-permute-start.18 = (f32[352,32]{0,1:T(8,128)S(1)}, f32[352,32]{0,1:T(8,128)S(1)}, u32[]{:S(2)}, u32[]{:S(2)}) collective-permute-start(f32[352,32]{0,1:T(8,128)S(1)} %add.92), channel_id=1, source_target_pairs={{0,4},{1,5},{2,6},{3,7},{4,0},{5,1},{6,2},{7,3},{8,12},{9,13},{10,... | collective-permute-start | bytes 135176 | tf_op jit(solution)/shard_map/ppermute | solution.py:41
  157.2 6.0 %collective-permute-start.19 = (f32[352,32]{0,1:T(8,128)S(1)}, f32[352,32]{0,1:T(8,128)S(1)}, u32[]{:S(2)}, u32[]{:S(2)}) collective-permute-start(f32[352,32]{0,1:T(8,128)S(1)} %add.93), channel_id=1, source_target_pairs={{0,32},{1,33},{2,34},{3,35},{4,36},{5,37},{6,38},{7,39},{8,40},{9,... | collective-permute-start | bytes 135176 | tf_op jit(solution)/shard_map/ppermute | solution.py:41
  163.2 6.0 %collective-permute-start.20 = (f32[352,32]{0,1:T(8,128)S(1)}, f32[352,32]{0,1:T(8,128)S(1)}, u32[]{:S(2)}, u32[]{:S(2)}) collective-permute-start(f32[352,32]{0,1:T(8,128)S(1)} %add.94), channel_id=1, source_target_pairs={{0,256},{1,257},{2,258},{3,259},{4,260},{5,261},{6,262},{7,263},{8... | collective-permute-start | bytes 135176 | tf_op jit(solution)/shard_map/ppermute | solution.py:41
  169.2 9.0 %collective-permute-start.21 = (f32[352,32]{0,1:T(8,128)S(1)}, f32[352,32]{0,1:T(8,128)S(1)}, u32[]{:S(2)}, u32[]{:S(2)}) collective-permute-start(f32[352,32]{0,1:T(8,128)S(1)} %add.95), channel_id=1, source_target_pairs={{0,8},{1,9},{2,10},{3,11},{4,12},{5,13},{6,14},{7,15},{8,0},{9,1},... | collective-permute-start | bytes 135176 | tf_op jit(solution)/shard_map/ppermute | solution.py:41
  178.2 8.7 %collective-permute-start.22 = (f32[352,32]{0,1:T(8,128)S(1)}, f32[352,32]{0,1:T(8,128)S(1)}, u32[]{:S(2)}, u32[]{:S(2)}) collective-permute-start(f32[352,32]{0,1:T(8,128)S(1)} %add.96), channel_id=1, source_target_pairs={{0,64},{1,65},{2,66},{3,67},{4,68},{5,69},{6,70},{7,71},{8,72},{9,... | collective-permute-start | bytes 135176 | tf_op jit(solution)/shard_map/ppermute | solution.py:41
  187.0 8.7 %collective-permute-start.23 = (f32[352,32]{0,1:T(8,128)S(1)}, f32[352,32]{0,1:T(8,128)S(1)}, u32[]{:S(2)}, u32[]{:S(2)}) collective-permute-start(f32[352,32]{0,1:T(8,128)S(1)} %add.97), channel_id=1, source_target_pairs={{0,512},{1,513},{2,514},{3,515},{4,516},{5,517},{6,518},{7,519},{8... | collective-permute-start | bytes 135176 | tf_op jit(solution)/shard_map/ppermute | solution.py:41
  195.7 4.8 %collective-permute-start.24 = (f32[352,32]{0,1:T(8,128)S(1)}, f32[352,32]{0,1:T(8,128)S(1)}, u32[]{:S(2)}, u32[]{:S(2)}) collective-permute-start(f32[352,32]{0,1:T(8,128)S(1)} %add.98), channel_id=1, source_target_pairs={{0,2},{1,3},{2,0},{3,1},{4,6},{5,7},{6,4},{7,5},{8,10},{9,11},{10,... | collective-permute-start | bytes 135176 | tf_op jit(solution)/shard_map/ppermute | solution.py:44
  200.7 14.8 %collective-permute-start.25 = (f32[704,32]{0,1:T(8,128)S(1)}, f32[704,32]{0,1:T(8,128)S(1)}, u32[]{:S(2)}, u32[]{:S(2)}) collective-permute-start(f32[704,32]{0,1:T(8,128)S(1)} %maximum_select_fusion.7), channel_id=1, source_target_pairs={{0,1},{1,0},{2,3},{3,2},{4,5},{5,4},{6,7},{7,6},{8,9},{9,8},{10,11... | collective-permute-start | bytes 270344 | tf_op jit(solution)/shard_map/ppermute | solution.py:44
  215.6 2.4 %copy-start.3 = (f32[1408,32]{0,1:T(8,128)}, f32[1408,32]{0,1:T(8,128)S(1)}, u32[]{:S(2)}) copy-start(f32[1408,32]{0,1:T(8,128)S(1)} %fusion.6) | copy-start | bytes 540676
